TPU v7x, 512 devices: a whole 4x4x16 slice. The times are simulated.
512 devices in a mesh: ctx: 16 (over z), ep: 32 (over x, y, core).
Axes of the slice: x: 4, y: 4, z: 16, core: 2. Of those that a mesh axis runs over, the one named last changes fastest.
Arguments:
- queries: bfloat16 [4096, 8192], P('ctx', 'ep'), may hold values from -6 to 6
- key_rows: bfloat16 [4096, 8192], P('ctx', 'ep'), may hold values from -6 to 6
- value_rows: bfloat16 [4096, 8192], P('ctx', 'ep'), may hold values from -6 to 6
- log_decay: float32 [4096, 64], P('ctx', 'ep'), may hold values from -1 to 0
- out_weight: bfloat16 [6144, 8192], P('ep'), may hold values from -0.0625 to 0.0625
- expert_ids: int32 [4096, 2], P('ctx'), may hold values from 0 to 31, all different within a row; in each aligned block of 256 rows (0 to 255, 256 to 511, ...) at most 32 rows name the same one
- flagged: int32 [1024], P('ctx'), may hold values from 0 to 4095, as said below
- direction: float32 [6144], P('ep'), as said below
Outputs:
- expert_tiles: bfloat16 [32, 512, 6144], P('ep', 'ctx')
Inputs may be any that keep to these rules, and one draw needn't show every extreme that they name: `expert_ids`: each row names 2 different experts; among the 256 rows of one block of the sequence no expert is named more than 32 times, a bound that some block reaches. `flagged`: entries 64 * b to 64 * b + 63 are distinct rows of block b of 256 rows. `direction`: not all zero.
All inputs are finite; a program needn't handle non-finite values.
Results may differ from a plain program's by a relative error of at most 0.0059.
Values may be sent and summed in bfloat16 or wider, within the bound.
No kernel may reach another device: no remote copies, remote signals or barrier semaphores. Data moves between devices by JAX's collectives and lax.ppermute only.
A program may use at most 64 MiB of HBM per device.

v0:
```python
import jax
import jax.numpy as jnp
from jax import lax
from jax.sharding import PartitionSpec as P

HEAD = 128
TOP = 2
EXP_DEV = 1
SUB = 256


def passed_along(value, axis, steps):
    count = lax.axis_size(axis)
    leading, last = (max(0, -steps), min(count, count - steps))
    return lax.ppermute(value, axis, [(source, source + steps) for source in range(leading, last)])


def local_step(carried_in, pieces):
    kv_state, offset = carried_in
    query_sub, key_sub, value_sub, decay_sub = pieces
    sub_rows = query_sub.shape[0]
    cumulated = jnp.cumsum(decay_sub, axis=0)
    scores = jnp.einsum("thd,shd->hts", query_sub, key_sub, preferred_element_type=jnp.float32)
    spread = jnp.transpose(cumulated)
    decay_gaps = jnp.minimum(spread[:, :, None] - spread[:, None, :], 0.0)
    causal = (
        jnp.arange(sub_rows, dtype=jnp.int32)[:, None]
        >= jnp.arange(sub_rows, dtype=jnp.int32)[None, :]
    )
    weights = jnp.where(causal[None], scores * jnp.exp(decay_gaps), 0.0).astype(jnp.bfloat16)
    inside = jnp.einsum("hts,shd->thd", weights, value_sub, preferred_element_type=jnp.float32)
    scaled = query_sub.astype(jnp.float32) * jnp.exp(cumulated)[:, :, None]
    carried = jnp.einsum("thd,hde->the", scaled, kv_state, precision=lax.Precision.HIGHEST)
    last_decay = cumulated[-1]
    key_scaled = (
        key_sub.astype(jnp.float32) * jnp.exp(last_decay[None, :] - cumulated)[:, :, None]
    ).astype(jnp.bfloat16)
    update = jnp.einsum("shd,she->hde", key_scaled, value_sub, preferred_element_type=jnp.float32)
    kv_state = jnp.exp(last_decay)[:, None, None] * kv_state + update
    reach_decay = jnp.exp(offset[None, :] + cumulated)
    return ((kv_state, offset + last_decay), (inside + carried, reach_decay))


def normalize(outputs):
    mean_square = jnp.mean(outputs * outputs, axis=-1, keepdims=True)
    return (outputs * lax.rsqrt(mean_square + 1e-06)).astype(jnp.bfloat16)


def local(queries, key_rows, value_rows, log_decay, out_weight, expert_ids, flagged, direction):
    block_rows = queries.shape[0]
    local_width = queries.shape[1]
    local_heads = local_width // HEAD
    sub_count = block_rows // SUB
    model_cols = out_weight.shape[0]

    def shaped(operand):
        return operand.reshape(sub_count, SUB, local_heads, HEAD)

    start_state = (
        jnp.zeros((local_heads, HEAD, HEAD), jnp.float32),
        jnp.zeros((local_heads,), jnp.float32),
    )
    scanned = lax.scan(
        local_step,
        start_state,
        (
            shaped(queries),
            shaped(key_rows),
            shaped(value_rows),
            log_decay.reshape(sub_count, SUB, local_heads),
        ),
    )
    local_state, total_decay = scanned[0]
    partial_out, reach_decay = scanned[1]
    block_gain = jnp.exp(total_decay)

    def pass_state(hop_index, incoming):
        passed = block_gain[:, None, None] * incoming + local_state
        return passed_along(passed, "ctx", 1)

    incoming = lax.fori_loop(0, lax.axis_size("ctx") - 1, pass_state, jnp.zeros_like(local_state))
    scaled = shaped(queries).astype(jnp.float32) * reach_decay[..., None]
    outputs = partial_out + jnp.einsum(
        "cthd,hde->cthe", scaled, incoming, precision=lax.Precision.HIGHEST
    )
    attended = normalize(outputs).reshape(block_rows, local_width)
    projected = lax.dot_general(
        lax.all_gather(attended, "ep", axis=1, tiled=True),
        out_weight,
        (((1,), (1,)), ((), ())),
        preferred_element_type=jnp.float32,
    ).astype(jnp.bfloat16)
    ctx_start = lax.axis_index("ctx") * block_rows
    local_flags = flagged - ctx_start
    experts_all = lax.axis_size("ep") * EXP_DEV
    capacity = 2 * block_rows * TOP // experts_all
    flat_ids = expert_ids.reshape(-1)
    matches = (flat_ids[:, None] == jnp.arange(experts_all, dtype=jnp.int32)[None, :]).astype(
        jnp.int32
    )
    slot_index = jnp.sum((jnp.cumsum(matches, axis=0) - matches) * matches, axis=1)
    source = jnp.arange(block_rows * TOP, dtype=jnp.int32) // TOP
    picked = projected[local_flags].astype(jnp.float32)
    partial_dot = jnp.dot(picked, direction, precision=lax.Precision.HIGHEST)
    products, norm_square = lax.psum((partial_dot, jnp.sum(direction * direction)), "ep")
    norm_square = norm_square + 1e-06
    removed = (picked - (products / norm_square)[:, None] * direction[None, :]).astype(jnp.bfloat16)
    ablated = projected.at[local_flags].set(removed)
    tile_rows = (
        jnp.zeros((experts_all, capacity, model_cols), jnp.bfloat16)
        .at[flat_ids, slot_index]
        .set(ablated[source])
    )
    return lax.all_to_all(tile_rows, "ep", split_axis=0, concat_axis=2, tiled=True)


def solution(mesh):
    placed = (
        P("ctx", "ep"),
        P("ctx", "ep"),
        P("ctx", "ep"),
        P("ctx", "ep"),
        P("ep", None),
        P("ctx", None),
        P("ctx"),
        P("ep"),
    )
    return jax.shard_map(
        local, mesh=mesh, in_specs=placed, out_specs=P("ep", "ctx", None), check_vma=False
    )
```

profile of v0, /device:TPU:1, one launch (start us, length us, event | category | flops | bytes accessed | tf_op | source)
XLA Modules:
  0.0 367.0 jit_solution(16979535435469610121)
XLA Ops:
  6.5 0.8 reshape.196
  7.4 0.6 reduce-window.16
  8.0 0.2 slice_reduce_fusion.1
  8.2 0.2 reduce-window.19
  8.4 0.2 slice_reduce_fusion.2
  8.7 1.0 copy.80
  9.7 1.1 convolution_add_fusion
  10.8 2.1 fusion.5
  12.9 2.2 fusion.4
  15.1 104.7 %while.2 = (s32[]{:T(128)}, f32[2,128,128]{2,1,0:T(8,128)S(1)}, f32[2]{0:T(128)S(1)}, f32[2,128,128]{2,1,0:T(8,128)S(1)}, s32[]{:T(128)}) while((s32[]{:T(128)}, f32[2,128,128]{2,1,0:T(8,128)S(1)}, f32[2]{0:T(128)S(1)}, f32[2,128,128]{2,1,0:T(8,128)S(1)}, s32[]{:T(128)}) %tuple.25), condition=%wide.region_6.7_spmd, body=%wide.region_5.6_spmd.sunk | while | flops 65538 | bytes 917613 | solution.py:81
  15.2 4.4 %collective-permute-start = (f32[2,128,128]{2,1,0:T(8,128)S(1)}, f32[2,128,128]{2,1,0:T(8,128)S(1)}, u32[]{:S(2)}, u32[]{:S(2)}) collective-permute-start(f32[2,128,128]{2,1,0:T(8,128)S(1)} %multiply_add_fusion.2), channel_id=1, source_target_pairs={{0,32},{32,64},{64,96},{96,128},{128,160},{160,192},{192,224},{224... | collective-permute-start | bytes 393224 | tf_op jit(solution)/shard_map/while/body/eval_jaxpr/ppermute | solution.py:15
  19.6 1.9 collective-permute-done
  21.6 3.8 %collective-permute-start = (f32[2,128,128]{2,1,0:T(8,128)S(1)}, f32[2,128,128]{2,1,0:T(8,128)S(1)}, u32[]{:S(2)}, u32[]{:S(2)}) collective-permute-start(f32[2,128,128]{2,1,0:T(8,128)S(1)} %multiply_add_fusion.2), channel_id=1, source_target_pairs={{0,32},{32,64},{64,96},{96,128},{128,160},{160,192},{192,224},{224... | collective-permute-start | bytes 393224 | tf_op jit(solution)/shard_map/while/body/eval_jaxpr/ppermute | solution.py:15
  25.4 1.9 collective-permute-done
  27.4 4.1 %collective-permute-start = (f32[2,128,128]{2,1,0:T(8,128)S(1)}, f32[2,128,128]{2,1,0:T(8,128)S(1)}, u32[]{:S(2)}, u32[]{:S(2)}) collective-permute-start(f32[2,128,128]{2,1,0:T(8,128)S(1)} %multiply_add_fusion.2), channel_id=1, source_target_pairs={{0,32},{32,64},{64,96},{96,128},{128,160},{160,192},{192,224},{224... | collective-permute-start | bytes 393224 | tf_op jit(solution)/shard_map/while/body/eval_jaxpr/ppermute | solution.py:15
  31.5 2.3 collective-permute-done
  33.8 3.9 %collective-permute-start = (f32[2,128,128]{2,1,0:T(8,128)S(1)}, f32[2,128,128]{2,1,0:T(8,128)S(1)}, u32[]{:S(2)}, u32[]{:S(2)}) collective-permute-start(f32[2,128,128]{2,1,0:T(8,128)S(1)} %multiply_add_fusion.2), channel_id=1, source_target_pairs={{0,32},{32,64},{64,96},{96,128},{128,160},{160,192},{192,224},{224... | collective-permute-start | bytes 393224 | tf_op jit(solution)/shard_map/while/body/eval_jaxpr/ppermute | solution.py:15
  37.7 3.2 collective-permute-done
  41.0 4.1 %collective-permute-start = (f32[2,128,128]{2,1,0:T(8,128)S(1)}, f32[2,128,128]{2,1,0:T(8,128)S(1)}, u32[]{:S(2)}, u32[]{:S(2)}) collective-permute-start(f32[2,128,128]{2,1,0:T(8,128)S(1)} %multiply_add_fusion.2), channel_id=1, source_target_pairs={{0,32},{32,64},{64,96},{96,128},{128,160},{160,192},{192,224},{224... | collective-permute-start | bytes 393224 | tf_op jit(solution)/shard_map/while/body/eval_jaxpr/ppermute | solution.py:15
  45.1 2.4 collective-permute-done
  47.6 4.5 %collective-permute-start = (f32[2,128,128]{2,1,0:T(8,128)S(1)}, f32[2,128,128]{2,1,0:T(8,128)S(1)}, u32[]{:S(2)}, u32[]{:S(2)}) collective-permute-start(f32[2,128,128]{2,1,0:T(8,128)S(1)} %multiply_add_fusion.2), channel_id=1, source_target_pairs={{0,32},{32,64},{64,96},{96,128},{128,160},{160,192},{192,224},{224... | collective-permute-start | bytes 393224 | tf_op jit(solution)/shard_map/while/body/eval_jaxpr/ppermute | solution.py:15
  52.1 1.9 collective-permute-done
  54.1 5.0 %collective-permute-start = (f32[2,128,128]{2,1,0:T(8,128)S(1)}, f32[2,128,128]{2,1,0:T(8,128)S(1)}, u32[]{:S(2)}, u32[]{:S(2)}) collective-permute-start(f32[2,128,128]{2,1,0:T(8,128)S(1)} %multiply_add_fusion.2), channel_id=1, source_target_pairs={{0,32},{32,64},{64,96},{96,128},{128,160},{160,192},{192,224},{224... | collective-permute-start | bytes 393224 | tf_op jit(solution)/shard_map/while/body/eval_jaxpr/ppermute | solution.py:15
  59.1 1.9 collective-permute-done
  61.1 5.4 %collective-permute-start = (f32[2,128,128]{2,1,0:T(8,128)S(1)}, f32[2,128,128]{2,1,0:T(8,128)S(1)}, u32[]{:S(2)}, u32[]{:S(2)}) collective-permute-start(f32[2,128,128]{2,1,0:T(8,128)S(1)} %multiply_add_fusion.2), channel_id=1, source_target_pairs={{0,32},{32,64},{64,96},{96,128},{128,160},{160,192},{192,224},{224... | collective-permute-start | bytes 393224 | tf_op jit(solution)/shard_map/while/body/eval_jaxpr/ppermute | solution.py:15
  66.4 2.3 collective-permute-done
  68.8 6.1 %collective-permute-start = (f32[2,128,128]{2,1,0:T(8,128)S(1)}, f32[2,128,128]{2,1,0:T(8,128)S(1)}, u32[]{:S(2)}, u32[]{:S(2)}) collective-permute-start(f32[2,128,128]{2,1,0:T(8,128)S(1)} %multiply_add_fusion.2), channel_id=1, source_target_pairs={{0,32},{32,64},{64,96},{96,128},{128,160},{160,192},{192,224},{224... | collective-permute-start | bytes 393224 | tf_op jit(solution)/shard_map/while/body/eval_jaxpr/ppermute | solution.py:15
  75.0 2.3 collective-permute-done
  77.3 4.6 %collective-permute-start = (f32[2,128,128]{2,1,0:T(8,128)S(1)}, f32[2,128,128]{2,1,0:T(8,128)S(1)}, u32[]{:S(2)}, u32[]{:S(2)}) collective-permute-start(f32[2,128,128]{2,1,0:T(8,128)S(1)} %multiply_add_fusion.2), channel_id=1, source_target_pairs={{0,32},{32,64},{64,96},{96,128},{128,160},{160,192},{192,224},{224... | collective-permute-start | bytes 393224 | tf_op jit(solution)/shard_map/while/body/eval_jaxpr/ppermute | solution.py:15
  82.0 1.9 collective-permute-done
  84.0 4.7 %collective-permute-start = (f32[2,128,128]{2,1,0:T(8,128)S(1)}, f32[2,128,128]{2,1,0:T(8,128)S(1)}, u32[]{:S(2)}, u32[]{:S(2)}) collective-permute-start(f32[2,128,128]{2,1,0:T(8,128)S(1)} %multiply_add_fusion.2), channel_id=1, source_target_pairs={{0,32},{32,64},{64,96},{96,128},{128,160},{160,192},{192,224},{224... | collective-permute-start | bytes 393224 | tf_op jit(solution)/shard_map/while/body/eval_jaxpr/ppermute | solution.py:15
  88.7 1.9 collective-permute-done
  90.7 5.3 %collective-permute-start = (f32[2,128,128]{2,1,0:T(8,128)S(1)}, f32[2,128,128]{2,1,0:T(8,128)S(1)}, u32[]{:S(2)}, u32[]{:S(2)}) collective-permute-start(f32[2,128,128]{2,1,0:T(8,128)S(1)} %multiply_add_fusion.2), channel_id=1, source_target_pairs={{0,32},{32,64},{64,96},{96,128},{128,160},{160,192},{192,224},{224... | collective-permute-start | bytes 393224 | tf_op jit(solution)/shard_map/while/body/eval_jaxpr/ppermute | solution.py:15
  96.1 1.9 collective-permute-done
  98.1 5.0 %collective-permute-start = (f32[2,128,128]{2,1,0:T(8,128)S(1)}, f32[2,128,128]{2,1,0:T(8,128)S(1)}, u32[]{:S(2)}, u32[]{:S(2)}) collective-permute-start(f32[2,128,128]{2,1,0:T(8,128)S(1)} %multiply_add_fusion.2), channel_id=1, source_target_pairs={{0,32},{32,64},{64,96},{96,128},{128,160},{160,192},{192,224},{224... | collective-permute-start | bytes 393224 | tf_op jit(solution)/shard_map/while/body/eval_jaxpr/ppermute | solution.py:15
  103.1 1.9 collective-permute-done
  105.1 5.0 %collective-permute-start = (f32[2,128,128]{2,1,0:T(8,128)S(1)}, f32[2,128,128]{2,1,0:T(8,128)S(1)}, u32[]{:S(2)}, u32[]{:S(2)}) collective-permute-start(f32[2,128,128]{2,1,0:T(8,128)S(1)} %multiply_add_fusion.2), channel_id=1, source_target_pairs={{0,32},{32,64},{64,96},{96,128},{128,160},{160,192},{192,224},{224... | collective-permute-start | bytes 393224 | tf_op jit(solution)/shard_map/while/body/eval_jaxpr/ppermute | solution.py:15
  110.1 1.9 collective-permute-done
  112.1 5.0 %collective-permute-start = (f32[2,128,128]{2,1,0:T(8,128)S(1)}, f32[2,128,128]{2,1,0:T(8,128)S(1)}, u32[]{:S(2)}, u32[]{:S(2)}) collective-permute-start(f32[2,128,128]{2,1,0:T(8,128)S(1)} %multiply_add_fusion.2), channel_id=1, source_target_pairs={{0,32},{32,64},{64,96},{96,128},{128,160},{160,192},{192,224},{224... | collective-permute-start | bytes 393224 | tf_op jit(solution)/shard_map/while/body/eval_jaxpr/ppermute | solution.py:15
  117.1 2.7 collective-permute-done
  119.8 1.5 multiply_reduce_fusion
  121.4 0.7 multiply_convert_fusion
  122.1 0.1 copy.63
  122.2 0.1 eq.29
  122.4 0.1 eq.25
  122.5 0.1 reshape.194
  122.7 1.2 reduce-window.14
  123.9 0.2 slice_reduce_fusion
  124.1 0.6 multiply_reduce_fusion.1
  124.8 0.7 compare_select_fusion.3
  125.4 0.1 fusion.31
  125.6 84.9 %all-gather.2.cloned.1.call-done = bf16[256,8192]{0,1:T(8,128)(2,1)} async-done(((bf16[256,256]{0,1:T(8,128)(2,1)}), bf16[256,8192]{0,1:T(8,128)(2,1)}) %all-gather.2.cloned.1.call-update) | async-done | bytes 4194320 | tf_op jit(solution)/shard_map/all_gather | solution.py:88
  210.5 3.2 convolution_convert_fusion
  213.7 0.1 copy.76
  213.8 0.7 gather_fusion
  214.5 0.1 convolution_bitcast_fusion.2
  214.6 62.8 %all-reduce = (f32[64]{0:T(128)S(1)}, f32[]{:T(128)}) all-reduce(f32[64]{0:T(128)S(1)} %convolution_bitcast_fusion.2, f32[]{:T(128)} %multiply_reduce_fusion.1), channel_id=1, replica_groups=mesh['ctx'=16,'ep'=32] {'ep'}, use_global_device_ids=true, to_apply=%region_8.9 | all-reduce | flops 65 | bytes 520 | tf_op jit(solution)/shard_map/psum | solution.py:105
  278.1 1.0 scatter_custom_fusion
  279.1 2.0 gather_fusion.1
  281.1 0.9 broadcast_in_dim.44
  281.9 56.4 %scatter_fusion = bf16[32,32,192]{2,1,0:T(8,128)(2,1)} fusion(bf16[32,32,192]{2,1,0:T(8,128)(2,1)} %broadcast_in_dim.44, s32[512]{0:T(512)S(1)} %bitcast.109, bf16[512,192]{1,0:T(8,128)(2,1)S(1)} %gather_fusion.1), kind=kCustom, calls=%fused_computation.3 | custom fusion | bytes 593920 | tf_op jit(solution)/shard_map/scatter | solution.py:112
  338.3 18.4 %all_to_all.18 = bf16[32,32,192]{2,1,0:T(8,128)(2,1)S(1)} all-to-all(bf16[32,32,192]{2,1,0:T(8,128)(2,1)} %scatter_fusion), channel_id=1, replica_groups=mesh['ctx'=16,'ep'=32] {'ep'}, dimensions={0} | all-to-all | bytes 786432 | tf_op jit(solution)/shard_map/all_to_all | solution.py:114
  356.7 1.1 copy.77
  357.7 2.4 all_to_all.16
  (38 shorter events, 1.5 us)
Async XLA Ops:
  6.5 204.0 %copy-start = (bf16[192,8192]{1,0:T(8,128)(2,1)S(1)}, bf16[192,8192]{1,0:T(8,128)(2,1)}, u32[]{:S(2)}) copy-start(bf16[192,8192]{1,0:T(8,128)(2,1)} %param.14) | copy-start | bytes 9437188
  6.5 115.5 %copy-start.1 = (s32[256,2]{0,1:T(2,128)S(1)}, s32[256,2]{0,1:T(2,128)}, u32[]{:S(2)}) copy-start(s32[256,2]{0,1:T(2,128)} %param.15) | copy-start | bytes 6148
  6.5 117.6 %copy-start.2 = (f32[192]{0:T(256)S(1)}, f32[192]{0:T(256)}, u32[]{:S(2)}) copy-start(f32[192]{0:T(256)} %param.17) | copy-start | bytes 2308
  6.5 204.0 %all-gather.2.cloned.1.call-start = ((), (), s32[]{:S(2)}) async-start(), calls=%async_computation.1 | async-start | bytes 4325376 | tf_op jit(solution)/shard_map/all_gather | solution.py:88
  15.2 6.3 %collective-permute-start = (f32[2,128,128]{2,1,0:T(8,128)S(1)}, f32[2,128,128]{2,1,0:T(8,128)S(1)}, u32[]{:S(2)}, u32[]{:S(2)}) collective-permute-start(f32[2,128,128]{2,1,0:T(8,128)S(1)} %multiply_add_fusion.2), channel_id=1, source_target_pairs={{0,32},{32,64},{64,96},{96,128},{128,160},{160,192},{192,224},{224... | collective-permute-start | bytes 393224 | tf_op jit(solution)/shard_map/while/body/eval_jaxpr/ppermute | solution.py:15
  21.6 5.7 %collective-permute-start = (f32[2,128,128]{2,1,0:T(8,128)S(1)}, f32[2,128,128]{2,1,0:T(8,128)S(1)}, u32[]{:S(2)}, u32[]{:S(2)}) collective-permute-start(f32[2,128,128]{2,1,0:T(8,128)S(1)} %multiply_add_fusion.2), channel_id=1, source_target_pairs={{0,32},{32,64},{64,96},{96,128},{128,160},{160,192},{192,224},{224... | collective-permute-start | bytes 393224 | tf_op jit(solution)/shard_map/while/body/eval_jaxpr/ppermute | solution.py:15
  27.4 6.4 %collective-permute-start = (f32[2,128,128]{2,1,0:T(8,128)S(1)}, f32[2,128,128]{2,1,0:T(8,128)S(1)}, u32[]{:S(2)}, u32[]{:S(2)}) collective-permute-start(f32[2,128,128]{2,1,0:T(8,128)S(1)} %multiply_add_fusion.2), channel_id=1, source_target_pairs={{0,32},{32,64},{64,96},{96,128},{128,160},{160,192},{192,224},{224... | collective-permute-start | bytes 393224 | tf_op jit(solution)/shard_map/while/body/eval_jaxpr/ppermute | solution.py:15
  33.8 7.1 %collective-permute-start = (f32[2,128,128]{2,1,0:T(8,128)S(1)}, f32[2,128,128]{2,1,0:T(8,128)S(1)}, u32[]{:S(2)}, u32[]{:S(2)}) collective-permute-start(f32[2,128,128]{2,1,0:T(8,128)S(1)} %multiply_add_fusion.2), channel_id=1, source_target_pairs={{0,32},{32,64},{64,96},{96,128},{128,160},{160,192},{192,224},{224... | collective-permute-start | bytes 393224 | tf_op jit(solution)/shard_map/while/body/eval_jaxpr/ppermute | solution.py:15
  41.0 6.5 %collective-permute-start = (f32[2,128,128]{2,1,0:T(8,128)S(1)}, f32[2,128,128]{2,1,0:T(8,128)S(1)}, u32[]{:S(2)}, u32[]{:S(2)}) collective-permute-start(f32[2,128,128]{2,1,0:T(8,128)S(1)} %multiply_add_fusion.2), channel_id=1, source_target_pairs={{0,32},{32,64},{64,96},{96,128},{128,160},{160,192},{192,224},{224... | collective-permute-start | bytes 393224 | tf_op jit(solution)/shard_map/while/body/eval_jaxpr/ppermute | solution.py:15
  47.6 6.4 %collective-permute-start = (f32[2,128,128]{2,1,0:T(8,128)S(1)}, f32[2,128,128]{2,1,0:T(8,128)S(1)}, u32[]{:S(2)}, u32[]{:S(2)}) collective-permute-start(f32[2,128,128]{2,1,0:T(8,128)S(1)} %multiply_add_fusion.2), channel_id=1, source_target_pairs={{0,32},{32,64},{64,96},{96,128},{128,160},{160,192},{192,224},{224... | collective-permute-start | bytes 393224 | tf_op jit(solution)/shard_map/while/body/eval_jaxpr/ppermute | solution.py:15
  54.1 6.9 %collective-permute-start = (f32[2,128,128]{2,1,0:T(8,128)S(1)}, f32[2,128,128]{2,1,0:T(8,128)S(1)}, u32[]{:S(2)}, u32[]{:S(2)}) collective-permute-start(f32[2,128,128]{2,1,0:T(8,128)S(1)} %multiply_add_fusion.2), channel_id=1, source_target_pairs={{0,32},{32,64},{64,96},{96,128},{128,160},{160,192},{192,224},{224... | collective-permute-start | bytes 393224 | tf_op jit(solution)/shard_map/while/body/eval_jaxpr/ppermute | solution.py:15
  61.1 7.7 %collective-permute-start = (f32[2,128,128]{2,1,0:T(8,128)S(1)}, f32[2,128,128]{2,1,0:T(8,128)S(1)}, u32[]{:S(2)}, u32[]{:S(2)}) collective-permute-start(f32[2,128,128]{2,1,0:T(8,128)S(1)} %multiply_add_fusion.2), channel_id=1, source_target_pairs={{0,32},{32,64},{64,96},{96,128},{128,160},{160,192},{192,224},{224... | collective-permute-start | bytes 393224 | tf_op jit(solution)/shard_map/while/body/eval_jaxpr/ppermute | solution.py:15
  68.8 8.4 %collective-permute-start = (f32[2,128,128]{2,1,0:T(8,128)S(1)}, f32[2,128,128]{2,1,0:T(8,128)S(1)}, u32[]{:S(2)}, u32[]{:S(2)}) collective-permute-start(f32[2,128,128]{2,1,0:T(8,128)S(1)} %multiply_add_fusion.2), channel_id=1, source_target_pairs={{0,32},{32,64},{64,96},{96,128},{128,160},{160,192},{192,224},{224... | collective-permute-start | bytes 393224 | tf_op jit(solution)/shard_map/while/body/eval_jaxpr/ppermute | solution.py:15
  77.3 6.5 %collective-permute-start = (f32[2,128,128]{2,1,0:T(8,128)S(1)}, f32[2,128,128]{2,1,0:T(8,128)S(1)}, u32[]{:S(2)}, u32[]{:S(2)}) collective-permute-start(f32[2,128,128]{2,1,0:T(8,128)S(1)} %multiply_add_fusion.2), channel_id=1, source_target_pairs={{0,32},{32,64},{64,96},{96,128},{128,160},{160,192},{192,224},{224... | collective-permute-start | bytes 393224 | tf_op jit(solution)/shard_map/while/body/eval_jaxpr/ppermute | solution.py:15
  84.0 6.7 %collective-permute-start = (f32[2,128,128]{2,1,0:T(8,128)S(1)}, f32[2,128,128]{2,1,0:T(8,128)S(1)}, u32[]{:S(2)}, u32[]{:S(2)}) collective-permute-start(f32[2,128,128]{2,1,0:T(8,128)S(1)} %multiply_add_fusion.2), channel_id=1, source_target_pairs={{0,32},{32,64},{64,96},{96,128},{128,160},{160,192},{192,224},{224... | collective-permute-start | bytes 393224 | tf_op jit(solution)/shard_map/while/body/eval_jaxpr/ppermute | solution.py:15
  90.7 7.3 %collective-permute-start = (f32[2,128,128]{2,1,0:T(8,128)S(1)}, f32[2,128,128]{2,1,0:T(8,128)S(1)}, u32[]{:S(2)}, u32[]{:S(2)}) collective-permute-start(f32[2,128,128]{2,1,0:T(8,128)S(1)} %multiply_add_fusion.2), channel_id=1, source_target_pairs={{0,32},{32,64},{64,96},{96,128},{128,160},{160,192},{192,224},{224... | collective-permute-start | bytes 393224 | tf_op jit(solution)/shard_map/while/body/eval_jaxpr/ppermute | solution.py:15
  98.1 6.9 %collective-permute-start = (f32[2,128,128]{2,1,0:T(8,128)S(1)}, f32[2,128,128]{2,1,0:T(8,128)S(1)}, u32[]{:S(2)}, u32[]{:S(2)}) collective-permute-start(f32[2,128,128]{2,1,0:T(8,128)S(1)} %multiply_add_fusion.2), channel_id=1, source_target_pairs={{0,32},{32,64},{64,96},{96,128},{128,160},{160,192},{192,224},{224... | collective-permute-start | bytes 393224 | tf_op jit(solution)/shard_map/while/body/eval_jaxpr/ppermute | solution.py:15
  105.1 6.9 %collective-permute-start = (f32[2,128,128]{2,1,0:T(8,128)S(1)}, f32[2,128,128]{2,1,0:T(8,128)S(1)}, u32[]{:S(2)}, u32[]{:S(2)}) collective-permute-start(f32[2,128,128]{2,1,0:T(8,128)S(1)} %multiply_add_fusion.2), channel_id=1, source_target_pairs={{0,32},{32,64},{64,96},{96,128},{128,160},{160,192},{192,224},{224... | collective-permute-start | bytes 393224 | tf_op jit(solution)/shard_map/while/body/eval_jaxpr/ppermute | solution.py:15
  112.1 7.7 %collective-permute-start = (f32[2,128,128]{2,1,0:T(8,128)S(1)}, f32[2,128,128]{2,1,0:T(8,128)S(1)}, u32[]{:S(2)}, u32[]{:S(2)}) collective-permute-start(f32[2,128,128]{2,1,0:T(8,128)S(1)} %multiply_add_fusion.2), channel_id=1, source_target_pairs={{0,32},{32,64},{64,96},{96,128},{128,160},{160,192},{192,224},{224... | collective-permute-start | bytes 393224 | tf_op jit(solution)/shard_map/while/body/eval_jaxpr/ppermute | solution.py:15
Sparse Core Ops, SparseCore 0:
  122.2 88.2 all-gather.1
where the time goes:
time: 369 us; the launch traced here: 367 us
  waiting for transfers between devices  117 us (32%)
  blocking collectives  81.2 us (22%)
  starting transfers between devices  70.8 us (19%)
  local copies, waits for them, and re-layouts  66.5 us (18%)
  between operations  14.2 us (4%)
  matrix products  10.2 us (3%)
  other arithmetic  6.49 us (2%)
    all_gather x1, waiting for transfers between devices, local(): lax.all_gather(attended, 'ep', axis=1, tiled=True)  84.9 us
    ppermute x15, starting transfers between devices, passed_along(): lax.ppermute(value, axis, [(source, source + steps) for source in range(l...  70.8 us
    psum x1, blocking collectives, local(): lax.psum((partial_dot, jnp.sum(direction * direction)), 'ep')  62.8 us
    scatter x1, local copies, waits for them, and re-layouts, local(): tile_rows = jnp.zeros((experts_all, capacity, model_cols), jnp.bfloat16)....  56.4 us
    ppermute x15, waiting for transfers between devices, passed_along(): lax.ppermute(value, axis, [(source, source + steps) for source in range(l...  32.4 us
    all_to_all x1, blocking collectives, local(): lax.all_to_all(tile_rows, 'ep', split_axis=0, concat_axis=2, tiled=True)  18.4 us
  transfers between devices with their start and end apart: 16, of which 16 were waited for; matrix products, arithmetic and copies ran while one was open for 1% of the time, Pallas kernels for 0%

commit v1 on v0

--- a/solution.py
+++ b/solution.py
@@ -7,12 +7,8 @@
 TOP = 2
 EXP_DEV = 1
 SUB = 256
-
-
-def passed_along(value, axis, steps):
-    count = lax.axis_size(axis)
-    leading, last = (max(0, -steps), min(count, count - steps))
-    return lax.ppermute(value, axis, [(source, source + steps) for source in range(leading, last)])
+PAD_ROWS = 8
+PARTS = 3
 
 
 def local_step(carried_in, pieces):
@@ -46,12 +42,34 @@
     return (outputs * lax.rsqrt(mean_square + 1e-06)).astype(jnp.bfloat16)
 
 
+def split_parts(values, width):
+    pieces = []
+    rest = values
+    for _ in range(PARTS):
+        part = lax.reduce_precision(rest, exponent_bits=8, mantissa_bits=7)
+        pieces.append(part)
+        rest = rest - part
+    stacked = jnp.stack(pieces).astype(jnp.bfloat16)
+    return jnp.pad(stacked, ((0, PAD_ROWS - PARTS), (0, width - values.shape[0])))
+
+
+def joined_parts(rows, width, used):
+    pieces = rows.astype(jnp.float32).reshape(PARTS, -1, width)[:, :, :used].reshape(PARTS, -1)
+    total = pieces[0]
+    for part in range(1, PARTS):
+        total = total + pieces[part]
+    return total
+
+
 def local(queries, key_rows, value_rows, log_decay, out_weight, expert_ids, flagged, direction):
     block_rows = queries.shape[0]
     local_width = queries.shape[1]
     local_heads = local_width // HEAD
     sub_count = block_rows // SUB
     model_cols = out_weight.shape[0]
+    ctx_count = lax.axis_size("ctx")
+    ctx_index = lax.axis_index("ctx")
+    ep_index = lax.axis_index("ep")
 
     def shaped(operand):
         return operand.reshape(sub_count, SUB, local_heads, HEAD)
@@ -72,26 +90,36 @@
     )
     local_state, total_decay = scanned[0]
     partial_out, reach_decay = scanned[1]
-    block_gain = jnp.exp(total_decay)
 
-    def pass_state(hop_index, incoming):
-        passed = block_gain[:, None, None] * incoming + local_state
-        return passed_along(passed, "ctx", 1)
+    packed = jnp.concatenate(
+        [local_state, jnp.broadcast_to(total_decay[:, None, None], (local_heads, PAD_ROWS, HEAD))],
+        axis=1,
+    )
+    gathered = lax.all_gather(packed, "ctx", axis=0)
+    states = gathered[:, :, :HEAD, :]
+    gains = jnp.exp(gathered[:, :, HEAD, 0])
+    incoming = jnp.zeros_like(local_state)
+    for source in range(ctx_count - 1):
+        folded = gains[source][:, None, None] * incoming + states[source]
+        incoming = jnp.where(source < ctx_index, folded, incoming)
 
-    incoming = lax.fori_loop(0, lax.axis_size("ctx") - 1, pass_state, jnp.zeros_like(local_state))
     scaled = shaped(queries).astype(jnp.float32) * reach_decay[..., None]
     outputs = partial_out + jnp.einsum(
         "cthd,hde->cthe", scaled, incoming, precision=lax.Precision.HIGHEST
     )
     attended = normalize(outputs).reshape(block_rows, local_width)
+    riders = split_parts(direction, local_width)
+    gathered_rows = lax.all_gather(
+        jnp.concatenate([attended, riders], axis=0), "ep", axis=1, tiled=True
+    )
     projected = lax.dot_general(
-        lax.all_gather(attended, "ep", axis=1, tiled=True),
+        gathered_rows,
         out_weight,
         (((1,), (1,)), ((), ())),
         preferred_element_type=jnp.float32,
-    ).astype(jnp.bfloat16)
-    ctx_start = lax.axis_index("ctx") * block_rows
-    local_flags = flagged - ctx_start
+    ).astype(jnp.bfloat16)[:block_rows]
+    direction_full = joined_parts(gathered_rows[block_rows : block_rows + PARTS], local_width, model_cols)
+
     experts_all = lax.axis_size("ep") * EXP_DEV
     capacity = 2 * block_rows * TOP // experts_all
     flat_ids = expert_ids.reshape(-1)
@@ -99,19 +127,37 @@
         jnp.int32
     )
     slot_index = jnp.sum((jnp.cumsum(matches, axis=0) - matches) * matches, axis=1)
+    position = (flat_ids * capacity + slot_index).reshape(block_rows, TOP)
+    places = jnp.arange(experts_all * capacity, dtype=jnp.int32)[:, None]
+    chosen = (position[None, :, 0] == places) | (position[None, :, 1] == places)
+    for pick in range(2, TOP):
+        chosen = chosen | (position[None, :, pick] == places)
+    tile_rows = jnp.dot(
+        chosen.astype(jnp.bfloat16), projected, preferred_element_type=jnp.float32
+    ).astype(jnp.bfloat16)
+    tile_rows = tile_rows.reshape(experts_all, capacity, model_cols)
+    received = lax.all_to_all(tile_rows, "ep", split_axis=0, concat_axis=2, tiled=True)
+
+    local_flags = flagged - ctx_index * block_rows
+    token_flag = jnp.any(
+        local_flags[None, :] == jnp.arange(block_rows, dtype=jnp.int32)[:, None], axis=1
+    )
     source = jnp.arange(block_rows * TOP, dtype=jnp.int32) // TOP
-    picked = projected[local_flags].astype(jnp.float32)
-    partial_dot = jnp.dot(picked, direction, precision=lax.Precision.HIGHEST)
-    products, norm_square = lax.psum((partial_dot, jnp.sum(direction * direction)), "ep")
-    norm_square = norm_square + 1e-06
-    removed = (picked - (products / norm_square)[:, None] * direction[None, :]).astype(jnp.bfloat16)
-    ablated = projected.at[local_flags].set(removed)
-    tile_rows = (
-        jnp.zeros((experts_all, capacity, model_cols), jnp.bfloat16)
-        .at[flat_ids, slot_index]
-        .set(ablated[source])
-    )
-    return lax.all_to_all(tile_rows, "ep", split_axis=0, concat_axis=2, tiled=True)
+    owned = (flat_ids // EXP_DEV == ep_index) & token_flag[source]
+    slot_ids = (flat_ids % EXP_DEV) * capacity + slot_index
+    slot_flag = jnp.any(
+        owned[None, :]
+        & (slot_ids[None, :] == jnp.arange(EXP_DEV * capacity, dtype=jnp.int32)[:, None]),
+        axis=1,
+    ).reshape(EXP_DEV, capacity)
+
+    norm_square = jnp.sum(direction_full * direction_full) + 1e-06
+    rows = received.astype(jnp.float32)
+    products = jnp.einsum("ecm,m->ec", rows, direction_full, precision=lax.Precision.HIGHEST)
+    removed = (
+        rows - (products / norm_square)[:, :, None] * direction_full[None, None, :]
+    ).astype(jnp.bfloat16)
+    return jnp.where(slot_flag[:, :, None], removed, received)
 
 
 def solution(mesh):

time: 369 us -> 224 us (0.61)
  blocking collectives: 81.2 us -> 0 us
  starting transfers between devices: 70.8 us -> 5.53 us
  local copies, waits for them, and re-layouts: 66.5 us -> 42.2 us
  waiting for transfers between devices: 117 us -> 138 us
    ppermute x15 -> x0, starting transfers between devices: 70.8 us -> none  [passed_along(): lax.ppermute(value, axis, [(source, source + steps) for source in range(l...]
    psum x1 -> x0, blocking collectives: 62.8 us -> none  [local(): lax.psum((partial_dot, jnp.sum(direction * direction)), 'ep')]
    scatter x1 -> x0, local copies, waits for them, and re-layouts: 56.4 us -> none  [local(): tile_rows = jnp.zeros((experts_all, capacity, model_cols), jnp.bfloat16)....]
    all_gather x1 -> x2, waiting for transfers between devices: 84.9 us -> 129 us  [the longest x1 64.7 us: local(): lax.all_gather(jnp.concatenate([attended, riders], axis=0), 'ep', axis=1,...]
    ppermute x15 -> x0, waiting for transfers between devices: 32.4 us -> none  [passed_along(): lax.ppermute(value, axis, [(source, source + steps) for source in range(l...]
    unnamed x8 -> x33, local copies, waits for them, and re-layouts: 0.15 us -> 25.8 us
    all_to_all x1 -> x0, blocking collectives: 18.4 us -> none  [local(): lax.all_to_all(tile_rows, 'ep', split_axis=0, concat_axis=2, tiled=True)]
    all_to_all x0 -> x1, waiting for transfers between devices: none -> 8.63 us  [local(): lax.all_to_all(tile_rows, 'ep', split_axis=0, concat_axis=2, tiled=True)]
  transfers between devices with their start and end apart: 16 -> 3, of which waited for: 16 -> 3; matrix products, arithmetic and copies ran while one was open for 1% -> 6% of each run, Pallas kernels for 0% -> 0%
where the time goes in v1:
time: 224 us; the launch traced here: 223 us
  waiting for transfers between devices  138 us (62%)
  local copies, waits for them, and re-layouts  42.2 us (19%)
  between operations  14.4 us (6%)
  matrix products  13.4 us (6%)
  other arithmetic  9.81 us (4%)
  starting transfers between devices  5.53 us (2%)
    all_gather x1, waiting for transfers between devices, local(): lax.all_gather(jnp.concatenate([attended, riders], axis=0), 'ep', axis=1,...  64.7 us
    all_gather x1, waiting for transfers between devices, local(): gathered = lax.all_gather(packed, 'ctx', axis=0)  64.2 us
    unnamed x33, local copies, waits for them, and re-layouts  25.8 us
    all_to_all x1, waiting for transfers between devices, local(): lax.all_to_all(tile_rows, 'ep', split_axis=0, concat_axis=2, tiled=True)  8.63 us
    all_to_all x1, starting transfers between devices, local(): lax.all_to_all(tile_rows, 'ep', split_axis=0, concat_axis=2, tiled=True)  5.48 us
  transfers between devices with their start and end apart: 3, of which 3 were waited for; matrix products, arithmetic and copies ran while one was open for 6% of the time, Pallas kernels for 0%

profile of v1, /device:TPU:1, one launch (start us, length us, event | category | flops | bytes accessed | tf_op | source)
XLA Modules:
  0.0 222.9 jit_solution(571478284537935060)
XLA Ops:
  6.5 0.8 reshape.366
  7.4 0.6 reduce-window.16
  8.0 0.2 slice_reduce_fusion.1
  8.2 0.2 reduce-window.19
  8.3 0.1 add_bitcast_fusion.1
  8.4 0.2 slice_reduce_fusion.2
  8.6 0.1 subtract_exponential_fusion
  8.7 1.0 copy.242
  9.7 1.1 convolution_add_fusion
  10.8 0.1 broadcast_in_dim.49
  10.9 0.7 pad_maximum_fusion
  11.7 0.7 reduce-precision_convert_fusion.1
  12.4 0.6 fusion.128
  13.0 2.1 fusion.5
  15.1 1.5 fusion.4
  16.6 64.2 %all-gather.6.cloned.1.call-done = f32[32,136,128]{2,1,0:T(8,128)} async-done(((f32[2,136,128]{2,1,0:T(8,128)}), f32[32,136,128]{2,1,0:T(8,128)}) %all-gather.6.cloned.1.call-update) | async-done | bytes 2228240 | tf_op jit(solution)/shard_map/all_gather | solution.py:98
  80.8 0.9 slice.218
  81.7 2.9 %fusion.136 = (f32[1,2,128,128]{3,2,1,0:T(8,128)}, f32[1,2,128,128]{3,2,1,0:T(8,128)}, f32[1,2,128,128]{3,2,1,0:T(8,128)}, f32[1,2,128,128]{3,2,1,0:T(8,128)}, f...) fusion(f32[16,2,136,128]{3,2,1,0:T(8,128)} %bitcast.284), kind=kLoop, calls=%fused_computation.201 | loop fusion | bytes 3932160 | tf_op jit(solution)/shard_map/slice | solution.py:103
  84.6 0.8 copy.226
  85.4 0.7 exp.30
  86.1 0.6 slice_bitcast_fusion.13
  86.7 1.7 copy.227
  88.4 1.6 copy.239
  90.0 1.7 copy.238
  91.7 1.7 copy.237
  93.3 1.7 copy.236
  95.0 1.7 copy.235
  96.6 1.7 copy.234
  98.3 1.7 copy.233
  100.0 1.6 copy.232
  101.6 1.7 copy.231
  103.3 1.6 copy.230
  104.9 1.7 copy.229
  106.6 1.6 copy.228
  108.2 1.7 copy.241
  109.9 1.7 copy.240
  111.5 2.3 %multiply_reduce_fusion = (f32[256,2]{0,1:T(2,128)S(1)}, f32[1,256,2,128]{1,3,2,0:T(8,128)S(1)}) fusion(f32[1,256,2,128]{1,3,2,0:T(8,128)S(1)} %fusion.4, f32[256,2]{0,1:T(2,128)S(1)} %copy-done.4, f32[1,2,128,128]{2,3,1,0:T(8,128)} %copy.241, f32[1,2,128,128]{2,3,1,0:T(8,128)} %copy.240, f32[1,2,128,128]{2,3,1,0:T(8,128)} %copy.239, ...), kind=kOutput, calls=%fused_computation.27 | convolution fusion | flops 102432256 | bytes 2625671 | tf_op jit(solution)/shard_map/cthd,hde->cthe/dot_general | solution.py:107
  113.9 0.1 copy.225
  114.0 0.7 pad_maximum_fusion.1
  114.7 0.1 copy.195
  114.8 0.1 reshape.364
  115.0 0.1 eq.99
  115.2 1.2 reduce-window.14
  116.3 0.2 slice_reduce_fusion
  116.6 0.1 fusion.82
  116.7 0.1 reduce_sum.30
  116.9 0.1 copy.198
  117.0 0.7 broadcast_subtract_fusion
  117.6 0.1 fusion.100
  117.7 3.4 %gather_fusion = pred[512]{0:T(512)(128)(4,1)S(1)} fusion(pred[256]{0:T(512)(128)(4,1)S(1)} %fusion.100, s32[1024]{0:T(1024)S(1)} %pad_clamp_fusion), kind=kCustom, calls=%fused_computation | custom fusion | bytes 3072 | tf_op jit(solution)/shard_map/gather | solution.py:146
  121.1 0.1 fusion.103
  121.2 64.7 %all-gather.4.cloned.1.call-done = bf16[264,8192]{1,0:T(8,128)(2,1)} async-done(((bf16[264,256]{1,0:T(8,128)(2,1)}), bf16[264,8192]{1,0:T(8,128)(2,1)}) %all-gather.4.cloned.1.call-update) | async-done | bytes 4325392 | tf_op jit(solution)/shard_map/all_gather | solution.py:112
  186.0 4.5 %fusion.138 = bf16[264,192]{0,1:T(8,128)(2,1)S(1)} fusion(bf16[264,8192]{1,0:T(8,128)(2,1)} %all-gather.4.cloned.1.call-done, bf16[192,8192]{1,0:T(8,128)(2,1)S(1)} %copy-done), kind=kOutput, calls=%fused_computation.203 | convolution fusion | flops 830472192 | bytes 7572480 | tf_op jit(solution)/shard_map/dot_general | solution.py:115
  190.4 0.4 convolution_convert_fusion
  190.9 1.0 copy.222
  191.9 5.5 %all-to-all-start = ((bf16[32,32,192]{2,1,0:T(8,128)(2,1)}), bf16[32,32,192]{2,1,0:T(8,128)(2,1)}, u32[]{:S(2)}, u32[]{:S(2)}) async-start(bf16[32,32,192]{2,1,0:T(8,128)(2,1)} %bitcast.282), calls=%async_computation | async-start | bytes 1048576 | tf_op jit(solution)/shard_map/all_to_all | solution.py:139
  197.4 0.9 slice_convert_fusion.2
  198.3 0.7 multiply_reduce_fusion.1
  199.0 0.7 add.172
  200.4 8.6 %all-to-all-done = bf16[32,32,192]{2,1,0:T(8,128)(2,1)} async-done(((bf16[32,32,192]{2,1,0:T(8,128)(2,1)}), bf16[32,32,192]{2,1,0:T(8,128)(2,1)}, u32[]{:S(2)}, u32[]{:S(2)}) %all-to-all-start) | async-done | bytes 393248 | tf_op jit(solution)/shard_map/all_to_all | solution.py:139
  209.0 2.1 copy.223
  211.1 1.7 all_to_all.16
  212.8 1.6 fusion.7
  214.4 1.7 fusion.10
  (35 shorter events, 0.3 us)
Async XLA Ops:
  6.5 179.4 %copy-start = (bf16[192,8192]{1,0:T(8,128)(2,1)S(1)}, bf16[192,8192]{1,0:T(8,128)(2,1)}, u32[]{:S(2)}) copy-start(bf16[192,8192]{1,0:T(8,128)(2,1)} %param.12) | copy-start | bytes 9437188
  6.5 74.2 %all-gather.6.cloned.1.call-start = ((), (), s32[]{:S(2)}) async-start(), calls=%async_computation.2 | async-start | bytes 2367488 | tf_op jit(solution)/shard_map/all_gather | solution.py:98
  8.7 72.1 %copy-start.3 = (f32[256,2]{0,1:T(2,128)}, f32[256,2]{0,1:T(2,128)S(1)}, u32[]{:S(2)}) copy-start(f32[256,2]{0,1:T(2,128)S(1)} %get-tuple-element.65) | copy-start | bytes 6148
  11.6 174.4 %all-gather.4.cloned.1.call-start = ((), (), s32[]{:S(2)}) async-start(), calls=%async_computation.1 | async-start | bytes 4460544 | tf_op jit(solution)/shard_map/all_gather | solution.py:112
  81.7 29.9 %copy-start.1 = (bf16[256,256]{1,0:T(8,128)(2,1)S(1)}, bf16[256,256]{1,0:T(8,128)(2,1)}, u32[]{:S(2)}) copy-start(bf16[256,256]{1,0:T(8,128)(2,1)} %param.8) | copy-start | bytes 393220
  85.4 26.2 %copy-start.4 = (f32[256,2]{0,1:T(2,128)S(1)}, f32[256,2]{0,1:T(2,128)}, u32[]{:S(2)}) copy-start(f32[256,2]{0,1:T(2,128)} %copy-done.3) | copy-start | bytes 6148
  93.3 20.7 %copy-start.5 = (bf16[8,256]{1,0:T(8,128)(2,1)S(1)}, bf16[8,256]{1,0:T(8,128)(2,1)}, u32[]{:S(2)}) copy-start(bf16[8,256]{1,0:T(8,128)(2,1)} %fusion.128) | copy-start | bytes 12292
  95.0 19.7 %copy-start.6 = (s32[256,2]{0,1:T(2,128)S(1)}, s32[256,2]{0,1:T(2,128)}, u32[]{:S(2)}) copy-start(s32[256,2]{0,1:T(2,128)} %param.13) | copy-start | bytes 6148
  191.9 17.1 %all-to-all-start = ((bf16[32,32,192]{2,1,0:T(8,128)(2,1)}), bf16[32,32,192]{2,1,0:T(8,128)(2,1)}, u32[]{:S(2)}, u32[]{:S(2)}) async-start(bf16[32,32,192]{2,1,0:T(8,128)(2,1)} %bitcast.282), calls=%async_computation | async-start | bytes 1048576 | tf_op jit(solution)/shard_map/all_to_all | solution.py:139
  199.0 10.0 %copy-start.2 = (f32[1,32,192]{2,1,0:T(8,128)}, f32[1,32,192]{2,1,0:T(8,128)S(1)}, u32[]{:S(2)}) copy-start(f32[1,32,192]{2,1,0:T(8,128)S(1)} %get-tuple-element.22) | copy-start | bytes 73732
Sparse Core Ops, SparseCore 0:
  11.7 69.0 all-gather.5
  114.8 71.0 all-gather.3

commit v2 on v1

--- a/solution.py
+++ b/solution.py
@@ -40,6 +40,18 @@
 def normalize(outputs):
     mean_square = jnp.mean(outputs * outputs, axis=-1, keepdims=True)
     return (outputs * lax.rsqrt(mean_square + 1e-06)).astype(jnp.bfloat16)
+
+
+def passed_along(value, axis, steps):
+    count = lax.axis_size(axis)
+    return lax.ppermute(value, axis, [(source, source + steps) for source in range(count - steps)])
+
+
+def combined(left, right):
+    right_log = right[:, HEAD:, :]
+    gain = jnp.exp(right_log[:, :1, :1])
+    state = gain * left[:, :HEAD, :] + right[:, :HEAD, :]
+    return jnp.concatenate([state, right_log + left[:, HEAD:, :]], axis=1)
 
 
 def split_parts(values, width):
@@ -95,13 +107,18 @@
         [local_state, jnp.broadcast_to(total_decay[:, None, None], (local_heads, PAD_ROWS, HEAD))],
         axis=1,
     )
-    gathered = lax.all_gather(packed, "ctx", axis=0)
-    states = gathered[:, :, :HEAD, :]
-    gains = jnp.exp(gathered[:, :, HEAD, 0])
-    incoming = jnp.zeros_like(local_state)
-    for source in range(ctx_count - 1):
-        folded = gains[source][:, None, None] * incoming + states[source]
-        incoming = jnp.where(source < ctx_index, folded, incoming)
+    inclusive = packed
+    exclusive = None
+    distance = 1
+    while distance < ctx_count:
+        arrived = passed_along(inclusive, "ctx", distance)
+        exclusive = arrived if exclusive is None else combined(arrived, exclusive)
+        if 2 * distance < ctx_count:
+            inclusive = combined(arrived, inclusive)
+        distance *= 2
+    incoming = (
+        jnp.zeros_like(local_state) if exclusive is None else exclusive[:, :HEAD, :]
+    )
 
     scaled = shaped(queries).astype(jnp.float32) * reach_decay[..., None]
     outputs = partial_out + jnp.einsum(

time: 224 us -> 177 us (0.79)
  waiting for transfers between devices: 138 us -> 83.1 us
  starting transfers between devices: 5.53 us -> 42.9 us
  local copies, waits for them, and re-layouts: 42.2 us -> 13.1 us
    all_gather x1 -> x0, waiting for transfers between devices: 64.2 us -> none  [local(): gathered = lax.all_gather(packed, 'ctx', axis=0)]
    ppermute x0 -> x4, starting transfers between devices: none -> 37.4 us  [passed_along(): lax.ppermute(value, axis, [(source, source + steps) for source in range(c...]
    unnamed x33 -> x19, local copies, waits for them, and re-layouts: 25.8 us -> 0.19 us
    all_gather x1, waiting for transfers between devices: 64.7 us -> 70 us  [local(): lax.all_gather(jnp.concatenate([attended, riders], axis=0), 'ep', axis=1,...]
    ppermute x0 -> x4, waiting for transfers between devices: none -> 4.4 us  [passed_along(): lax.ppermute(value, axis, [(source, source + steps) for source in range(c...]
    slice x2 -> x0, local copies, waits for them, and re-layouts: 3.79 us -> none  [the longest x1 2.87 us: local(): folded = gains[source][:, None, None] * incoming + states[source]]
    add x0 -> x5, other arithmetic: none -> 2.24 us  [the longest x2 1.36 us: combined(): return jnp.concatenate([state, right_log + left[:, HEAD:, :]], axis=1)]
  transfers between devices with their start and end apart: 3 -> 6, of which waited for: 3 -> 5; matrix products, arithmetic and copies ran while one was open for 6% -> 8% of each run, Pallas kernels for 0% -> 0%
where the time goes in v2:
time: 177 us
  waiting for transfers between devices  83.1 us (47%)
  starting transfers between devices  42.9 us (24%)
  between operations  14.4 us (8%)
  local copies, waits for them, and re-layouts  13.1 us (7%)
  matrix products  11.8 us (7%)
  other arithmetic  11.5 us (6%)
    all_gather x1, waiting for transfers between devices, local(): lax.all_gather(jnp.concatenate([attended, riders], axis=0), 'ep', axis=1,...  70 us
    ppermute x4, starting transfers between devices, passed_along(): lax.ppermute(value, axis, [(source, source + steps) for source in range(c...  37.4 us
    all_to_all x1, waiting for transfers between devices, local(): lax.all_to_all(tile_rows, 'ep', split_axis=0, concat_axis=2, tiled=True)  8.63 us
    all_to_all x1, starting transfers between devices, local(): lax.all_to_all(tile_rows, 'ep', split_axis=0, concat_axis=2, tiled=True)  5.48 us
    dot_general x1, matrix products, local(): lax.dot_general(gathered_rows, out_weight, (((1,), (1,)), ((), ())), pref...  4.47 us
    ppermute x4, waiting for transfers between devices, passed_along(): lax.ppermute(value, axis, [(source, source + steps) for source in range(c...  4.4 us
    all_to_all x2, local copies, waits for them, and re-layouts, local(): lax.all_to_all(tile_rows, 'ep', split_axis=0, concat_axis=2, tiled=True)  3.8 us
  transfers between devices with their start and end apart: 6, of which 5 were waited for; matrix products, arithmetic and copies ran while one was open for 8% of the time, Pallas kernels for 0%

profile of v2, /device:TPU:1, one launch (start us, length us, event | category | flops | bytes accessed | tf_op | source)
XLA Modules:
  0.0 176.7 jit_solution(10965975187130654311)
XLA Ops:
  6.5 0.8 reshape.320
  7.4 0.6 reduce-window.16
  8.0 0.2 slice_reduce_fusion.1
  8.2 0.2 reduce-window.19
  8.3 0.1 add_bitcast_fusion.1
  8.4 0.2 slice_reduce_fusion.2
  8.6 0.6 fusion.78
  9.2 0.0 copy-done.6
  9.2 0.1 subtract_exponential_fusion
  9.2 1.0 copy.103
  10.3 1.1 convolution_add_fusion
  11.4 0.7 broadcast_in_dim.77
  12.1 0.7 pad_maximum_fusion
  12.7 4.4 %collective-permute-start = (f32[2,136,128]{2,1,0:T(8,128)}, f32[2,136,128]{2,1,0:T(8,128)S(1)}, u32[]{:S(2)}, u32[]{:S(2)}) collective-permute-start(f32[2,136,128]{2,1,0:T(8,128)} %pad_maximum_fusion), channel_id=1, source_target_pairs={{0,32},{32,64},{64,96},{96,128},{128,160},{160,192},{192,224},{224... | collective-permute-start | bytes 417800 | tf_op jit(solution)/shard_map/ppermute | solution.py:47
  17.1 0.6 iota_compare_fusion.3
  17.7 2.2 %fusion.5 = f32[256,2,128]{0,2,1:T(8,128)} fusion(bf16[256,2,128]{0,2,1:T(8,128)(2,1)} %bitcast.122, f32[2,256]{1,0:T(2,128)} %bitcast.129, pred[256,256]{1,0:T(8,128)(4,1)} %iota_compare_fusion.3, bf16[256,256]{1,0:T(8,128)(2,1)} %param.10, bf16[256,256]{1,0:T(8,128)(2,1)} %param.8), kind=kOutput, calls=%fused_computation.10 | convolution fusion | flops 67764224 | bytes 722944 | tf_op jit(solution)/shard_map/while/body/eval_jaxpr/hts,shd->thd/dot_general | solution.py:27
  19.9 0.7 reduce-precision_convert_fusion.1
  20.6 0.0 collective-permute-done
  20.6 0.7 slice_add_fusion.4
  21.3 0.7 multiply_add_fusion.2
  22.0 0.0 copy-start.7
  22.0 4.9 %collective-permute-start.1 = (f32[2,136,128]{2,1,0:T(8,128)S(1)}, f32[2,136,128]{2,1,0:T(8,128)S(1)}, u32[]{:S(2)}, u32[]{:S(2)}) collective-permute-start(f32[2,136,128]{2,1,0:T(8,128)S(1)} %pad_maximum_fusion.1), channel_id=1, source_target_pairs={{0,64},{32,96},{64,128},{96,160},{128,192},{160,224},{192,256},{22... | collective-permute-start | bytes 417800 | tf_op jit(solution)/shard_map/ppermute | solution.py:47
  26.9 1.5 fusion.4
  28.5 0.1 fusion.69
  28.6 0.3 collective-permute-done.1
  28.9 0.7 slice_add_fusion.3
  29.6 0.1 multiply_add_fusion.1
  29.7 15.0 %collective-permute-start.2 = (f32[2,136,128]{2,1,0:T(8,128)S(1)}, f32[2,136,128]{2,1,0:T(8,128)S(1)}, u32[]{:S(2)}, u32[]{:S(2)}) collective-permute-start(f32[2,136,128]{2,1,0:T(8,128)S(1)} %pad_maximum_fusion.2), channel_id=1, source_target_pairs={{0,128},{32,160},{64,192},{96,224},{128,256},{160,288},{192,320},{... | collective-permute-start | bytes 417800 | tf_op jit(solution)/shard_map/ppermute | solution.py:47
  44.7 0.1 fusion.70
  44.8 2.3 %collective-permute-done.2 = f32[2,136,128]{2,1,0:T(8,128)S(1)} collective-permute-done((f32[2,136,128]{2,1,0:T(8,128)S(1)}, f32[2,136,128]{2,1,0:T(8,128)S(1)}, u32[]{:S(2)}, u32[]{:S(2)}) %collective-permute-start.2) | collective-permute-done | bytes 139296 | tf_op jit(solution)/shard_map/ppermute | solution.py:47
  47.1 0.1 multiply_add_fusion
  47.2 13.2 %collective-permute-start.3 = (f32[2,136,128]{2,1,0:T(8,128)S(1)}, f32[2,136,128]{2,1,0:T(8,128)S(1)}, u32[]{:S(2)}, u32[]{:S(2)}) collective-permute-start(f32[2,136,128]{2,1,0:T(8,128)S(1)} %pad_maximum_fusion.3), channel_id=1, source_target_pairs={{0,256},{32,288},{64,320},{96,352},{128,384},{160,416},{192,448},{... | collective-permute-start | bytes 417800 | tf_op jit(solution)/shard_map/ppermute | solution.py:47
  60.4 0.1 fusion.71
  60.5 0.1 fusion.72
  60.6 1.8 %collective-permute-done.3 = f32[2,136,128]{2,1,0:T(8,128)S(1)} collective-permute-done((f32[2,136,128]{2,1,0:T(8,128)S(1)}, f32[2,136,128]{2,1,0:T(8,128)S(1)}, u32[]{:S(2)}, u32[]{:S(2)}) %collective-permute-start.3) | collective-permute-done | bytes 139296 | tf_op jit(solution)/shard_map/ppermute | solution.py:47
  62.4 0.6 multiply_reduce_fusion
  63.0 0.1 copy.102
  63.1 0.7 pad_maximum_fusion.4
  63.8 0.0 all-gather.2.cloned.1.call-update
  63.8 0.0 copy-done.4
  63.8 0.1 copy.86
  64.0 0.1 reshape.318
  64.1 0.1 eq.99
  64.3 1.2 reduce-window.14
  65.4 0.2 slice_reduce_fusion
  65.7 0.1 fusion.47
  65.8 0.1 reduce_sum.30
  66.0 0.1 copy.89
  66.1 0.1 fusion.52
  66.2 3.4 %gather_fusion = pred[512]{0:T(512)(128)(4,1)S(1)} fusion(pred[256]{0:T(512)(128)(4,1)S(1)} %fusion.52, s32[1024]{0:T(1024)S(1)} %pad_clamp_fusion), kind=kCustom, calls=%fused_computation | custom fusion | bytes 3072 | tf_op jit(solution)/shard_map/gather | solution.py:163
  69.6 0.1 fusion.55
  69.7 70.0 %all-gather.2.cloned.1.call-done = bf16[264,8192]{1,0:T(8,128)(2,1)} async-done(((bf16[264,256]{1,0:T(8,128)(2,1)}), bf16[264,8192]{1,0:T(8,128)(2,1)}) %all-gather.2.cloned.1.call-update) | async-done | bytes 4325392 | tf_op jit(solution)/shard_map/all_gather | solution.py:129
  139.7 4.5 %fusion.79 = bf16[264,192]{0,1:T(8,128)(2,1)S(1)} fusion(bf16[264,8192]{1,0:T(8,128)(2,1)} %all-gather.2.cloned.1.call-done, bf16[192,8192]{1,0:T(8,128)(2,1)S(1)} %copy-done), kind=kOutput, calls=%fused_computation.144 | convolution fusion | flops 830472192 | bytes 7572480 | tf_op jit(solution)/shard_map/dot_general | solution.py:132
  144.2 0.4 convolution_convert_fusion
  144.6 1.0 copy.98
  145.6 5.5 %all-to-all-start = ((bf16[32,32,192]{2,1,0:T(8,128)(2,1)}), bf16[32,32,192]{2,1,0:T(8,128)(2,1)}, u32[]{:S(2)}, u32[]{:S(2)}) async-start(bf16[32,32,192]{2,1,0:T(8,128)(2,1)} %bitcast.118), calls=%async_computation | async-start | bytes 1048576 | tf_op jit(solution)/shard_map/all_to_all | solution.py:156
  151.1 0.9 slice_convert_fusion.2
  152.1 0.7 multiply_reduce_fusion.1
  152.8 0.7 add.156
  154.1 8.6 %all-to-all-done = bf16[32,32,192]{2,1,0:T(8,128)(2,1)} async-done(((bf16[32,32,192]{2,1,0:T(8,128)(2,1)}), bf16[32,32,192]{2,1,0:T(8,128)(2,1)}, u32[]{:S(2)}, u32[]{:S(2)}) %all-to-all-start) | async-done | bytes 393248 | tf_op jit(solution)/shard_map/all_to_all | solution.py:156
  162.8 2.1 %copy.99 = bf16[1,32,32,192]{3,2,1,0:T(8,128)(2,1)} copy(bf16[1,32,32,192]{3,1,2,0:T(8,128)(2,1)} %bitcast.14) | data formatting | bytes 786432 | tf_op jit(solution)/shard_map/all_to_all | solution.py:156
  164.9 1.7 all_to_all.16
  166.6 1.6 fusion.7
  168.1 1.7 fusion.10
  (35 shorter events, 0.2 us)
Async XLA Ops:
  6.5 133.2 %copy-start = (bf16[192,8192]{1,0:T(8,128)(2,1)S(1)}, bf16[192,8192]{1,0:T(8,128)(2,1)}, u32[]{:S(2)}) copy-start(bf16[192,8192]{1,0:T(8,128)(2,1)} %param.12) | copy-start | bytes 9437188
  6.5 55.9 %copy-start.1 = (bf16[256,256]{1,0:T(8,128)(2,1)S(1)}, bf16[256,256]{1,0:T(8,128)(2,1)}, u32[]{:S(2)}) copy-start(bf16[256,256]{1,0:T(8,128)(2,1)} %param.8) | copy-start | bytes 393220
  6.5 57.3 %copy-start.4 = (s32[256,2]{0,1:T(2,128)S(1)}, s32[256,2]{0,1:T(2,128)}, u32[]{:S(2)}) copy-start(s32[256,2]{0,1:T(2,128)} %param.13) | copy-start | bytes 6148
  6.5 133.2 %all-gather.2.cloned.1.call-start = ((), (), s32[]{:S(2)}) async-start(), calls=%async_computation.1 | async-start | bytes 4460544 | tf_op jit(solution)/shard_map/all_gather | solution.py:129
  8.4 0.7 copy-start.6
  8.6 0.6 copy-start.5
  10.3 1.8 %copy-start.2 = (bf16[256,256]{0,1:T(8,128)(2,1)}, bf16[256,256]{0,1:T(8,128)(2,1)S(1)}, u32[]{:S(2)}) copy-start(bf16[256,256]{0,1:T(8,128)(2,1)S(1)} %copy.103) | copy-start | bytes 393220
  12.7 7.9 %collective-permute-start = (f32[2,136,128]{2,1,0:T(8,128)}, f32[2,136,128]{2,1,0:T(8,128)S(1)}, u32[]{:S(2)}, u32[]{:S(2)}) collective-permute-start(f32[2,136,128]{2,1,0:T(8,128)} %pad_maximum_fusion), channel_id=1, source_target_pairs={{0,32},{32,64},{64,96},{96,128},{128,160},{160,192},{192,224},{224... | collective-permute-start | bytes 417800 | tf_op jit(solution)/shard_map/ppermute | solution.py:47
  22.0 44.1 %copy-start.7 = (s32[64]{0:T(128)S(1)}, s32[64]{0:T(128)}, u32[]{:S(2)}) copy-start(s32[64]{0:T(128)} %param.14) | copy-start | bytes 772
  22.0 6.9 %collective-permute-start.1 = (f32[2,136,128]{2,1,0:T(8,128)S(1)}, f32[2,136,128]{2,1,0:T(8,128)S(1)}, u32[]{:S(2)}, u32[]{:S(2)}) collective-permute-start(f32[2,136,128]{2,1,0:T(8,128)S(1)} %pad_maximum_fusion.1), channel_id=1, source_target_pairs={{0,64},{32,96},{64,128},{96,160},{128,192},{160,224},{192,256},{22... | collective-permute-start | bytes 417800 | tf_op jit(solution)/shard_map/ppermute | solution.py:47
  29.7 17.4 %collective-permute-start.2 = (f32[2,136,128]{2,1,0:T(8,128)S(1)}, f32[2,136,128]{2,1,0:T(8,128)S(1)}, u32[]{:S(2)}, u32[]{:S(2)}) collective-permute-start(f32[2,136,128]{2,1,0:T(8,128)S(1)} %pad_maximum_fusion.2), channel_id=1, source_target_pairs={{0,128},{32,160},{64,192},{96,224},{128,256},{160,288},{192,320},{... | collective-permute-start | bytes 417800 | tf_op jit(solution)/shard_map/ppermute | solution.py:47
  47.2 15.2 %collective-permute-start.3 = (f32[2,136,128]{2,1,0:T(8,128)S(1)}, f32[2,136,128]{2,1,0:T(8,128)S(1)}, u32[]{:S(2)}, u32[]{:S(2)}) collective-permute-start(f32[2,136,128]{2,1,0:T(8,128)S(1)} %pad_maximum_fusion.3), channel_id=1, source_target_pairs={{0,256},{32,288},{64,320},{96,352},{128,384},{160,416},{192,448},{... | collective-permute-start | bytes 417800 | tf_op jit(solution)/shard_map/ppermute | solution.py:47
  145.6 17.1 %all-to-all-start = ((bf16[32,32,192]{2,1,0:T(8,128)(2,1)}), bf16[32,32,192]{2,1,0:T(8,128)(2,1)}, u32[]{:S(2)}, u32[]{:S(2)}) async-start(bf16[32,32,192]{2,1,0:T(8,128)(2,1)} %bitcast.118), calls=%async_computation | async-start | bytes 1048576 | tf_op jit(solution)/shard_map/all_to_all | solution.py:156
  152.8 10.0 %copy-start.3 = (f32[1,32,192]{2,1,0:T(8,128)}, f32[1,32,192]{2,1,0:T(8,128)S(1)}, u32[]{:S(2)}) copy-start(f32[1,32,192]{2,1,0:T(8,128)S(1)} %get-tuple-element.24) | copy-start | bytes 73732
Sparse Core Ops, SparseCore 0:
  63.9 75.7 all-gather.1

commit v3 on v2

--- a/solution.py
+++ b/solution.py
@@ -1,6 +1,8 @@
 import jax
 import jax.numpy as jnp
+import numpy as np
 from jax import lax
+from jax.sharding import Mesh
 from jax.sharding import PartitionSpec as P
 
 HEAD = 128
@@ -9,6 +11,9 @@
 SUB = 256
 PAD_ROWS = 8
 PARTS = 3
+RING = 4
+EP = ("x", "y", "core")
+OFFSETS = (0, -1, 1, 2)
 
 
 def local_step(carried_in, pieces):
@@ -54,6 +59,18 @@
     return jnp.concatenate([state, right_log + left[:, HEAD:, :]], axis=1)
 
 
+def ring_gathered(blocks, axis):
+    forward = [(i, (i + 1) % RING) for i in range(RING)]
+    backward = [(i, (i - 1) % RING) for i in range(RING)]
+    half = blocks.shape[-1] // 2
+    from_left = lax.ppermute(blocks, axis, forward)
+    from_right = lax.ppermute(blocks, axis, backward)
+    far_left = lax.ppermute(from_left[..., :half], axis, forward)
+    far_right = lax.ppermute(from_right[..., half:], axis, backward)
+    far = jnp.concatenate([far_left, far_right], axis=-1)
+    return jnp.concatenate([blocks, from_left, from_right, far], axis=0)
+
+
 def split_parts(values, width):
     pieces = []
     rest = values
@@ -81,7 +98,7 @@
     model_cols = out_weight.shape[0]
     ctx_count = lax.axis_size("ctx")
     ctx_index = lax.axis_index("ctx")
-    ep_index = lax.axis_index("ep")
+    ep_index = lax.axis_index(EP)
 
     def shaped(operand):
         return operand.reshape(sub_count, SUB, local_heads, HEAD)
@@ -126,18 +143,39 @@
     )
     attended = normalize(outputs).reshape(block_rows, local_width)
     riders = split_parts(direction, local_width)
-    gathered_rows = lax.all_gather(
-        jnp.concatenate([attended, riders], axis=0), "ep", axis=1, tiled=True
-    )
+    block = jnp.concatenate([attended, riders], axis=0)
+    near = ring_gathered(ring_gathered(block[None], "x"), "y")
+    far = lax.ppermute(near, "core", [(0, 1), (1, 0)])
+
+    offsets = jnp.asarray(OFFSETS, jnp.int32)
+    origin_x = (lax.axis_index("x") + offsets) % RING
+    origin_y = (lax.axis_index("y") + offsets) % RING
+    near_origin = ((origin_x[None, :] * RING + origin_y[:, None]) * 2).reshape(-1)
+    core_index = lax.axis_index("core")
+    origin = jnp.concatenate([near_origin + core_index, near_origin + (1 - core_index)])
+    slots = origin.shape[0]
+    weight_slots = jnp.take(out_weight.reshape(model_cols, slots, local_width), origin, axis=1)
+    half = near.shape[0]
     projected = lax.dot_general(
-        gathered_rows,
-        out_weight,
-        (((1,), (1,)), ((), ())),
+        near,
+        weight_slots[:, :half],
+        (((0, 2), (1, 2)), ((), ())),
         preferred_element_type=jnp.float32,
-    ).astype(jnp.bfloat16)[:block_rows]
-    direction_full = joined_parts(gathered_rows[block_rows : block_rows + PARTS], local_width, model_cols)
-
-    experts_all = lax.axis_size("ep") * EXP_DEV
+    ) + lax.dot_general(
+        far,
+        weight_slots[:, half:],
+        (((0, 2), (1, 2)), ((), ())),
+        preferred_element_type=jnp.float32,
+    )
+    projected = projected.astype(jnp.bfloat16)[:block_rows]
+    rider_rows = jnp.concatenate(
+        [near[:, block_rows : block_rows + PARTS], far[:, block_rows : block_rows + PARTS]], axis=0
+    )
+    reorder = (origin[None, :] == jnp.arange(slots, dtype=jnp.int32)[:, None]).astype(jnp.bfloat16)
+    ordered = jnp.einsum("os,spk->pok", reorder, rider_rows, preferred_element_type=jnp.float32)
+    direction_full = joined_parts(ordered.astype(jnp.bfloat16), local_width, model_cols)
+
+    experts_all = lax.axis_size(EP) * EXP_DEV
     capacity = 2 * block_rows * TOP // experts_all
     flat_ids = expert_ids.reshape(-1)
     matches = (flat_ids[:, None] == jnp.arange(experts_all, dtype=jnp.int32)[None, :]).astype(
@@ -153,7 +191,7 @@
         chosen.astype(jnp.bfloat16), projected, preferred_element_type=jnp.float32
     ).astype(jnp.bfloat16)
     tile_rows = tile_rows.reshape(experts_all, capacity, model_cols)
-    received = lax.all_to_all(tile_rows, "ep", split_axis=0, concat_axis=2, tiled=True)
+    received = lax.all_to_all(tile_rows, EP, split_axis=0, concat_axis=2, tiled=True)
 
     local_flags = flagged - ctx_index * block_rows
     token_flag = jnp.any(
@@ -178,16 +216,18 @@
 
 
 def solution(mesh):
+    devices = np.asarray(mesh.devices)
+    fine = Mesh(devices.reshape(devices.shape[0], RING, RING, 2), ("ctx",) + EP)
     placed = (
-        P("ctx", "ep"),
-        P("ctx", "ep"),
-        P("ctx", "ep"),
-        P("ctx", "ep"),
-        P("ep", None),
+        P("ctx", EP),
+        P("ctx", EP),
+        P("ctx", EP),
+        P("ctx", EP),
+        P(EP, None),
         P("ctx", None),
         P("ctx"),
-        P("ep"),
+        P(EP),
     )
     return jax.shard_map(
-        local, mesh=mesh, in_specs=placed, out_specs=P("ep", "ctx", None), check_vma=False
-    )
+        local, mesh=fine, in_specs=placed, out_specs=P(EP, "ctx", None), check_vma=False
+    )

time: 177 us -> 156 us (0.88); the launches traced: 177 us -> 153 us
  waiting for transfers between devices: 83.1 us -> 20.2 us
  starting transfers between devices: 42.9 us -> 83.6 us
  local copies, waits for them, and re-layouts: 13.1 us -> 27.3 us
  between operations: 14.4 us -> 1.24 us
  matrix products: 11.8 us -> 10 us
    all_gather x1 -> x0, waiting for transfers between devices: 70 us -> none  [local(): lax.all_gather(jnp.concatenate([attended, riders], axis=0), 'ep', axis=1,...]
    ppermute x0 -> x9, starting transfers between devices: none -> 42.6 us  [the longest x1 16.5 us: local(): far = lax.ppermute(near, 'core', [(0, 1), (1, 0)])]
    unnamed x19 -> x30, local copies, waits for them, and re-layouts: 0.19 us -> 7.82 us
    ppermute x0 -> x9, waiting for transfers between devices: none -> 5.61 us  [the longest x2 2.32 us: ring_gathered(): from_right = lax.ppermute(blocks, axis, backward)]
    slice x0 -> x6, local copies, waits for them, and re-layouts: none -> 3.1 us  [the longest x1 0.85 us: local(): near[:, block_rows:block_rows + PARTS]]
    all_to_all x2, local copies, waits for them, and re-layouts: 3.8 us -> 0.84 us  [local(): lax.all_to_all(tile_rows, EP, split_axis=0, concat_axis=2, tiled=True)]
    gather x0 -> x1, local copies, waits for them, and re-layouts: none -> 2.41 us  [local(): jnp.take(out_weight.reshape(model_cols, slots, local_width), origin, axis=1)]
    select_n x0 -> x2, other arithmetic: none -> 2.33 us  [local(): jnp.take(out_weight.reshape(model_cols, slots, local_width), origin, axis=1)]
  transfers between devices with their start and end apart: 6 -> 14, of which waited for: 5 -> 7; matrix products, arithmetic and copies ran while one was open for 8% -> 22% of each run, Pallas kernels for 0% -> 0%
where the time goes in v3:
time: 156 us; the launch traced here: 153 us
  starting transfers between devices  83.6 us (54%)
  local copies, waits for them, and re-layouts  27.3 us (18%)
  waiting for transfers between devices  20.2 us (13%)
  other arithmetic  10.5 us (7%)
  matrix products  10 us (6%)
    ppermute x4, starting transfers between devices, passed_along(): lax.ppermute(value, axis, [(source, source + steps) for source in range(c...  36.9 us
    ppermute x1, starting transfers between devices, local(): far = lax.ppermute(near, 'core', [(0, 1), (1, 0)])  16.5 us
    all_to_all x1, waiting for transfers between devices, local(): lax.all_to_all(tile_rows, EP, split_axis=0, concat_axis=2, tiled=True)  9.21 us
    ppermute x2, starting transfers between devices, ring_gathered(): far_right = lax.ppermute(from_right[..., half:], axis, backward)  9.07 us
    unnamed x30, local copies, waits for them, and re-layouts  7.82 us
    ppermute x2, starting transfers between devices, ring_gathered(): from_right = lax.ppermute(blocks, axis, backward)  6.66 us
    ppermute x2, starting transfers between devices, ring_gathered(): from_left = lax.ppermute(blocks, axis, forward)  6.5 us
    ppermute x4, waiting for transfers between devices, passed_along(): lax.ppermute(value, axis, [(source, source + steps) for source in range(c...  5.36 us
  transfers between devices with their start and end apart: 14, of which 7 were waited for; matrix products, arithmetic and copies ran while one was open for 22% of the time, Pallas kernels for 0%

profile of v3, /device:TPU:1, one launch (start us, length us, event | category | flops | bytes accessed | tf_op | source)
XLA Modules:
  0.0 152.9 jit_solution(5547296155486215841)
XLA Ops:
  0.0 0.7 reshape.438
  0.7 0.6 reduce-window.16
  1.8 0.2 slice_reduce_fusion.2
  2.0 1.0 copy.113
  3.1 1.1 convolution_add_fusion
  4.2 4.4 %collective-permute-start = (f32[2,136,128]{2,1,0:T(8,128)S(1)}, f32[2,136,128]{2,1,0:T(8,128)S(1)}, u32[]{:S(2)}, u32[]{:S(2)}) collective-permute-start(f32[2,136,128]{2,1,0:T(8,128)S(1)} %pad_maximum_fusion), channel_id=1, source_target_pairs={{0,32},{32,64},{64,96},{96,128},{128,160},{160,192},{192,224},{224... | collective-permute-start | bytes 417800 | tf_op jit(solution)/shard_map/ppermute | solution.py:52
  8.6 0.8 copy.95
  9.6 0.7 reduce-precision_convert_fusion.1
  10.3 1.3 fusion.15
  11.8 4.9 %collective-permute-start.1 = (f32[2,136,128]{2,1,0:T(8,128)S(1)}, f32[2,136,128]{2,1,0:T(8,128)S(1)}, u32[]{:S(2)}, u32[]{:S(2)}) collective-permute-start(f32[2,136,128]{2,1,0:T(8,128)S(1)} %pad_maximum_fusion.1), channel_id=1, source_target_pairs={{0,64},{32,96},{64,128},{96,160},{128,192},{160,224},{192,256},{22... | collective-permute-start | bytes 417800 | tf_op jit(solution)/shard_map/ppermute | solution.py:52
  16.7 0.5 fusion.14
  17.4 1.4 collective-permute-done.1
  18.9 15.0 %collective-permute-start.2 = (f32[2,136,128]{2,1,0:T(8,128)S(1)}, f32[2,136,128]{2,1,0:T(8,128)S(1)}, u32[]{:S(2)}, u32[]{:S(2)}) collective-permute-start(f32[2,136,128]{2,1,0:T(8,128)S(1)} %pad_maximum_fusion.2), channel_id=1, source_target_pairs={{0,128},{32,160},{64,192},{96,224},{128,256},{160,288},{192,320},{... | collective-permute-start | bytes 417800 | tf_op jit(solution)/shard_map/ppermute | solution.py:52
  34.0 2.2 %collective-permute-done.2 = f32[2,136,128]{2,1,0:T(8,128)S(1)} collective-permute-done((f32[2,136,128]{2,1,0:T(8,128)S(1)}, f32[2,136,128]{2,1,0:T(8,128)S(1)}, u32[]{:S(2)}, u32[]{:S(2)}) %collective-permute-start.2) | collective-permute-done | bytes 139296 | tf_op jit(solution)/shard_map/ppermute | solution.py:52
  36.4 12.6 %collective-permute-start.3 = (f32[2,136,128]{2,1,0:T(8,128)S(1)}, f32[2,136,128]{2,1,0:T(8,128)S(1)}, u32[]{:S(2)}, u32[]{:S(2)}) collective-permute-start(f32[2,136,128]{2,1,0:T(8,128)S(1)} %pad_maximum_fusion.3), channel_id=1, source_target_pairs={{0,256},{32,288},{64,320},{96,352},{128,384},{160,416},{192,448},{... | collective-permute-start | bytes 417800 | tf_op jit(solution)/shard_map/ppermute | solution.py:52
  49.2 1.8 %collective-permute-done.3 = f32[2,136,128]{2,1,0:T(8,128)S(1)} collective-permute-done((f32[2,136,128]{2,1,0:T(8,128)S(1)}, f32[2,136,128]{2,1,0:T(8,128)S(1)}, u32[]{:S(2)}, u32[]{:S(2)}) %collective-permute-start.3) | collective-permute-done | bytes 139296 | tf_op jit(solution)/shard_map/ppermute | solution.py:52
  51.0 0.5 multiply_reduce_fusion
  51.7 3.2 %collective-permute-start.4 = (bf16[1,264,256]{2,1,0:T(8,128)(2,1)S(1)}, bf16[1,264,256]{2,1,0:T(8,128)(2,1)S(1)}, u32[]{:S(2)}, u32[]{:S(2)}) collective-permute-start(bf16[1,264,256]{2,1,0:T(8,128)(2,1)S(1)} %maximum_bitcast_fusion), channel_id=1, source_target_pairs={{0,8},{8,16},{16,24},{24,0},{1,9},{9,17},{17,25},{25,1},{2,10},{10... | collective-permute-start | bytes 405512 | tf_op jit(solution)/shard_map/ppermute | solution.py:66
  54.9 3.3 %collective-permute-start.5 = (bf16[1,264,256]{2,1,0:T(8,128)(2,1)S(1)}, bf16[1,264,256]{2,1,0:T(8,128)(2,1)S(1)}, u32[]{:S(2)}, u32[]{:S(2)}) collective-permute-start(bf16[1,264,256]{2,1,0:T(8,128)(2,1)S(1)} %maximum_bitcast_fusion), channel_id=1, source_target_pairs={{0,24},{8,0},{16,8},{24,16},{1,25},{9,1},{17,9},{25,17},{2,26},{10... | collective-permute-start | bytes 405512 | tf_op jit(solution)/shard_map/ppermute | solution.py:67
  58.4 0.7 concatenate.72
  59.1 0.6 add.302
  59.7 0.6 concatenate.71
  60.3 0.7 add.299
  60.9 1.1 reduce-window.14
  62.1 0.2 slice_reduce_fusion
  62.4 0.6 slice.162
  63.0 2.0 %collective-permute-start.6 = (bf16[1,264,128]{2,1,0:T(8,128)(2,1)}, bf16[1,264,128]{2,1,0:T(8,128)(2,1)}, u32[]{:S(2)}, u32[]{:S(2)}) collective-permute-start(bf16[1,264,128]{2,1,0:T(8,128)(2,1)} %slice.162), channel_id=1, source_target_pairs={{0,8},{8,16},{16,24},{24,0},{1,9},{9,17},{17,25},{25,1},{2,10},{10... | collective-permute-start | bytes 202760 | tf_op jit(solution)/shard_map/ppermute | solution.py:68
  65.0 0.7 slice.163
  65.7 4.5 %collective-permute-start.7 = (bf16[1,264,128]{2,1,0:T(8,128)(2,1)}, bf16[1,264,128]{2,1,0:T(8,128)(2,1)}, u32[]{:S(2)}, u32[]{:S(2)}) collective-permute-start(bf16[1,264,128]{2,1,0:T(8,128)(2,1)} %slice.163), channel_id=1, source_target_pairs={{0,24},{8,0},{16,8},{24,16},{1,25},{9,1},{17,9},{25,17},{2,26},{10... | collective-permute-start | bytes 202760 | tf_op jit(solution)/shard_map/ppermute | solution.py:69
  70.4 0.7 copy.98
  71.1 2.3 %copy.155 = bf16[24,32,8,256]{3,2,0,1:T(8,128)(2,1)S(1)} copy(bf16[24,32,8,256]{3,2,1,0:T(8,128)(2,1)} %bitcast.136) | data formatting | bytes 6291456 | tf_op jit(solution)/shard_map/reshape | solution.py:157
  73.4 1.1 maximum_maximum_fusion
  74.5 3.3 %collective-permute-start.8 = (bf16[4,264,256]{2,1,0:T(8,128)(2,1)S(1)}, bf16[4,264,256]{2,1,0:T(8,128)(2,1)S(1)}, u32[]{:S(2)}, u32[]{:S(2)}) collective-permute-start(bf16[4,264,256]{2,1,0:T(8,128)(2,1)S(1)} %maximum_maximum_fusion), channel_id=1, source_target_pairs={{0,2},{2,4},{4,6},{6,0},{1,3},{3,5},{5,7},{7,1},{8,10},{10,12},{12... | collective-permute-start | bytes 1622024 | tf_op jit(solution)/shard_map/ppermute | solution.py:66
  77.8 3.4 %collective-permute-start.9 = (bf16[4,264,256]{2,1,0:T(8,128)(2,1)S(1)}, bf16[4,264,256]{2,1,0:T(8,128)(2,1)S(1)}, u32[]{:S(2)}, u32[]{:S(2)}) collective-permute-start(bf16[4,264,256]{2,1,0:T(8,128)(2,1)S(1)} %maximum_maximum_fusion), channel_id=1, source_target_pairs={{0,6},{2,0},{4,2},{6,4},{1,7},{3,1},{5,3},{7,5},{8,14},{10,8},{12,... | collective-permute-start | bytes 1622024 | tf_op jit(solution)/shard_map/ppermute | solution.py:67
  81.2 0.6 constant_dynamic-update-slice_fusion.6
  81.8 0.7 constant_dynamic-update-slice_fusion.5
  82.5 1.6 %constant_dynamic-update-slice_fusion.4 = bf16[16,264,256]{2,1,0:T(8,128)(2,1)} fusion(bf16[16,264,256]{2,1,0:T(8,128)(2,1)} %constant_dynamic-update-slice_fusion.5, bf16[1,264,256]{2,1,0:T(8,128)(2,1)} %copy-done.1), kind=kLoop, calls=%fused_computation.109 | loop fusion | bytes 270336
  84.1 1.5 constant_dynamic-update-slice_fusion.3
  85.6 2.3 %collective-permute-done.9 = bf16[4,264,256]{2,1,0:T(8,128)(2,1)S(1)} collective-permute-done((bf16[4,264,256]{2,1,0:T(8,128)(2,1)S(1)}, bf16[4,264,256]{2,1,0:T(8,128)(2,1)S(1)}, u32[]{:S(2)}, u32[]{:S(2)}) %collective-permute-start.9) | collective-permute-done | bytes 540704 | tf_op jit(solution)/shard_map/ppermute | solution.py:67
  88.0 4.6 %collective-permute-start.11 = (bf16[4,264,128]{2,1,0:T(8,128)(2,1)S(1)}, bf16[4,264,128]{2,1,0:T(8,128)(2,1)S(1)}, u32[]{:S(2)}, u32[]{:S(2)}) collective-permute-start(bf16[4,264,128]{2,1,0:T(8,128)(2,1)S(1)} %slice.165), channel_id=1, source_target_pairs={{0,6},{2,0},{4,2},{6,4},{1,7},{3,1},{5,3},{7,5},{8,14},{10,8},{12,... | collective-permute-start | bytes 811016 | tf_op jit(solution)/shard_map/ppermute | solution.py:69
  92.6 1.9 %collective-permute-start.10 = (bf16[4,264,128]{2,1,0:T(8,128)(2,1)S(1)}, bf16[4,264,128]{2,1,0:T(8,128)(2,1)S(1)}, u32[]{:S(2)}, u32[]{:S(2)}) collective-permute-start(bf16[4,264,128]{2,1,0:T(8,128)(2,1)S(1)} %slice.164), channel_id=1, source_target_pairs={{0,2},{2,4},{4,6},{6,0},{1,3},{3,5},{5,7},{7,1},{8,10},{10,12},{12... | collective-permute-start | bytes 811016 | tf_op jit(solution)/shard_map/ppermute | solution.py:68
  94.5 1.5 constant_dynamic-update-slice_fusion.2
  96.1 0.8 constant_dynamic-update-slice_fusion.1
  96.9 0.9 constant_dynamic-update-slice_fusion
  97.7 1.1 collective-permute-done.11
  98.8 2.2 %collective-permute-done.10 = bf16[4,264,128]{2,1,0:T(8,128)(2,1)S(1)} collective-permute-done((bf16[4,264,128]{2,1,0:T(8,128)(2,1)S(1)}, bf16[4,264,128]{2,1,0:T(8,128)(2,1)S(1)}, u32[]{:S(2)}, u32[]{:S(2)}) %collective-permute-start.10) | collective-permute-done | bytes 270368 | tf_op jit(solution)/shard_map/ppermute | solution.py:68
  101.0 0.9 maximum_dynamic-update-slice_fusion
  101.9 16.5 %collective-permute-start.12 = (bf16[16,264,256]{2,1,0:T(8,128)(2,1)}, bf16[16,264,256]{2,1,0:T(8,128)(2,1)}, u32[]{:S(2)}, u32[]{:S(2)}) collective-permute-start(bf16[16,264,256]{2,1,0:T(8,128)(2,1)} %maximum_dynamic-update-slice_fusion), channel_id=1, source_target_pairs={{0,1},{1,0},{2,3},{3,2},{4,5},{5,4},{6,7},{7,6},{8,9},{9,8},{10,11... | collective-permute-start | bytes 6488072 | tf_op jit(solution)/shard_map/ppermute | solution.py:148
  118.6 2.4 %gather_fusion.1 = bf16[32,192,256]{2,1,0:T(8,128)(2,1)} fusion(bf16[192,32,256]{2,0,1:T(8,128)(2,1)S(1)} %bitcast.135, s32[1024]{0:T(1024)S(1)} %get-tuple-element.59), kind=kCustom, calls=%fused_computation.1 | custom fusion | bytes 6291584 | tf_op jit(solution)/shard_map/jit(_take)/gather | solution.py:157
  121.1 3.4 %gather_fusion = pred[512]{0:T(512)(128)(4,1)S(1)} fusion(pred[256]{0:T(512)(128)(4,1)S(1)} %fusion.66, s32[1024]{0:T(1024)S(1)} %get-tuple-element.60), kind=kCustom, calls=%fused_computation | custom fusion | bytes 3072 | tf_op jit(solution)/shard_map/gather | solution.py:201
  124.7 2.3 %select_bitcast_fusion = bf16[192,32,256]{2,0,1:T(8,128)(2,1)S(1)} fusion(bf16[32,192,256]{2,1,0:T(8,128)(2,1)} %gather_fusion.1, pred[32]{0:T(512)(128)(4,1)S(1)} %get-tuple-element.25), kind=kLoop, calls=%fused_computation.3 | loop fusion | flops 1572864 | bytes 6291488 | tf_op jit(solution)/shard_map/jit(_take)/select_n | solution.py:157
  127.0 0.9 slice.170
  127.9 2.8 %fusion.6 = f32[264,192]{0,1:T(8,128)S(1)} fusion(bf16[16,264,256]{2,1,0:T(8,128)(2,1)} %maximum_dynamic-update-slice_fusion, bf16[192,32,256]{2,0,1:T(8,128)(2,1)S(1)} %select_bitcast_fusion), kind=kOutput, calls=%fused_computation.12 | convolution fusion | flops 415236096 | bytes 3938304 | tf_op jit(solution)/shard_map/dot_general | solution.py:159
  130.7 2.8 %fusion.9 = f32[264,192]{0,1:T(8,128)S(1)} fusion(bf16[16,264,256]{2,1,0:T(8,128)(2,1)} %collective-permute-done.12, bf16[192,32,256]{2,0,1:T(8,128)(2,1)S(1)} %select_bitcast_fusion), kind=kOutput, calls=%fused_computation.13 | convolution fusion | flops 415236096 | bytes 3938304 | tf_op jit(solution)/shard_map/dot_general | solution.py:164
  133.4 0.4 convolution_convert_fusion
  133.9 1.0 copy.108
  134.9 4.1 %all-to-all-start = ((bf16[32,32,192]{2,1,0:T(8,128)(2,1)}), bf16[32,32,192]{2,1,0:T(8,128)(2,1)S(1)}, u32[]{:S(2)}, u32[]{:S(2)}) async-start(bf16[32,32,192]{2,1,0:T(8,128)(2,1)} %bitcast.17), calls=%async_computation | async-start | bytes 1048576 | tf_op jit(solution)/shard_map/all_to_all | solution.py:194
  139.0 0.9 slice.171
  140.0 0.6 multiply_reduce_fusion.1
  141.3 9.2 %all-to-all-done = bf16[32,32,192]{2,1,0:T(8,128)(2,1)S(1)} async-done(((bf16[32,32,192]{2,1,0:T(8,128)(2,1)}), bf16[32,32,192]{2,1,0:T(8,128)(2,1)S(1)}, u32[]{:S(2)}, u32[]{:S(2)}) %all-to-all-start) | async-done | bytes 393248 | tf_op jit(solution)/shard_map/all_to_all | solution.py:194
  150.5 0.3 copy.109
  150.8 0.5 all_to_all.16
  151.4 0.5 fusion.19
  151.9 1.0 fusion.22
  (83 shorter events, 3.1 us)
Async XLA Ops:
  0.0 10.3 %copy-start = (bf16[256,256]{1,0:T(8,128)(2,1)S(1)}, bf16[256,256]{1,0:T(8,128)(2,1)}, u32[]{:S(2)}) copy-start(bf16[256,256]{1,0:T(8,128)(2,1)} %param.9) | copy-start | bytes 393220
  0.0 11.6 %copy-start.9 = (s32[4]{0:T(128)S(1)}, s32[4]{0:T(128)}, u32[]{:S(2)}) copy-start(s32[4]{0:T(128)} %constant.140.clone) | copy-start | bytes 52
  4.2 7.4 %collective-permute-start = (f32[2,136,128]{2,1,0:T(8,128)S(1)}, f32[2,136,128]{2,1,0:T(8,128)S(1)}, u32[]{:S(2)}, u32[]{:S(2)}) collective-permute-start(f32[2,136,128]{2,1,0:T(8,128)S(1)} %pad_maximum_fusion), channel_id=1, source_target_pairs={{0,32},{32,64},{64,96},{96,128},{128,160},{160,192},{192,224},{224... | collective-permute-start | bytes 417800 | tf_op jit(solution)/shard_map/ppermute | solution.py:52
  11.8 6.9 %collective-permute-start.1 = (f32[2,136,128]{2,1,0:T(8,128)S(1)}, f32[2,136,128]{2,1,0:T(8,128)S(1)}, u32[]{:S(2)}, u32[]{:S(2)}) collective-permute-start(f32[2,136,128]{2,1,0:T(8,128)S(1)} %pad_maximum_fusion.1), channel_id=1, source_target_pairs={{0,64},{32,96},{64,128},{96,160},{128,192},{160,224},{192,256},{22... | collective-permute-start | bytes 417800 | tf_op jit(solution)/shard_map/ppermute | solution.py:52
  18.9 17.3 %collective-permute-start.2 = (f32[2,136,128]{2,1,0:T(8,128)S(1)}, f32[2,136,128]{2,1,0:T(8,128)S(1)}, u32[]{:S(2)}, u32[]{:S(2)}) collective-permute-start(f32[2,136,128]{2,1,0:T(8,128)S(1)} %pad_maximum_fusion.2), channel_id=1, source_target_pairs={{0,128},{32,160},{64,192},{96,224},{128,256},{160,288},{192,320},{... | collective-permute-start | bytes 417800 | tf_op jit(solution)/shard_map/ppermute | solution.py:52
  36.4 14.6 %collective-permute-start.3 = (f32[2,136,128]{2,1,0:T(8,128)S(1)}, f32[2,136,128]{2,1,0:T(8,128)S(1)}, u32[]{:S(2)}, u32[]{:S(2)}) collective-permute-start(f32[2,136,128]{2,1,0:T(8,128)S(1)} %pad_maximum_fusion.3), channel_id=1, source_target_pairs={{0,256},{32,288},{64,320},{96,352},{128,384},{160,416},{192,448},{... | collective-permute-start | bytes 417800 | tf_op jit(solution)/shard_map/ppermute | solution.py:52
  51.7 19.4 %copy-start.2 = (bf16[1,264,256]{2,1,0:T(8,128)(2,1)}, bf16[1,264,256]{2,1,0:T(8,128)(2,1)S(1)}, u32[]{:S(2)}) copy-start(bf16[1,264,256]{2,1,0:T(8,128)(2,1)S(1)} %maximum_bitcast_fusion) | copy-start | bytes 405508
  51.7 10.7 %collective-permute-start.4 = (bf16[1,264,256]{2,1,0:T(8,128)(2,1)S(1)}, bf16[1,264,256]{2,1,0:T(8,128)(2,1)S(1)}, u32[]{:S(2)}, u32[]{:S(2)}) collective-permute-start(bf16[1,264,256]{2,1,0:T(8,128)(2,1)S(1)} %maximum_bitcast_fusion), channel_id=1, source_target_pairs={{0,8},{8,16},{16,24},{24,0},{1,9},{9,17},{17,25},{25,1},{2,10},{10... | collective-permute-start | bytes 405512 | tf_op jit(solution)/shard_map/ppermute | solution.py:66
  54.9 10.1 %collective-permute-start.5 = (bf16[1,264,256]{2,1,0:T(8,128)(2,1)S(1)}, bf16[1,264,256]{2,1,0:T(8,128)(2,1)S(1)}, u32[]{:S(2)}, u32[]{:S(2)}) collective-permute-start(bf16[1,264,256]{2,1,0:T(8,128)(2,1)S(1)} %maximum_bitcast_fusion), channel_id=1, source_target_pairs={{0,24},{8,0},{16,8},{24,16},{1,25},{9,1},{17,9},{25,17},{2,26},{10... | collective-permute-start | bytes 405512 | tf_op jit(solution)/shard_map/ppermute | solution.py:67
  63.0 10.4 %collective-permute-start.6 = (bf16[1,264,128]{2,1,0:T(8,128)(2,1)}, bf16[1,264,128]{2,1,0:T(8,128)(2,1)}, u32[]{:S(2)}, u32[]{:S(2)}) collective-permute-start(bf16[1,264,128]{2,1,0:T(8,128)(2,1)} %slice.162), channel_id=1, source_target_pairs={{0,8},{8,16},{16,24},{24,0},{1,9},{9,17},{17,25},{25,1},{2,10},{10... | collective-permute-start | bytes 202760 | tf_op jit(solution)/shard_map/ppermute | solution.py:68
  65.0 6.1 %copy-start.1 = (bf16[1,264,256]{2,1,0:T(8,128)(2,1)}, bf16[1,264,256]{2,1,0:T(8,128)(2,1)S(1)}, u32[]{:S(2)}) copy-start(bf16[1,264,256]{2,1,0:T(8,128)(2,1)S(1)} %collective-permute-done.5) | copy-start | bytes 405508
  65.7 7.7 %collective-permute-start.7 = (bf16[1,264,128]{2,1,0:T(8,128)(2,1)}, bf16[1,264,128]{2,1,0:T(8,128)(2,1)}, u32[]{:S(2)}, u32[]{:S(2)}) collective-permute-start(bf16[1,264,128]{2,1,0:T(8,128)(2,1)} %slice.163), channel_id=1, source_target_pairs={{0,24},{8,0},{16,8},{24,16},{1,25},{9,1},{17,9},{25,17},{2,26},{10... | collective-permute-start | bytes 202760 | tf_op jit(solution)/shard_map/ppermute | solution.py:69
  74.5 18.1 %collective-permute-start.8 = (bf16[4,264,256]{2,1,0:T(8,128)(2,1)S(1)}, bf16[4,264,256]{2,1,0:T(8,128)(2,1)S(1)}, u32[]{:S(2)}, u32[]{:S(2)}) collective-permute-start(bf16[4,264,256]{2,1,0:T(8,128)(2,1)S(1)} %maximum_maximum_fusion), channel_id=1, source_target_pairs={{0,2},{2,4},{4,6},{6,0},{1,3},{3,5},{5,7},{7,1},{8,10},{10,12},{12... | collective-permute-start | bytes 1622024 | tf_op jit(solution)/shard_map/ppermute | solution.py:66
  77.8 10.1 %collective-permute-start.9 = (bf16[4,264,256]{2,1,0:T(8,128)(2,1)S(1)}, bf16[4,264,256]{2,1,0:T(8,128)(2,1)S(1)}, u32[]{:S(2)}, u32[]{:S(2)}) collective-permute-start(bf16[4,264,256]{2,1,0:T(8,128)(2,1)S(1)} %maximum_maximum_fusion), channel_id=1, source_target_pairs={{0,6},{2,0},{4,2},{6,4},{1,7},{3,1},{5,3},{7,5},{8,14},{10,8},{12,... | collective-permute-start | bytes 1622024 | tf_op jit(solution)/shard_map/ppermute | solution.py:67
  85.6 32.8 %copy-start.7 = (s32[16,1]{0,1:T(1,128)S(1)}, s32[16,1]{0,1:T(1,128)}, u32[]{:S(2)}) copy-start(s32[16,1]{0,1:T(1,128)} %concatenate.72) | copy-start | bytes 196
  85.6 32.8 %copy-start.8 = (s32[16,1]{0,1:T(1,128)S(1)}, s32[16,1]{0,1:T(1,128)}, u32[]{:S(2)}) copy-start(s32[16,1]{0,1:T(1,128)} %concatenate.71) | copy-start | bytes 196
  88.0 10.9 %collective-permute-start.11 = (bf16[4,264,128]{2,1,0:T(8,128)(2,1)S(1)}, bf16[4,264,128]{2,1,0:T(8,128)(2,1)S(1)}, u32[]{:S(2)}, u32[]{:S(2)}) collective-permute-start(bf16[4,264,128]{2,1,0:T(8,128)(2,1)S(1)} %slice.165), channel_id=1, source_target_pairs={{0,6},{2,0},{4,2},{6,4},{1,7},{3,1},{5,3},{7,5},{8,14},{10,8},{12,... | collective-permute-start | bytes 811016 | tf_op jit(solution)/shard_map/ppermute | solution.py:69
  92.6 8.4 %collective-permute-start.10 = (bf16[4,264,128]{2,1,0:T(8,128)(2,1)S(1)}, bf16[4,264,128]{2,1,0:T(8,128)(2,1)S(1)}, u32[]{:S(2)}, u32[]{:S(2)}) collective-permute-start(bf16[4,264,128]{2,1,0:T(8,128)(2,1)S(1)} %slice.164), channel_id=1, source_target_pairs={{0,2},{2,4},{4,6},{6,0},{1,3},{3,5},{5,7},{7,1},{8,10},{10,12},{12... | collective-permute-start | bytes 811016 | tf_op jit(solution)/shard_map/ppermute | solution.py:68
  101.9 28.8 %collective-permute-start.12 = (bf16[16,264,256]{2,1,0:T(8,128)(2,1)}, bf16[16,264,256]{2,1,0:T(8,128)(2,1)}, u32[]{:S(2)}, u32[]{:S(2)}) collective-permute-start(bf16[16,264,256]{2,1,0:T(8,128)(2,1)} %maximum_dynamic-update-slice_fusion), channel_id=1, source_target_pairs={{0,1},{1,0},{2,3},{3,2},{4,5},{5,4},{6,7},{7,6},{8,9},{9,8},{10,11... | collective-permute-start | bytes 6488072 | tf_op jit(solution)/shard_map/ppermute | solution.py:148
  118.5 2.5 %copy-start.10 = (s32[64]{0:T(128)S(1)}, s32[64]{0:T(128)}, u32[]{:S(2)}) copy-start(s32[64]{0:T(128)} %param.15) | copy-start | bytes 772
  118.5 5.9 %copy-start.5 = (s32[16]{0:T(128)S(1)}, s32[16]{0:T(128)}, u32[]{:S(2)}) copy-start(s32[16]{0:T(128)} %add.302) | copy-start | bytes 196
  118.5 5.9 %copy-start.6 = (s32[16]{0:T(128)S(1)}, s32[16]{0:T(128)}, u32[]{:S(2)}) copy-start(s32[16]{0:T(128)} %add.299) | copy-start | bytes 196
  118.6 6.1 %copy-start.3 = (s32[256,2]{0,1:T(2,128)S(1)}, s32[256,2]{0,1:T(2,128)}, u32[]{:S(2)}) copy-start(s32[256,2]{0,1:T(2,128)} %param.14) | copy-start | bytes 6148
  118.6 6.1 %copy-start.4 = (s32[256,2]{0,1:T(2,128)S(1)}, s32[256,2]{0,1:T(2,128)}, u32[]{:S(2)}) copy-start(s32[256,2]{0,1:T(2,128)} %copy.98) | copy-start | bytes 6148
  134.9 15.7 %all-to-all-start = ((bf16[32,32,192]{2,1,0:T(8,128)(2,1)}), bf16[32,32,192]{2,1,0:T(8,128)(2,1)S(1)}, u32[]{:S(2)}, u32[]{:S(2)}) async-start(bf16[32,32,192]{2,1,0:T(8,128)(2,1)} %bitcast.17), calls=%async_computation | async-start | bytes 1048576 | tf_op jit(solution)/shard_map/all_to_all | solution.py:194

commit v4 on v3

--- a/solution.py
+++ b/solution.py
@@ -13,7 +13,6 @@
 PARTS = 3
 RING = 4
 EP = ("x", "y", "core")
-OFFSETS = (0, -1, 1, 2)
 
 
 def local_step(carried_in, pieces):
@@ -60,15 +59,14 @@
 
 
 def ring_gathered(blocks, axis):
-    forward = [(i, (i + 1) % RING) for i in range(RING)]
-    backward = [(i, (i - 1) % RING) for i in range(RING)]
+    def shifted(value, steps):
+        return lax.ppermute(value, axis, [(i, (i + steps) % RING) for i in range(RING)])
+
     half = blocks.shape[-1] // 2
-    from_left = lax.ppermute(blocks, axis, forward)
-    from_right = lax.ppermute(blocks, axis, backward)
-    far_left = lax.ppermute(from_left[..., :half], axis, forward)
-    far_right = lax.ppermute(from_right[..., half:], axis, backward)
-    far = jnp.concatenate([far_left, far_right], axis=-1)
-    return jnp.concatenate([blocks, from_left, from_right, far], axis=0)
+    from_right = shifted(blocks, -1)
+    from_left = shifted(blocks, 1)
+    far = jnp.concatenate([shifted(blocks[..., :half], 2), shifted(blocks[..., half:], -2)], axis=-1)
+    return jnp.concatenate([blocks, from_right, far, from_left], axis=0)
 
 
 def split_parts(values, width):
@@ -147,14 +145,16 @@
     near = ring_gathered(ring_gathered(block[None], "x"), "y")
     far = lax.ppermute(near, "core", [(0, 1), (1, 0)])
 
-    offsets = jnp.asarray(OFFSETS, jnp.int32)
+    offsets = jnp.arange(RING, dtype=jnp.int32)
     origin_x = (lax.axis_index("x") + offsets) % RING
     origin_y = (lax.axis_index("y") + offsets) % RING
     near_origin = ((origin_x[None, :] * RING + origin_y[:, None]) * 2).reshape(-1)
     core_index = lax.axis_index("core")
     origin = jnp.concatenate([near_origin + core_index, near_origin + (1 - core_index)])
     slots = origin.shape[0]
-    weight_slots = jnp.take(out_weight.reshape(model_cols, slots, local_width), origin, axis=1)
+    weight_slots = jnp.take(
+        out_weight.reshape(model_cols, slots, local_width), origin, axis=1, mode="clip"
+    )
     half = near.shape[0]
     projected = lax.dot_general(
         near,
@@ -197,8 +197,7 @@
     token_flag = jnp.any(
         local_flags[None, :] == jnp.arange(block_rows, dtype=jnp.int32)[:, None], axis=1
     )
-    source = jnp.arange(block_rows * TOP, dtype=jnp.int32) // TOP
-    owned = (flat_ids // EXP_DEV == ep_index) & token_flag[source]
+    owned = ((expert_ids // EXP_DEV == ep_index) & token_flag[:, None]).reshape(-1)
     slot_ids = (flat_ids % EXP_DEV) * capacity + slot_index
     slot_flag = jnp.any(
         owned[None, :]

time: 156 us -> 141 us (0.904)
  local copies, waits for them, and re-layouts: 27.3 us -> 17.4 us
  other arithmetic: 10.5 us -> 6.52 us
  starting transfers between devices: 83.6 us -> 81.3 us
    ppermute x1, starting transfers between devices: 16.5 us -> 12.9 us  [local(): far = lax.ppermute(near, 'core', [(0, 1), (1, 0)])]
    unnamed x30 -> x17, local copies, waits for them, and re-layouts: 7.82 us -> 4.3 us
    gather x2 -> x1, local copies, waits for them, and re-layouts: 5.77 us -> 2.42 us  [local(): jnp.take(out_weight.reshape(model_cols, slots, local_width), origin, axis...]
    ppermute x8, waiting for transfers between devices: 5.61 us -> 8 us  [shifted(): lax.ppermute(value, axis, [(i, (i + steps) % RING) for i in range(RING)])]
    select_n x3 -> x1, other arithmetic: 2.34 us -> 0.01 us  [local(): origin_y = (lax.axis_index('y') + offsets) % RING]
    concatenate x2, other arithmetic: 1.95 us -> 0.13 us  [the longest x1 0.08 us: local(): jnp.concatenate([near_origin + core_index, near_origin + (1 - core_index)])]
  transfers between devices with their start and end apart: 14 -> 14, of which waited for: 7 -> 7; matrix products, arithmetic and copies ran while one was open for 22% -> 16% of each run, Pallas kernels for 0% -> 0%
where the time goes in v4:
time: 141 us; the launch traced here: 138 us
  starting transfers between devices  81.3 us (58%)
  waiting for transfers between devices  21.4 us (15%)
  local copies, waits for them, and re-layouts  17.4 us (12%)
  matrix products  10.6 us (8%)
  other arithmetic  6.52 us (5%)
    ppermute x4, starting transfers between devices, passed_along(): lax.ppermute(value, axis, [(source, source + steps) for source in range(c...  37.2 us
    ppermute x8, starting transfers between devices, shifted(): lax.ppermute(value, axis, [(i, (i + steps) % RING) for i in range(RING)])  26.4 us
    ppermute x1, starting transfers between devices, local(): far = lax.ppermute(near, 'core', [(0, 1), (1, 0)])  12.9 us
    all_to_all x1, waiting for transfers between devices, local(): lax.all_to_all(tile_rows, EP, split_axis=0, concat_axis=2, tiled=True)  9.21 us
    ppermute x8, waiting for transfers between devices, shifted(): lax.ppermute(value, axis, [(i, (i + steps) % RING) for i in range(RING)])  8 us
    all_to_all x1, starting transfers between devices, local(): lax.all_to_all(tile_rows, EP, split_axis=0, concat_axis=2, tiled=True)  4.64 us
    unnamed x17, local copies, waits for them, and re-layouts  4.3 us
    ppermute x4, waiting for transfers between devices, passed_along(): lax.ppermute(value, axis, [(source, source + steps) for source in range(c...  4.24 us
  transfers between devices with their start and end apart: 14, of which 7 were waited for; matrix products, arithmetic and copies ran while one was open for 16% of the time, Pallas kernels for 0%

profile of v4, /device:TPU:1, one launch (start us, length us, event | category | flops | bytes accessed | tf_op | source)
XLA Modules:
  0.0 138.4 jit_solution(14979779389082017876)
XLA Ops:
  0.0 0.7 reshape.306
  0.7 0.6 reduce-window.16
  1.3 0.2 slice_reduce_fusion.1
  1.5 0.2 reduce-window.19
  1.8 0.2 slice_reduce_fusion.2
  2.0 1.0 copy.119
  3.1 1.1 convolution_add_fusion
  4.2 4.4 %collective-permute-start = (f32[2,136,128]{2,1,0:T(8,128)S(1)}, f32[2,136,128]{2,1,0:T(8,128)S(1)}, u32[]{:S(2)}, u32[]{:S(2)}) collective-permute-start(f32[2,136,128]{2,1,0:T(8,128)S(1)} %pad_maximum_fusion.1), channel_id=1, source_target_pairs={{0,32},{32,64},{64,96},{96,128},{128,160},{160,192},{192,224},{224... | collective-permute-start | bytes 417800 | tf_op jit(solution)/shard_map/ppermute | solution.py:51
  8.6 0.8 copy.101
  9.5 0.1 eq.114
  9.6 1.3 fusion.15
  11.1 5.4 %collective-permute-start.1 = (f32[2,136,128]{2,1,0:T(8,128)S(1)}, f32[2,136,128]{2,1,0:T(8,128)S(1)}, u32[]{:S(2)}, u32[]{:S(2)}) collective-permute-start(f32[2,136,128]{2,1,0:T(8,128)S(1)} %pad_maximum_fusion.2), channel_id=1, source_target_pairs={{0,64},{32,96},{64,128},{96,160},{128,192},{160,224},{192,256},{22... | collective-permute-start | bytes 417800 | tf_op jit(solution)/shard_map/ppermute | solution.py:51
  16.6 0.5 fusion.14
  17.2 1.4 collective-permute-done.1
  18.8 14.8 %collective-permute-start.2 = (f32[2,136,128]{2,1,0:T(8,128)S(1)}, f32[2,136,128]{2,1,0:T(8,128)S(1)}, u32[]{:S(2)}, u32[]{:S(2)}) collective-permute-start(f32[2,136,128]{2,1,0:T(8,128)S(1)} %pad_maximum_fusion.3), channel_id=1, source_target_pairs={{0,128},{32,160},{64,192},{96,224},{128,256},{160,288},{192,320},{... | collective-permute-start | bytes 417800 | tf_op jit(solution)/shard_map/ppermute | solution.py:51
  33.6 1.2 reduce-window.14
  34.9 1.1 collective-permute-done.2
  36.1 12.6 %collective-permute-start.3 = (f32[2,136,128]{2,1,0:T(8,128)S(1)}, f32[2,136,128]{2,1,0:T(8,128)S(1)}, u32[]{:S(2)}, u32[]{:S(2)}) collective-permute-start(f32[2,136,128]{2,1,0:T(8,128)S(1)} %pad_maximum_fusion.4), channel_id=1, source_target_pairs={{0,256},{32,288},{64,320},{96,352},{128,384},{160,416},{192,448},{... | collective-permute-start | bytes 417800 | tf_op jit(solution)/shard_map/ppermute | solution.py:51
  48.7 0.1 fusion.91
  48.8 0.1 fusion.92
  48.9 1.8 %collective-permute-done.3 = f32[2,136,128]{2,1,0:T(8,128)S(1)} collective-permute-done((f32[2,136,128]{2,1,0:T(8,128)S(1)}, f32[2,136,128]{2,1,0:T(8,128)S(1)}, u32[]{:S(2)}, u32[]{:S(2)}) %collective-permute-start.3) | collective-permute-done | bytes 139296 | tf_op jit(solution)/shard_map/ppermute | solution.py:51
  50.7 0.5 multiply_reduce_fusion
  51.4 4.4 %collective-permute-start.4 = (bf16[1,264,256]{2,1,0:T(8,128)(2,1)S(1)}, bf16[1,264,256]{2,1,0:T(8,128)(2,1)S(1)}, u32[]{:S(2)}, u32[]{:S(2)}) collective-permute-start(bf16[1,264,256]{2,1,0:T(8,128)(2,1)S(1)} %maximum_bitcast_fusion), channel_id=1, source_target_pairs={{0,24},{8,0},{16,8},{24,16},{1,25},{9,1},{17,9},{25,17},{2,26},{10... | collective-permute-start | bytes 405512 | tf_op jit(solution)/shard_map/ppermute | solution.py:63
  55.8 1.9 %collective-permute-start.7 = (bf16[1,264,256]{2,1,0:T(8,128)(2,1)S(1)}, bf16[1,264,256]{2,1,0:T(8,128)(2,1)S(1)}, u32[]{:S(2)}, u32[]{:S(2)}) collective-permute-start(bf16[1,264,256]{2,1,0:T(8,128)(2,1)S(1)} %maximum_bitcast_fusion), channel_id=1, source_target_pairs={{0,8},{8,16},{16,24},{24,0},{1,9},{9,17},{17,25},{25,1},{2,10},{10... | collective-permute-start | bytes 405512 | tf_op jit(solution)/shard_map/ppermute | solution.py:63
  57.8 3.6 %collective-permute-start.5 = (bf16[1,264,128]{2,1,0:T(8,128)(2,1)S(1)}, bf16[1,264,128]{2,1,0:T(8,128)(2,1)S(1)}, u32[]{:S(2)}, u32[]{:S(2)}) collective-permute-start(bf16[1,264,128]{2,1,0:T(8,128)(2,1)S(1)} %get-tuple-element.43), channel_id=1, source_target_pairs={{0,16},{8,24},{16,0},{24,8},{1,17},{9,25},{17,1},{25,9},{2,18},{10... | collective-permute-start | bytes 202760 | tf_op jit(solution)/shard_map/ppermute | solution.py:63
  61.4 3.1 %collective-permute-start.6 = (bf16[1,264,128]{2,1,0:T(8,128)(2,1)S(1)}, bf16[1,264,128]{2,1,0:T(8,128)(2,1)S(1)}, u32[]{:S(2)}, u32[]{:S(2)}) collective-permute-start(bf16[1,264,128]{2,1,0:T(8,128)(2,1)S(1)} %get-tuple-element.42), channel_id=1, source_target_pairs={{0,16},{8,24},{16,0},{24,8},{1,17},{9,25},{17,1},{25,9},{2,18},{10... | collective-permute-start | bytes 202760 | tf_op jit(solution)/shard_map/ppermute | solution.py:63
  64.6 0.6 constant_dynamic-update-slice_fusion.6
  65.2 2.7 %collective-permute-done.6 = bf16[1,264,128]{2,1,0:T(8,128)(2,1)S(1)} collective-permute-done((bf16[1,264,128]{2,1,0:T(8,128)(2,1)S(1)}, bf16[1,264,128]{2,1,0:T(8,128)(2,1)S(1)}, u32[]{:S(2)}, u32[]{:S(2)}) %collective-permute-start.6) | collective-permute-done | bytes 67616 | tf_op jit(solution)/shard_map/ppermute | solution.py:63
  68.0 4.6 %collective-permute-start.8 = (bf16[4,264,256]{2,1,0:T(8,128)(2,1)S(1)}, bf16[4,264,256]{2,1,0:T(8,128)(2,1)S(1)}, u32[]{:S(2)}, u32[]{:S(2)}) collective-permute-start(bf16[4,264,256]{2,1,0:T(8,128)(2,1)S(1)} %pad_maximum_fusion), channel_id=1, source_target_pairs={{0,6},{2,0},{4,2},{6,4},{1,7},{3,1},{5,3},{7,5},{8,14},{10,8},{12,... | collective-permute-start | bytes 1622024 | tf_op jit(solution)/shard_map/ppermute | solution.py:63
  72.8 1.9 %collective-permute-start.11 = (bf16[4,264,256]{2,1,0:T(8,128)(2,1)S(1)}, bf16[4,264,256]{2,1,0:T(8,128)(2,1)S(1)}, u32[]{:S(2)}, u32[]{:S(2)}) collective-permute-start(bf16[4,264,256]{2,1,0:T(8,128)(2,1)S(1)} %pad_maximum_fusion), channel_id=1, source_target_pairs={{0,2},{2,4},{4,6},{6,0},{1,3},{3,5},{5,7},{7,1},{8,10},{10,12},{12... | collective-permute-start | bytes 1622024 | tf_op jit(solution)/shard_map/ppermute | solution.py:63
  74.7 3.5 %collective-permute-start.10 = (bf16[4,264,128]{2,1,0:T(8,128)(2,1)S(1)}, bf16[4,264,128]{2,1,0:T(8,128)(2,1)S(1)}, u32[]{:S(2)}, u32[]{:S(2)}) collective-permute-start(bf16[4,264,128]{2,1,0:T(8,128)(2,1)S(1)} %get-tuple-element.26), channel_id=1, source_target_pairs={{0,4},{2,6},{4,0},{6,2},{1,5},{3,7},{5,1},{7,3},{8,12},{10,14},{12... | collective-permute-start | bytes 811016 | tf_op jit(solution)/shard_map/ppermute | solution.py:63
  78.2 3.2 %collective-permute-start.9 = (bf16[4,264,128]{2,1,0:T(8,128)(2,1)S(1)}, bf16[4,264,128]{2,1,0:T(8,128)(2,1)S(1)}, u32[]{:S(2)}, u32[]{:S(2)}) collective-permute-start(bf16[4,264,128]{2,1,0:T(8,128)(2,1)S(1)} %get-tuple-element.25), channel_id=1, source_target_pairs={{0,4},{2,6},{4,0},{6,2},{1,5},{3,7},{5,1},{7,3},{8,12},{10,14},{12... | collective-permute-start | bytes 811016 | tf_op jit(solution)/shard_map/ppermute | solution.py:63
  81.5 0.7 constant_dynamic-update-slice_fusion.5
  82.2 0.6 constant_dynamic-update-slice_fusion.4
  82.8 0.7 constant_dynamic-update-slice_fusion.3
  83.5 0.7 constant_dynamic-update-slice_fusion.2
  84.1 0.8 constant_dynamic-update-slice_fusion.1
  85.0 1.1 collective-permute-done.10
  86.1 4.2 %collective-permute-done.9 = bf16[4,264,128]{2,1,0:T(8,128)(2,1)S(1)} collective-permute-done((bf16[4,264,128]{2,1,0:T(8,128)(2,1)S(1)}, bf16[4,264,128]{2,1,0:T(8,128)(2,1)S(1)}, u32[]{:S(2)}, u32[]{:S(2)}) %collective-permute-start.9) | collective-permute-done | bytes 270368 | tf_op jit(solution)/shard_map/ppermute | solution.py:63
  90.2 0.9 maximum_dynamic-update-slice_fusion
  91.1 0.8 constant_dynamic-update-slice_fusion
  92.0 12.9 %collective-permute-start.12 = (bf16[16,264,256]{2,1,0:T(8,128)(2,1)}, bf16[16,264,256]{2,1,0:T(8,128)(2,1)}, u32[]{:S(2)}, u32[]{:S(2)}) collective-permute-start(bf16[16,264,256]{2,1,0:T(8,128)(2,1)} %constant_dynamic-update-slice_fusion), channel_id=1, source_target_pairs={{0,1},{1,0},{2,3},{3,2},{4,5},{5,4},{6,7},{7,6},{8,9},{9,8},{10,11... | collective-permute-start | bytes 6488072 | tf_op jit(solution)/shard_map/ppermute | solution.py:146
  104.9 0.2 slice_reduce_fusion
  105.1 0.1 eq.110
  105.4 0.1 reduce_sum.30
  105.6 2.3 %copy.161 = bf16[24,32,8,256]{3,2,0,1:T(8,128)(2,1)S(1)} copy(bf16[24,32,8,256]{3,2,1,0:T(8,128)(2,1)} %bitcast.132) | data formatting | bytes 6291456 | tf_op jit(solution)/shard_map/reshape | solution.py:156
  108.4 0.2 copy.100
  108.5 0.2 and.54
  108.8 2.4 %gather_fusion = bf16[32,192,256]{2,1,0:T(8,128)(2,1)} fusion(bf16[192,32,256]{2,0,1:T(8,128)(2,1)S(1)} %bitcast.131, s32[1024]{0:T(1024)S(1)} %pad_clamp_fusion), kind=kCustom, calls=%fused_computation | custom fusion | bytes 6291584 | tf_op jit(solution)/shard_map/jit(_take)/gather | solution.py:155
  111.2 0.1 fusion.69
  111.3 0.9 slice.168
  112.2 3.4 %fusion.6 = f32[264,192]{0,1:T(8,128)S(1)} fusion(bf16[16,264,256]{2,1,0:T(8,128)(2,1)} %constant_dynamic-update-slice_fusion, bf16[192,32,256]{2,0,1:T(8,128)(2,1)} %bitcast.133), kind=kOutput, calls=%fused_computation.10 | convolution fusion | flops 415236096 | bytes 3938304 | tf_op jit(solution)/shard_map/dot_general | solution.py:159
  115.6 2.8 %fusion.9 = f32[264,192]{0,1:T(8,128)S(1)} fusion(bf16[16,264,256]{2,1,0:T(8,128)(2,1)} %collective-permute-done.12, bf16[192,32,256]{2,0,1:T(8,128)(2,1)S(1)} %bitcast.134), kind=kOutput, calls=%fused_computation.11 | convolution fusion | flops 415236096 | bytes 3938304 | tf_op jit(solution)/shard_map/dot_general | solution.py:164
  118.4 0.4 convolution_convert_fusion
  118.8 1.0 copy.114
  119.8 4.6 %all-to-all-start = ((bf16[32,32,192]{2,1,0:T(8,128)(2,1)}), bf16[32,32,192]{2,1,0:T(8,128)(2,1)S(1)}, u32[]{:S(2)}, u32[]{:S(2)}) async-start(bf16[32,32,192]{2,1,0:T(8,128)(2,1)} %bitcast.15), calls=%async_computation | async-start | bytes 1048576 | tf_op jit(solution)/shard_map/all_to_all | solution.py:194
  124.5 0.9 slice.169
  125.4 0.1 fusion.18
  125.5 0.6 multiply_reduce_fusion.1
  126.8 9.2 %all-to-all-done = bf16[32,32,192]{2,1,0:T(8,128)(2,1)S(1)} async-done(((bf16[32,32,192]{2,1,0:T(8,128)(2,1)}), bf16[32,32,192]{2,1,0:T(8,128)(2,1)S(1)}, u32[]{:S(2)}, u32[]{:S(2)}) %all-to-all-start) | async-done | bytes 393248 | tf_op jit(solution)/shard_map/all_to_all | solution.py:194
  136.0 0.3 copy.115
  136.3 0.5 all_to_all.16
  136.9 0.5 fusion.19
  137.4 1.0 fusion.22
  (65 shorter events, 2.1 us)
Async XLA Ops:
  0.0 9.6 %copy-start = (bf16[256,256]{1,0:T(8,128)(2,1)S(1)}, bf16[256,256]{1,0:T(8,128)(2,1)}, u32[]{:S(2)}) copy-start(bf16[256,256]{1,0:T(8,128)(2,1)} %param.8) | copy-start | bytes 393220
  0.0 10.9 %copy-start.3 = (f32[192]{0:T(256)S(1)}, f32[192]{0:T(256)}, u32[]{:S(2)}) copy-start(f32[192]{0:T(256)} %param.15) | copy-start | bytes 2308
  4.2 6.7 %collective-permute-start = (f32[2,136,128]{2,1,0:T(8,128)S(1)}, f32[2,136,128]{2,1,0:T(8,128)S(1)}, u32[]{:S(2)}, u32[]{:S(2)}) collective-permute-start(f32[2,136,128]{2,1,0:T(8,128)S(1)} %pad_maximum_fusion.1), channel_id=1, source_target_pairs={{0,32},{32,64},{64,96},{96,128},{128,160},{160,192},{192,224},{224... | collective-permute-start | bytes 417800 | tf_op jit(solution)/shard_map/ppermute | solution.py:51
  11.1 7.5 %collective-permute-start.1 = (f32[2,136,128]{2,1,0:T(8,128)S(1)}, f32[2,136,128]{2,1,0:T(8,128)S(1)}, u32[]{:S(2)}, u32[]{:S(2)}) collective-permute-start(f32[2,136,128]{2,1,0:T(8,128)S(1)} %pad_maximum_fusion.2), channel_id=1, source_target_pairs={{0,64},{32,96},{64,128},{96,160},{128,192},{160,224},{192,256},{22... | collective-permute-start | bytes 417800 | tf_op jit(solution)/shard_map/ppermute | solution.py:51
  18.8 17.2 %collective-permute-start.2 = (f32[2,136,128]{2,1,0:T(8,128)S(1)}, f32[2,136,128]{2,1,0:T(8,128)S(1)}, u32[]{:S(2)}, u32[]{:S(2)}) collective-permute-start(f32[2,136,128]{2,1,0:T(8,128)S(1)} %pad_maximum_fusion.3), channel_id=1, source_target_pairs={{0,128},{32,160},{64,192},{96,224},{128,256},{160,288},{192,320},{... | collective-permute-start | bytes 417800 | tf_op jit(solution)/shard_map/ppermute | solution.py:51
  36.1 14.6 %collective-permute-start.3 = (f32[2,136,128]{2,1,0:T(8,128)S(1)}, f32[2,136,128]{2,1,0:T(8,128)S(1)}, u32[]{:S(2)}, u32[]{:S(2)}) collective-permute-start(f32[2,136,128]{2,1,0:T(8,128)S(1)} %pad_maximum_fusion.4), channel_id=1, source_target_pairs={{0,256},{32,288},{64,320},{96,352},{128,384},{160,416},{192,448},{... | collective-permute-start | bytes 417800 | tf_op jit(solution)/shard_map/ppermute | solution.py:51
  51.4 16.5 %collective-permute-start.4 = (bf16[1,264,256]{2,1,0:T(8,128)(2,1)S(1)}, bf16[1,264,256]{2,1,0:T(8,128)(2,1)S(1)}, u32[]{:S(2)}, u32[]{:S(2)}) collective-permute-start(bf16[1,264,256]{2,1,0:T(8,128)(2,1)S(1)} %maximum_bitcast_fusion), channel_id=1, source_target_pairs={{0,24},{8,0},{16,8},{24,16},{1,25},{9,1},{17,9},{25,17},{2,26},{10... | collective-permute-start | bytes 405512 | tf_op jit(solution)/shard_map/ppermute | solution.py:63
  55.8 12.1 %collective-permute-start.7 = (bf16[1,264,256]{2,1,0:T(8,128)(2,1)S(1)}, bf16[1,264,256]{2,1,0:T(8,128)(2,1)S(1)}, u32[]{:S(2)}, u32[]{:S(2)}) collective-permute-start(bf16[1,264,256]{2,1,0:T(8,128)(2,1)S(1)} %maximum_bitcast_fusion), channel_id=1, source_target_pairs={{0,8},{8,16},{16,24},{24,0},{1,9},{9,17},{17,25},{25,1},{2,10},{10... | collective-permute-start | bytes 405512 | tf_op jit(solution)/shard_map/ppermute | solution.py:63
  57.8 7.5 %collective-permute-start.5 = (bf16[1,264,128]{2,1,0:T(8,128)(2,1)S(1)}, bf16[1,264,128]{2,1,0:T(8,128)(2,1)S(1)}, u32[]{:S(2)}, u32[]{:S(2)}) collective-permute-start(bf16[1,264,128]{2,1,0:T(8,128)(2,1)S(1)} %get-tuple-element.43), channel_id=1, source_target_pairs={{0,16},{8,24},{16,0},{24,8},{1,17},{9,25},{17,1},{25,9},{2,18},{10... | collective-permute-start | bytes 202760 | tf_op jit(solution)/shard_map/ppermute | solution.py:63
  61.4 6.5 %collective-permute-start.6 = (bf16[1,264,128]{2,1,0:T(8,128)(2,1)S(1)}, bf16[1,264,128]{2,1,0:T(8,128)(2,1)S(1)}, u32[]{:S(2)}, u32[]{:S(2)}) collective-permute-start(bf16[1,264,128]{2,1,0:T(8,128)(2,1)S(1)} %get-tuple-element.42), channel_id=1, source_target_pairs={{0,16},{8,24},{16,0},{24,8},{1,17},{9,25},{17,1},{25,9},{2,18},{10... | collective-permute-start | bytes 202760 | tf_op jit(solution)/shard_map/ppermute | solution.py:63
  68.0 16.1 %collective-permute-start.8 = (bf16[4,264,256]{2,1,0:T(8,128)(2,1)S(1)}, bf16[4,264,256]{2,1,0:T(8,128)(2,1)S(1)}, u32[]{:S(2)}, u32[]{:S(2)}) collective-permute-start(bf16[4,264,256]{2,1,0:T(8,128)(2,1)S(1)} %pad_maximum_fusion), channel_id=1, source_target_pairs={{0,6},{2,0},{4,2},{6,4},{1,7},{3,1},{5,3},{7,5},{8,14},{10,8},{12,... | collective-permute-start | bytes 1622024 | tf_op jit(solution)/shard_map/ppermute | solution.py:63
  72.8 18.3 %collective-permute-start.11 = (bf16[4,264,256]{2,1,0:T(8,128)(2,1)S(1)}, bf16[4,264,256]{2,1,0:T(8,128)(2,1)S(1)}, u32[]{:S(2)}, u32[]{:S(2)}) collective-permute-start(bf16[4,264,256]{2,1,0:T(8,128)(2,1)S(1)} %pad_maximum_fusion), channel_id=1, source_target_pairs={{0,2},{2,4},{4,6},{6,0},{1,3},{3,5},{5,7},{7,1},{8,10},{10,12},{12... | collective-permute-start | bytes 1622024 | tf_op jit(solution)/shard_map/ppermute | solution.py:63
  74.7 11.4 %collective-permute-start.10 = (bf16[4,264,128]{2,1,0:T(8,128)(2,1)S(1)}, bf16[4,264,128]{2,1,0:T(8,128)(2,1)S(1)}, u32[]{:S(2)}, u32[]{:S(2)}) collective-permute-start(bf16[4,264,128]{2,1,0:T(8,128)(2,1)S(1)} %get-tuple-element.26), channel_id=1, source_target_pairs={{0,4},{2,6},{4,0},{6,2},{1,5},{3,7},{5,1},{7,3},{8,12},{10,14},{12... | collective-permute-start | bytes 811016 | tf_op jit(solution)/shard_map/ppermute | solution.py:63
  78.2 12.0 %collective-permute-start.9 = (bf16[4,264,128]{2,1,0:T(8,128)(2,1)S(1)}, bf16[4,264,128]{2,1,0:T(8,128)(2,1)S(1)}, u32[]{:S(2)}, u32[]{:S(2)}) collective-permute-start(bf16[4,264,128]{2,1,0:T(8,128)(2,1)S(1)} %get-tuple-element.25), channel_id=1, source_target_pairs={{0,4},{2,6},{4,0},{6,2},{1,5},{3,7},{5,1},{7,3},{8,12},{10,14},{12... | collective-permute-start | bytes 811016 | tf_op jit(solution)/shard_map/ppermute | solution.py:63
  92.0 23.6 %collective-permute-start.12 = (bf16[16,264,256]{2,1,0:T(8,128)(2,1)}, bf16[16,264,256]{2,1,0:T(8,128)(2,1)}, u32[]{:S(2)}, u32[]{:S(2)}) collective-permute-start(bf16[16,264,256]{2,1,0:T(8,128)(2,1)} %constant_dynamic-update-slice_fusion), channel_id=1, source_target_pairs={{0,1},{1,0},{2,3},{3,2},{4,5},{5,4},{6,7},{7,6},{8,9},{9,8},{10,11... | collective-permute-start | bytes 6488072 | tf_op jit(solution)/shard_map/ppermute | solution.py:146
  105.6 2.6 %copy-start.4 = (s32[64]{0:T(128)S(1)}, s32[64]{0:T(128)}, u32[]{:S(2)}) copy-start(s32[64]{0:T(128)} %param.14) | copy-start | bytes 772
  105.6 2.7 %copy-start.2 = (s32[256,2]{0,1:T(2,128)S(1)}, s32[256,2]{0,1:T(2,128)}, u32[]{:S(2)}) copy-start(s32[256,2]{0,1:T(2,128)} %param.13) | copy-start | bytes 6148
  112.2 3.4 %copy-start.1 = (bf16[32,192,256]{2,1,0:T(8,128)(2,1)S(1)}, bf16[32,192,256]{2,1,0:T(8,128)(2,1)}, u32[]{:S(2)}) copy-start(bf16[32,192,256]{2,1,0:T(8,128)(2,1)} %gather_fusion) | copy-start | bytes 9437188
  119.8 16.2 %all-to-all-start = ((bf16[32,32,192]{2,1,0:T(8,128)(2,1)}), bf16[32,32,192]{2,1,0:T(8,128)(2,1)S(1)}, u32[]{:S(2)}, u32[]{:S(2)}) async-start(bf16[32,32,192]{2,1,0:T(8,128)(2,1)} %bitcast.15), calls=%async_computation | async-start | bytes 1048576 | tf_op jit(solution)/shard_map/all_to_all | solution.py:194

commit v5 on v4

--- a/solution.py
+++ b/solution.py
@@ -69,6 +69,51 @@
     return jnp.concatenate([blocks, from_right, far, from_left], axis=0)
 
 
+def received_by(pairs, count, position):
+    table = [False] * count
+    for _, target in pairs:
+        table[target] = True
+    return jnp.asarray(table)[position]
+
+
+def exclusive_scan(value, axis, count):
+    position = lax.axis_index(axis)
+    if count == 1:
+        return jnp.zeros_like(value)
+
+    def step(current, pairs, merge):
+        arrived = lax.ppermute(current, axis, pairs)
+        return arrived, jnp.where(received_by(pairs, count, position), merge(arrived), current)
+
+    segment = value
+    left_raw = None
+    distance = 1
+    while 4 * distance <= count:
+        pairs = [(j - distance, j) for j in range(count) if (j + 1) % (2 * distance) == 0]
+        arrived, segment = step(segment, pairs, lambda got, seg=segment: combined(got, seg))
+        if left_raw is None:
+            left_raw = arrived
+        distance *= 2
+    distance //= 2
+    while distance >= 2:
+        pairs = [
+            (j, j + distance)
+            for j in range(count)
+            if (j + 1) % (2 * distance) == 0 and j + distance < count
+        ]
+        _, segment = step(segment, pairs, lambda got, seg=segment: combined(got, seg))
+        distance //= 2
+    if left_raw is None:
+        left_raw = lax.ppermute(segment, axis, [(j - 1, j) for j in range(1, count, 2)])
+    to_even = [(j, j + 1) for j in range(1, count - 1, 2)]
+    to_odd = [(j, j + 2) for j in range(1, count - 2, 2)]
+    from_odd = lax.ppermute(segment, axis, to_even)
+    from_odd_far = lax.ppermute(segment, axis, to_odd)
+    odd_result = jnp.where(position >= 3, combined(from_odd_far, left_raw), left_raw)
+    result = jnp.where(position % 2 == 1, odd_result, from_odd)
+    return jnp.where(position == 0, jnp.zeros_like(value), result)
+
+
 def split_parts(values, width):
     pieces = []
     rest = values
@@ -122,18 +167,8 @@
         [local_state, jnp.broadcast_to(total_decay[:, None, None], (local_heads, PAD_ROWS, HEAD))],
         axis=1,
     )
-    inclusive = packed
-    exclusive = None
-    distance = 1
-    while distance < ctx_count:
-        arrived = passed_along(inclusive, "ctx", distance)
-        exclusive = arrived if exclusive is None else combined(arrived, exclusive)
-        if 2 * distance < ctx_count:
-            inclusive = combined(arrived, inclusive)
-        distance *= 2
-    incoming = (
-        jnp.zeros_like(local_state) if exclusive is None else exclusive[:, :HEAD, :]
-    )
+    exclusive = exclusive_scan(packed, "ctx", ctx_count)
+    incoming = exclusive[:, :HEAD, :]
 
     scaled = shaped(queries).astype(jnp.float32) * reach_decay[..., None]
     outputs = partial_out + jnp.einsum(

time: 141 us -> 142 us (level)
  the two profiles are of different devices: /device:TPU:1 before, /device:TPU:385 now
where the time goes in v5:
time: 142 us; the launch traced here: 141 us
  starting transfers between devices  51.8 us (36%)
  waiting for transfers between devices  46.7 us (33%)
  local copies, waits for them, and re-layouts  20.6 us (15%)
  matrix products  10.6 us (7%)
  other arithmetic  9.89 us (7%)
    ppermute x1, waiting for transfers between devices, exclusive_scan(): from_odd = lax.ppermute(segment, axis, to_even)  28.9 us
    ppermute x8, starting transfers between devices, shifted(): lax.ppermute(value, axis, [(i, (i + steps) % RING) for i in range(RING)])  26.5 us
    ppermute x1, starting transfers between devices, local(): far = lax.ppermute(near, 'core', [(0, 1), (1, 0)])  13.4 us
    all_to_all x1, waiting for transfers between devices, local(): lax.all_to_all(tile_rows, EP, split_axis=0, concat_axis=2, tiled=True)  9.21 us
    ppermute x8, waiting for transfers between devices, shifted(): lax.ppermute(value, axis, [(i, (i + steps) % RING) for i in range(RING)])  7.5 us
    ppermute x5, starting transfers between devices, step(): arrived = lax.ppermute(current, axis, pairs)  5.33 us
    all_to_all x1, starting transfers between devices, local(): lax.all_to_all(tile_rows, EP, split_axis=0, concat_axis=2, tiled=True)  4.65 us
    unnamed x25, local copies, waits for them, and re-layouts  3.65 us
  transfers between devices with their start and end apart: 17, of which 7 were waited for; matrix products, arithmetic and copies ran while one was open for 18% of the time, Pallas kernels for 0%

profile of v5, /device:TPU:385, one launch (start us, length us, event | category | flops | bytes accessed | tf_op | source)
XLA Modules:
  0.0 140.8 jit_solution(17227484421481504463)
XLA Ops:
  0.0 0.7 reshape.306
  0.8 0.6 reduce-window.16
  1.8 0.2 slice_reduce_fusion.2
  2.1 1.0 copy.124
  3.1 1.1 convolution_add_fusion
  4.3 2.7 %collective-permute-start = (f32[2,136,128]{2,1,0:T(8,128)S(1)}, f32[2,136,128]{2,1,0:T(8,128)S(1)}, u32[]{:S(2)}, u32[]{:S(2)}) collective-permute-start(f32[2,136,128]{2,1,0:T(8,128)S(1)} %pad_maximum_fusion.1), channel_id=1, source_target_pairs={{0,32},{64,96},{128,160},{192,224},{256,288},{320,352},{384,416},{... | collective-permute-start | bytes 417800 | tf_op jit(solution)/shard_map/ppermute | solution.py:85
  6.9 1.2 dynamic_slice.29
  8.2 1.0 collective-permute-done
  9.4 0.7 maximum_select_fusion
  10.1 0.7 collective-permute-start.1
  10.8 1.3 fusion.15
  12.4 0.6 dynamic_slice.28
  13.2 0.7 maximum_select_fusion.1
  13.8 0.7 collective-permute-start.2
  14.5 0.6 dynamic_slice.27
  15.3 0.7 maximum_select_fusion.2
  16.0 0.7 collective-permute-start.3
  16.7 0.6 dynamic_slice.26
  17.5 0.7 maximum_select_fusion.3
  18.2 0.7 collective-permute-start.4
  18.9 0.5 fusion.14
  19.4 0.6 dynamic_slice.25
  20.2 0.7 maximum_select_fusion.4
  20.9 0.7 collective-permute-start.5
  21.6 1.2 reduce-window.14
  22.8 1.3 collective-permute-start.6
  24.2 28.9 %collective-permute-done.6 = f32[2,136,128]{2,1,0:T(8,128)S(1)} collective-permute-done((f32[2,136,128]{2,1,0:T(8,128)S(1)}, f32[2,136,128]{2,1,0:T(8,128)S(1)}, u32[]{:S(2)}, u32[]{:S(2)}) %collective-permute-start.6) | collective-permute-done | bytes 139296 | tf_op jit(solution)/shard_map/ppermute | solution.py:110
  53.2 0.5 multiply_reduce_fusion
  53.9 4.4 %collective-permute-start.7 = (bf16[1,264,256]{2,1,0:T(8,128)(2,1)S(1)}, bf16[1,264,256]{2,1,0:T(8,128)(2,1)S(1)}, u32[]{:S(2)}, u32[]{:S(2)}) collective-permute-start(bf16[1,264,256]{2,1,0:T(8,128)(2,1)S(1)} %maximum_bitcast_fusion), channel_id=1, source_target_pairs={{0,24},{8,0},{16,8},{24,16},{1,25},{9,1},{17,9},{25,17},{2,26},{10... | collective-permute-start | bytes 405512 | tf_op jit(solution)/shard_map/ppermute | solution.py:63
  58.3 1.9 %collective-permute-start.10 = (bf16[1,264,256]{2,1,0:T(8,128)(2,1)S(1)}, bf16[1,264,256]{2,1,0:T(8,128)(2,1)S(1)}, u32[]{:S(2)}, u32[]{:S(2)}) collective-permute-start(bf16[1,264,256]{2,1,0:T(8,128)(2,1)S(1)} %maximum_bitcast_fusion), channel_id=1, source_target_pairs={{0,8},{8,16},{16,24},{24,0},{1,9},{9,17},{17,25},{25,1},{2,10},{10... | collective-permute-start | bytes 405512 | tf_op jit(solution)/shard_map/ppermute | solution.py:63
  60.2 3.6 %collective-permute-start.8 = (bf16[1,264,128]{2,1,0:T(8,128)(2,1)S(1)}, bf16[1,264,128]{2,1,0:T(8,128)(2,1)S(1)}, u32[]{:S(2)}, u32[]{:S(2)}) collective-permute-start(bf16[1,264,128]{2,1,0:T(8,128)(2,1)S(1)} %get-tuple-element.26), channel_id=1, source_target_pairs={{0,16},{8,24},{16,0},{24,8},{1,17},{9,25},{17,1},{25,9},{2,18},{10... | collective-permute-start | bytes 202760 | tf_op jit(solution)/shard_map/ppermute | solution.py:63
  63.9 3.2 %collective-permute-start.9 = (bf16[1,264,128]{2,1,0:T(8,128)(2,1)S(1)}, bf16[1,264,128]{2,1,0:T(8,128)(2,1)S(1)}, u32[]{:S(2)}, u32[]{:S(2)}) collective-permute-start(bf16[1,264,128]{2,1,0:T(8,128)(2,1)S(1)} %get-tuple-element.25), channel_id=1, source_target_pairs={{0,16},{8,24},{16,0},{24,8},{1,17},{9,25},{17,1},{25,9},{2,18},{10... | collective-permute-start | bytes 202760 | tf_op jit(solution)/shard_map/ppermute | solution.py:63
  67.0 0.6 constant_dynamic-update-slice_fusion.6
  67.7 2.7 %collective-permute-done.9 = bf16[1,264,128]{2,1,0:T(8,128)(2,1)S(1)} collective-permute-done((bf16[1,264,128]{2,1,0:T(8,128)(2,1)S(1)}, bf16[1,264,128]{2,1,0:T(8,128)(2,1)S(1)}, u32[]{:S(2)}, u32[]{:S(2)}) %collective-permute-start.9) | collective-permute-done | bytes 67616 | tf_op jit(solution)/shard_map/ppermute | solution.py:63
  70.5 4.6 %collective-permute-start.11 = (bf16[4,264,256]{2,1,0:T(8,128)(2,1)S(1)}, bf16[4,264,256]{2,1,0:T(8,128)(2,1)S(1)}, u32[]{:S(2)}, u32[]{:S(2)}) collective-permute-start(bf16[4,264,256]{2,1,0:T(8,128)(2,1)S(1)} %pad_maximum_fusion), channel_id=1, source_target_pairs={{0,6},{2,0},{4,2},{6,4},{1,7},{3,1},{5,3},{7,5},{8,14},{10,8},{12,... | collective-permute-start | bytes 1622024 | tf_op jit(solution)/shard_map/ppermute | solution.py:63
  75.2 1.9 %collective-permute-start.14 = (bf16[4,264,256]{2,1,0:T(8,128)(2,1)S(1)}, bf16[4,264,256]{2,1,0:T(8,128)(2,1)S(1)}, u32[]{:S(2)}, u32[]{:S(2)}) collective-permute-start(bf16[4,264,256]{2,1,0:T(8,128)(2,1)S(1)} %pad_maximum_fusion), channel_id=1, source_target_pairs={{0,2},{2,4},{4,6},{6,0},{1,3},{3,5},{5,7},{7,1},{8,10},{10,12},{12... | collective-permute-start | bytes 1622024 | tf_op jit(solution)/shard_map/ppermute | solution.py:63
  77.2 3.5 %collective-permute-start.13 = (bf16[4,264,128]{2,1,0:T(8,128)(2,1)S(1)}, bf16[4,264,128]{2,1,0:T(8,128)(2,1)S(1)}, u32[]{:S(2)}, u32[]{:S(2)}) collective-permute-start(bf16[4,264,128]{2,1,0:T(8,128)(2,1)S(1)} %get-tuple-element.24), channel_id=1, source_target_pairs={{0,4},{2,6},{4,0},{6,2},{1,5},{3,7},{5,1},{7,3},{8,12},{10,14},{12... | collective-permute-start | bytes 811016 | tf_op jit(solution)/shard_map/ppermute | solution.py:63
  80.7 3.2 %collective-permute-start.12 = (bf16[4,264,128]{2,1,0:T(8,128)(2,1)S(1)}, bf16[4,264,128]{2,1,0:T(8,128)(2,1)S(1)}, u32[]{:S(2)}, u32[]{:S(2)}) collective-permute-start(bf16[4,264,128]{2,1,0:T(8,128)(2,1)S(1)} %get-tuple-element.23), channel_id=1, source_target_pairs={{0,4},{2,6},{4,0},{6,2},{1,5},{3,7},{5,1},{7,3},{8,12},{10,14},{12... | collective-permute-start | bytes 811016 | tf_op jit(solution)/shard_map/ppermute | solution.py:63
  84.0 0.7 constant_dynamic-update-slice_fusion.5
  84.6 0.6 constant_dynamic-update-slice_fusion.4
  85.3 0.7 constant_dynamic-update-slice_fusion.3
  85.9 0.7 constant_dynamic-update-slice_fusion.2
  86.6 0.8 constant_dynamic-update-slice_fusion.1
  87.4 1.1 collective-permute-done.13
  88.5 3.6 %collective-permute-done.12 = bf16[4,264,128]{2,1,0:T(8,128)(2,1)S(1)} collective-permute-done((bf16[4,264,128]{2,1,0:T(8,128)(2,1)S(1)}, bf16[4,264,128]{2,1,0:T(8,128)(2,1)S(1)}, u32[]{:S(2)}, u32[]{:S(2)}) %collective-permute-start.12) | collective-permute-done | bytes 270368 | tf_op jit(solution)/shard_map/ppermute | solution.py:63
  92.1 0.9 maximum_dynamic-update-slice_fusion
  93.1 0.8 constant_dynamic-update-slice_fusion
  93.9 13.4 %collective-permute-start.15 = (bf16[16,264,256]{2,1,0:T(8,128)(2,1)}, bf16[16,264,256]{2,1,0:T(8,128)(2,1)}, u32[]{:S(2)}, u32[]{:S(2)}) collective-permute-start(bf16[16,264,256]{2,1,0:T(8,128)(2,1)} %constant_dynamic-update-slice_fusion), channel_id=1, source_target_pairs={{0,1},{1,0},{2,3},{3,2},{4,5},{5,4},{6,7},{7,6},{8,9},{9,8},{10,11... | collective-permute-start | bytes 6488072 | tf_op jit(solution)/shard_map/ppermute | solution.py:181
  107.4 0.2 slice_reduce_fusion
  108.1 2.3 %copy.166 = bf16[24,32,8,256]{3,2,0,1:T(8,128)(2,1)S(1)} copy(bf16[24,32,8,256]{3,2,1,0:T(8,128)(2,1)} %bitcast.137) | data formatting | bytes 6291456 | tf_op jit(solution)/shard_map/reshape | solution.py:191
  111.2 2.4 %gather_fusion = bf16[32,192,256]{2,1,0:T(8,128)(2,1)} fusion(bf16[192,32,256]{2,0,1:T(8,128)(2,1)S(1)} %bitcast.136, s32[1024]{0:T(1024)S(1)} %pad_clamp_fusion), kind=kCustom, calls=%fused_computation | custom fusion | bytes 6291584 | tf_op jit(solution)/shard_map/jit(_take)/gather | solution.py:190
  113.8 0.9 slice.238
  114.6 3.4 %fusion.6 = f32[264,192]{0,1:T(8,128)S(1)} fusion(bf16[16,264,256]{2,1,0:T(8,128)(2,1)} %constant_dynamic-update-slice_fusion, bf16[192,32,256]{2,0,1:T(8,128)(2,1)} %bitcast.138), kind=kOutput, calls=%fused_computation.10 | convolution fusion | flops 415236096 | bytes 3938304 | tf_op jit(solution)/shard_map/dot_general | solution.py:194
  118.0 2.8 %fusion.9 = f32[264,192]{0,1:T(8,128)S(1)} fusion(bf16[16,264,256]{2,1,0:T(8,128)(2,1)} %collective-permute-done.15, bf16[192,32,256]{2,0,1:T(8,128)(2,1)S(1)} %bitcast.139), kind=kOutput, calls=%fused_computation.11 | convolution fusion | flops 415236096 | bytes 3938304 | tf_op jit(solution)/shard_map/dot_general | solution.py:199
  120.8 0.4 convolution_convert_fusion
  121.2 1.0 copy.119
  122.2 4.7 %all-to-all-start = ((bf16[32,32,192]{2,1,0:T(8,128)(2,1)}), bf16[32,32,192]{2,1,0:T(8,128)(2,1)S(1)}, u32[]{:S(2)}, u32[]{:S(2)}) async-start(bf16[32,32,192]{2,1,0:T(8,128)(2,1)} %bitcast.20), calls=%async_computation | async-start | bytes 1048576 | tf_op jit(solution)/shard_map/all_to_all | solution.py:229
  126.9 0.9 slice.239
  127.9 0.6 multiply_reduce_fusion.1
  129.3 9.2 %all-to-all-done = bf16[32,32,192]{2,1,0:T(8,128)(2,1)S(1)} async-done(((bf16[32,32,192]{2,1,0:T(8,128)(2,1)}), bf16[32,32,192]{2,1,0:T(8,128)(2,1)S(1)}, u32[]{:S(2)}, u32[]{:S(2)}) %all-to-all-start) | async-done | bytes 393248 | tf_op jit(solution)/shard_map/all_to_all | solution.py:229
  138.5 0.3 copy.120
  138.8 0.5 all_to_all.16
  139.3 0.5 fusion.19
  139.9 1.0 fusion.22
  (93 shorter events, 4.2 us)
Async XLA Ops:
  0.0 10.8 %copy-start = (bf16[256,256]{1,0:T(8,128)(2,1)S(1)}, bf16[256,256]{1,0:T(8,128)(2,1)}, u32[]{:S(2)}) copy-start(bf16[256,256]{1,0:T(8,128)(2,1)} %param.13) | copy-start | bytes 393220
  0.0 12.4 %copy-start.8 = (pred[16]{0:T(512)(128)(4,1)S(1)}, pred[16]{0:T(512)(128)(4,1)}, u32[]{:S(2)}) copy-start(pred[16]{0:T(512)(128)(4,1)} %constant.136.clone) | copy-start | bytes 52
  0.0 12.1 %copy-start.2 = (s32[256,2]{0,1:T(2,128)S(1)}, s32[256,2]{0,1:T(2,128)}, u32[]{:S(2)}) copy-start(s32[256,2]{0,1:T(2,128)} %param.18) | copy-start | bytes 6148
  2.0 12.5 %copy-start.7 = (pred[16]{0:T(512)(128)(4,1)S(1)}, pred[16]{0:T(512)(128)(4,1)}, u32[]{:S(2)}) copy-start(pred[16]{0:T(512)(128)(4,1)} %constant.137.clone) | copy-start | bytes 52
  4.3 5.0 %collective-permute-start = (f32[2,136,128]{2,1,0:T(8,128)S(1)}, f32[2,136,128]{2,1,0:T(8,128)S(1)}, u32[]{:S(2)}, u32[]{:S(2)}) collective-permute-start(f32[2,136,128]{2,1,0:T(8,128)S(1)} %pad_maximum_fusion.1), channel_id=1, source_target_pairs={{0,32},{64,96},{128,160},{192,224},{256,288},{320,352},{384,416},{... | collective-permute-start | bytes 417800 | tf_op jit(solution)/shard_map/ppermute | solution.py:85
  6.9 9.8 %copy-start.3 = (f32[192]{0:T(256)S(1)}, f32[192]{0:T(256)}, u32[]{:S(2)}) copy-start(f32[192]{0:T(256)} %param.20) | copy-start | bytes 2308
  6.9 9.8 %copy-start.6 = (pred[16]{0:T(512)(128)(4,1)S(1)}, pred[16]{0:T(512)(128)(4,1)}, u32[]{:S(2)}) copy-start(pred[16]{0:T(512)(128)(4,1)} %constant.138.clone) | copy-start | bytes 52
  10.1 9.3 %copy-start.5 = (pred[16]{0:T(512)(128)(4,1)S(1)}, pred[16]{0:T(512)(128)(4,1)}, u32[]{:S(2)}) copy-start(pred[16]{0:T(512)(128)(4,1)} %constant.139.clone) | copy-start | bytes 52
  10.1 3.0 %collective-permute-start.1 = (f32[2,136,128]{2,1,0:T(8,128)S(1)}, f32[2,136,128]{2,1,0:T(8,128)S(1)}, u32[]{:S(2)}, u32[]{:S(2)}) collective-permute-start(f32[2,136,128]{2,1,0:T(8,128)S(1)} %maximum_select_fusion), channel_id=1, source_target_pairs={{32,96},{160,224},{288,352},{416,480},{33,97},{161,225},{289,353},... | collective-permute-start | bytes 417800 | tf_op jit(solution)/shard_map/ppermute | solution.py:85
  13.8 1.4 collective-permute-start.2
  16.0 1.4 %collective-permute-start.3 = (f32[2,136,128]{2,1,0:T(8,128)S(1)}, f32[2,136,128]{2,1,0:T(8,128)S(1)}, u32[]{:S(2)}, u32[]{:S(2)}) collective-permute-start(f32[2,136,128]{2,1,0:T(8,128)S(1)} %maximum_select_fusion.2), channel_id=1, source_target_pairs={{224,352},{225,353},{226,354},{227,355},{228,356},{229,357},{230,3... | collective-permute-start | bytes 417800 | tf_op jit(solution)/shard_map/ppermute | solution.py:85
  18.2 1.9 %collective-permute-start.4 = (f32[2,136,128]{2,1,0:T(8,128)S(1)}, f32[2,136,128]{2,1,0:T(8,128)S(1)}, u32[]{:S(2)}, u32[]{:S(2)}) collective-permute-start(f32[2,136,128]{2,1,0:T(8,128)S(1)} %maximum_select_fusion.3), channel_id=1, source_target_pairs={{96,160},{224,288},{352,416},{97,161},{225,289},{353,417},{98,162}... | collective-permute-start | bytes 417800 | tf_op jit(solution)/shard_map/ppermute | solution.py:85
  20.9 3.3 %collective-permute-start.5 = (f32[2,136,128]{2,1,0:T(8,128)S(1)}, f32[2,136,128]{2,1,0:T(8,128)S(1)}, u32[]{:S(2)}, u32[]{:S(2)}) collective-permute-start(f32[2,136,128]{2,1,0:T(8,128)S(1)} %maximum_select_fusion.4), channel_id=1, source_target_pairs={{32,96},{96,160},{160,224},{224,288},{288,352},{352,416},{416,480}... | collective-permute-start | bytes 417800 | tf_op jit(solution)/shard_map/ppermute | solution.py:111
  22.8 30.3 %collective-permute-start.6 = (f32[2,136,128]{2,1,0:T(8,128)S(1)}, f32[2,136,128]{2,1,0:T(8,128)S(1)}, u32[]{:S(2)}, u32[]{:S(2)}) collective-permute-start(f32[2,136,128]{2,1,0:T(8,128)S(1)} %maximum_select_fusion.4), channel_id=1, source_target_pairs={{32,64},{96,128},{160,192},{224,256},{288,320},{352,384},{416,448}... | collective-permute-start | bytes 417800 | tf_op jit(solution)/shard_map/ppermute | solution.py:110
  53.9 16.5 %collective-permute-start.7 = (bf16[1,264,256]{2,1,0:T(8,128)(2,1)S(1)}, bf16[1,264,256]{2,1,0:T(8,128)(2,1)S(1)}, u32[]{:S(2)}, u32[]{:S(2)}) collective-permute-start(bf16[1,264,256]{2,1,0:T(8,128)(2,1)S(1)} %maximum_bitcast_fusion), channel_id=1, source_target_pairs={{0,24},{8,0},{16,8},{24,16},{1,25},{9,1},{17,9},{25,17},{2,26},{10... | collective-permute-start | bytes 405512 | tf_op jit(solution)/shard_map/ppermute | solution.py:63
  58.3 12.1 %collective-permute-start.10 = (bf16[1,264,256]{2,1,0:T(8,128)(2,1)S(1)}, bf16[1,264,256]{2,1,0:T(8,128)(2,1)S(1)}, u32[]{:S(2)}, u32[]{:S(2)}) collective-permute-start(bf16[1,264,256]{2,1,0:T(8,128)(2,1)S(1)} %maximum_bitcast_fusion), channel_id=1, source_target_pairs={{0,8},{8,16},{16,24},{24,0},{1,9},{9,17},{17,25},{25,1},{2,10},{10... | collective-permute-start | bytes 405512 | tf_op jit(solution)/shard_map/ppermute | solution.py:63
  60.2 7.5 %collective-permute-start.8 = (bf16[1,264,128]{2,1,0:T(8,128)(2,1)S(1)}, bf16[1,264,128]{2,1,0:T(8,128)(2,1)S(1)}, u32[]{:S(2)}, u32[]{:S(2)}) collective-permute-start(bf16[1,264,128]{2,1,0:T(8,128)(2,1)S(1)} %get-tuple-element.26), channel_id=1, source_target_pairs={{0,16},{8,24},{16,0},{24,8},{1,17},{9,25},{17,1},{25,9},{2,18},{10... | collective-permute-start | bytes 202760 | tf_op jit(solution)/shard_map/ppermute | solution.py:63
  63.9 6.5 %collective-permute-start.9 = (bf16[1,264,128]{2,1,0:T(8,128)(2,1)S(1)}, bf16[1,264,128]{2,1,0:T(8,128)(2,1)S(1)}, u32[]{:S(2)}, u32[]{:S(2)}) collective-permute-start(bf16[1,264,128]{2,1,0:T(8,128)(2,1)S(1)} %get-tuple-element.25), channel_id=1, source_target_pairs={{0,16},{8,24},{16,0},{24,8},{1,17},{9,25},{17,1},{25,9},{2,18},{10... | collective-permute-start | bytes 202760 | tf_op jit(solution)/shard_map/ppermute | solution.py:63
  70.5 16.1 %collective-permute-start.11 = (bf16[4,264,256]{2,1,0:T(8,128)(2,1)S(1)}, bf16[4,264,256]{2,1,0:T(8,128)(2,1)S(1)}, u32[]{:S(2)}, u32[]{:S(2)}) collective-permute-start(bf16[4,264,256]{2,1,0:T(8,128)(2,1)S(1)} %pad_maximum_fusion), channel_id=1, source_target_pairs={{0,6},{2,0},{4,2},{6,4},{1,7},{3,1},{5,3},{7,5},{8,14},{10,8},{12,... | collective-permute-start | bytes 1622024 | tf_op jit(solution)/shard_map/ppermute | solution.py:63
  75.2 17.9 %collective-permute-start.14 = (bf16[4,264,256]{2,1,0:T(8,128)(2,1)S(1)}, bf16[4,264,256]{2,1,0:T(8,128)(2,1)S(1)}, u32[]{:S(2)}, u32[]{:S(2)}) collective-permute-start(bf16[4,264,256]{2,1,0:T(8,128)(2,1)S(1)} %pad_maximum_fusion), channel_id=1, source_target_pairs={{0,2},{2,4},{4,6},{6,0},{1,3},{3,5},{5,7},{7,1},{8,10},{10,12},{12... | collective-permute-start | bytes 1622024 | tf_op jit(solution)/shard_map/ppermute | solution.py:63
  77.2 11.4 %collective-permute-start.13 = (bf16[4,264,128]{2,1,0:T(8,128)(2,1)S(1)}, bf16[4,264,128]{2,1,0:T(8,128)(2,1)S(1)}, u32[]{:S(2)}, u32[]{:S(2)}) collective-permute-start(bf16[4,264,128]{2,1,0:T(8,128)(2,1)S(1)} %get-tuple-element.24), channel_id=1, source_target_pairs={{0,4},{2,6},{4,0},{6,2},{1,5},{3,7},{5,1},{7,3},{8,12},{10,14},{12... | collective-permute-start | bytes 811016 | tf_op jit(solution)/shard_map/ppermute | solution.py:63
  80.7 11.4 %collective-permute-start.12 = (bf16[4,264,128]{2,1,0:T(8,128)(2,1)S(1)}, bf16[4,264,128]{2,1,0:T(8,128)(2,1)S(1)}, u32[]{:S(2)}, u32[]{:S(2)}) collective-permute-start(bf16[4,264,128]{2,1,0:T(8,128)(2,1)S(1)} %get-tuple-element.23), channel_id=1, source_target_pairs={{0,4},{2,6},{4,0},{6,2},{1,5},{3,7},{5,1},{7,3},{8,12},{10,14},{12... | collective-permute-start | bytes 811016 | tf_op jit(solution)/shard_map/ppermute | solution.py:63
  93.9 24.1 %collective-permute-start.15 = (bf16[16,264,256]{2,1,0:T(8,128)(2,1)}, bf16[16,264,256]{2,1,0:T(8,128)(2,1)}, u32[]{:S(2)}, u32[]{:S(2)}) collective-permute-start(bf16[16,264,256]{2,1,0:T(8,128)(2,1)} %constant_dynamic-update-slice_fusion), channel_id=1, source_target_pairs={{0,1},{1,0},{2,3},{3,2},{4,5},{5,4},{6,7},{7,6},{8,9},{9,8},{10,11... | collective-permute-start | bytes 6488072 | tf_op jit(solution)/shard_map/ppermute | solution.py:181
  108.1 2.6 %copy-start.4 = (s32[64]{0:T(128)S(1)}, s32[64]{0:T(128)}, u32[]{:S(2)}) copy-start(s32[64]{0:T(128)} %param.19) | copy-start | bytes 772
  114.6 3.4 %copy-start.1 = (bf16[32,192,256]{2,1,0:T(8,128)(2,1)S(1)}, bf16[32,192,256]{2,1,0:T(8,128)(2,1)}, u32[]{:S(2)}) copy-start(bf16[32,192,256]{2,1,0:T(8,128)(2,1)} %gather_fusion) | copy-start | bytes 9437188
  122.2 16.3 %all-to-all-start = ((bf16[32,32,192]{2,1,0:T(8,128)(2,1)}), bf16[32,32,192]{2,1,0:T(8,128)(2,1)S(1)}, u32[]{:S(2)}, u32[]{:S(2)}) async-start(bf16[32,32,192]{2,1,0:T(8,128)(2,1)} %bitcast.20), calls=%async_computation | async-start | bytes 1048576 | tf_op jit(solution)/shard_map/all_to_all | solution.py:229

commit v6 on v5

--- a/solution.py
+++ b/solution.py
@@ -44,11 +44,6 @@
 def normalize(outputs):
     mean_square = jnp.mean(outputs * outputs, axis=-1, keepdims=True)
     return (outputs * lax.rsqrt(mean_square + 1e-06)).astype(jnp.bfloat16)
-
-
-def passed_along(value, axis, steps):
-    count = lax.axis_size(axis)
-    return lax.ppermute(value, axis, [(source, source + steps) for source in range(count - steps)])
 
 
 def combined(left, right):
@@ -133,7 +128,7 @@
     return total
 
 
-def local(queries, key_rows, value_rows, log_decay, out_weight, expert_ids, flagged, direction):
+def local_body(queries, key_rows, value_rows, log_decay, out_weight, expert_ids, flagged, direction):
     block_rows = queries.shape[0]
     local_width = queries.shape[1]
     local_heads = local_width // HEAD
@@ -263,5 +258,5 @@
         P(EP),
     )
     return jax.shard_map(
-        local, mesh=fine, in_specs=placed, out_specs=P(EP, "ctx", None), check_vma=False
-    )
+        local_body, mesh=fine, in_specs=placed, out_specs=P(EP, "ctx", None), check_vma=False
+    )

time: 142 us -> 142 us (level)
  no operation moved by 1% of the time
where the time goes in v6:
time: 142 us; the launch traced here: 141 us
  starting transfers between devices  51.8 us (36%)
  waiting for transfers between devices  46.7 us (33%)
  local copies, waits for them, and re-layouts  20.6 us (15%)
  matrix products  10.6 us (7%)
  other arithmetic  9.89 us (7%)
    ppermute x1, waiting for transfers between devices, exclusive_scan(): from_odd = lax.ppermute(segment, axis, to_even)  28.9 us
    ppermute x8, starting transfers between devices, shifted(): lax.ppermute(value, axis, [(i, (i + steps) % RING) for i in range(RING)])  26.5 us
    ppermute x1, starting transfers between devices, local_body(): far = lax.ppermute(near, 'core', [(0, 1), (1, 0)])  13.4 us
    all_to_all x1, waiting for transfers between devices, local_body(): lax.all_to_all(tile_rows, EP, split_axis=0, concat_axis=2, tiled=True)  9.21 us
    ppermute x8, waiting for transfers between devices, shifted(): lax.ppermute(value, axis, [(i, (i + steps) % RING) for i in range(RING)])  7.5 us
    ppermute x5, starting transfers between devices, step(): arrived = lax.ppermute(current, axis, pairs)  5.33 us
    all_to_all x1, starting transfers between devices, local_body(): lax.all_to_all(tile_rows, EP, split_axis=0, concat_axis=2, tiled=True)  4.65 us
    unnamed x25, local copies, waits for them, and re-layouts  3.65 us
  transfers between devices with their start and end apart: 17, of which 7 were waited for; matrix products, arithmetic and copies ran while one was open for 18% of the time, Pallas kernels for 0%

profile of v6, /device:TPU:385, one launch (start us, length us, event | category | flops | bytes accessed | tf_op | source)
XLA Modules:
  0.0 140.8 jit_solution(17227484421481504463)
XLA Ops:
  0.0 0.7 reshape.306
  0.8 0.6 reduce-window.16
  1.8 0.2 slice_reduce_fusion.2
  2.1 1.0 copy.124
  3.1 1.1 convolution_add_fusion
  4.3 2.7 %collective-permute-start = (f32[2,136,128]{2,1,0:T(8,128)S(1)}, f32[2,136,128]{2,1,0:T(8,128)S(1)}, u32[]{:S(2)}, u32[]{:S(2)}) collective-permute-start(f32[2,136,128]{2,1,0:T(8,128)S(1)} %pad_maximum_fusion.1), channel_id=1, source_target_pairs={{0,32},{64,96},{128,160},{192,224},{256,288},{320,352},{384,416},{... | collective-permute-start | bytes 417800 | tf_op jit(solution)/shard_map/ppermute | solution.py:80
  6.9 1.2 dynamic_slice.29
  8.2 1.0 collective-permute-done
  9.4 0.7 maximum_select_fusion
  10.1 0.7 collective-permute-start.1
  10.8 1.3 fusion.15
  12.4 0.6 dynamic_slice.28
  13.2 0.7 maximum_select_fusion.1
  13.8 0.7 collective-permute-start.2
  14.5 0.6 dynamic_slice.27
  15.3 0.7 maximum_select_fusion.2
  16.0 0.7 collective-permute-start.3
  16.7 0.6 dynamic_slice.26
  17.5 0.7 maximum_select_fusion.3
  18.2 0.7 collective-permute-start.4
  18.9 0.5 fusion.14
  19.4 0.6 dynamic_slice.25
  20.2 0.7 maximum_select_fusion.4
  20.9 0.7 collective-permute-start.5
  21.6 1.2 reduce-window.14
  22.8 1.3 collective-permute-start.6
  24.2 28.9 %collective-permute-done.6 = f32[2,136,128]{2,1,0:T(8,128)S(1)} collective-permute-done((f32[2,136,128]{2,1,0:T(8,128)S(1)}, f32[2,136,128]{2,1,0:T(8,128)S(1)}, u32[]{:S(2)}, u32[]{:S(2)}) %collective-permute-start.6) | collective-permute-done | bytes 139296 | tf_op jit(solution)/shard_map/ppermute | solution.py:105
  53.2 0.5 multiply_reduce_fusion
  53.9 4.4 %collective-permute-start.7 = (bf16[1,264,256]{2,1,0:T(8,128)(2,1)S(1)}, bf16[1,264,256]{2,1,0:T(8,128)(2,1)S(1)}, u32[]{:S(2)}, u32[]{:S(2)}) collective-permute-start(bf16[1,264,256]{2,1,0:T(8,128)(2,1)S(1)} %maximum_bitcast_fusion), channel_id=1, source_target_pairs={{0,24},{8,0},{16,8},{24,16},{1,25},{9,1},{17,9},{25,17},{2,26},{10... | collective-permute-start | bytes 405512 | tf_op jit(solution)/shard_map/ppermute | solution.py:58
  58.3 1.9 %collective-permute-start.10 = (bf16[1,264,256]{2,1,0:T(8,128)(2,1)S(1)}, bf16[1,264,256]{2,1,0:T(8,128)(2,1)S(1)}, u32[]{:S(2)}, u32[]{:S(2)}) collective-permute-start(bf16[1,264,256]{2,1,0:T(8,128)(2,1)S(1)} %maximum_bitcast_fusion), channel_id=1, source_target_pairs={{0,8},{8,16},{16,24},{24,0},{1,9},{9,17},{17,25},{25,1},{2,10},{10... | collective-permute-start | bytes 405512 | tf_op jit(solution)/shard_map/ppermute | solution.py:58
  60.2 3.6 %collective-permute-start.8 = (bf16[1,264,128]{2,1,0:T(8,128)(2,1)S(1)}, bf16[1,264,128]{2,1,0:T(8,128)(2,1)S(1)}, u32[]{:S(2)}, u32[]{:S(2)}) collective-permute-start(bf16[1,264,128]{2,1,0:T(8,128)(2,1)S(1)} %get-tuple-element.26), channel_id=1, source_target_pairs={{0,16},{8,24},{16,0},{24,8},{1,17},{9,25},{17,1},{25,9},{2,18},{10... | collective-permute-start | bytes 202760 | tf_op jit(solution)/shard_map/ppermute | solution.py:58
  63.9 3.2 %collective-permute-start.9 = (bf16[1,264,128]{2,1,0:T(8,128)(2,1)S(1)}, bf16[1,264,128]{2,1,0:T(8,128)(2,1)S(1)}, u32[]{:S(2)}, u32[]{:S(2)}) collective-permute-start(bf16[1,264,128]{2,1,0:T(8,128)(2,1)S(1)} %get-tuple-element.25), channel_id=1, source_target_pairs={{0,16},{8,24},{16,0},{24,8},{1,17},{9,25},{17,1},{25,9},{2,18},{10... | collective-permute-start | bytes 202760 | tf_op jit(solution)/shard_map/ppermute | solution.py:58
  67.0 0.6 constant_dynamic-update-slice_fusion.6
  67.7 2.7 %collective-permute-done.9 = bf16[1,264,128]{2,1,0:T(8,128)(2,1)S(1)} collective-permute-done((bf16[1,264,128]{2,1,0:T(8,128)(2,1)S(1)}, bf16[1,264,128]{2,1,0:T(8,128)(2,1)S(1)}, u32[]{:S(2)}, u32[]{:S(2)}) %collective-permute-start.9) | collective-permute-done | bytes 67616 | tf_op jit(solution)/shard_map/ppermute | solution.py:58
  70.5 4.6 %collective-permute-start.11 = (bf16[4,264,256]{2,1,0:T(8,128)(2,1)S(1)}, bf16[4,264,256]{2,1,0:T(8,128)(2,1)S(1)}, u32[]{:S(2)}, u32[]{:S(2)}) collective-permute-start(bf16[4,264,256]{2,1,0:T(8,128)(2,1)S(1)} %pad_maximum_fusion), channel_id=1, source_target_pairs={{0,6},{2,0},{4,2},{6,4},{1,7},{3,1},{5,3},{7,5},{8,14},{10,8},{12,... | collective-permute-start | bytes 1622024 | tf_op jit(solution)/shard_map/ppermute | solution.py:58
  75.2 1.9 %collective-permute-start.14 = (bf16[4,264,256]{2,1,0:T(8,128)(2,1)S(1)}, bf16[4,264,256]{2,1,0:T(8,128)(2,1)S(1)}, u32[]{:S(2)}, u32[]{:S(2)}) collective-permute-start(bf16[4,264,256]{2,1,0:T(8,128)(2,1)S(1)} %pad_maximum_fusion), channel_id=1, source_target_pairs={{0,2},{2,4},{4,6},{6,0},{1,3},{3,5},{5,7},{7,1},{8,10},{10,12},{12... | collective-permute-start | bytes 1622024 | tf_op jit(solution)/shard_map/ppermute | solution.py:58
  77.2 3.5 %collective-permute-start.13 = (bf16[4,264,128]{2,1,0:T(8,128)(2,1)S(1)}, bf16[4,264,128]{2,1,0:T(8,128)(2,1)S(1)}, u32[]{:S(2)}, u32[]{:S(2)}) collective-permute-start(bf16[4,264,128]{2,1,0:T(8,128)(2,1)S(1)} %get-tuple-element.24), channel_id=1, source_target_pairs={{0,4},{2,6},{4,0},{6,2},{1,5},{3,7},{5,1},{7,3},{8,12},{10,14},{12... | collective-permute-start | bytes 811016 | tf_op jit(solution)/shard_map/ppermute | solution.py:58
  80.7 3.2 %collective-permute-start.12 = (bf16[4,264,128]{2,1,0:T(8,128)(2,1)S(1)}, bf16[4,264,128]{2,1,0:T(8,128)(2,1)S(1)}, u32[]{:S(2)}, u32[]{:S(2)}) collective-permute-start(bf16[4,264,128]{2,1,0:T(8,128)(2,1)S(1)} %get-tuple-element.23), channel_id=1, source_target_pairs={{0,4},{2,6},{4,0},{6,2},{1,5},{3,7},{5,1},{7,3},{8,12},{10,14},{12... | collective-permute-start | bytes 811016 | tf_op jit(solution)/shard_map/ppermute | solution.py:58
  84.0 0.7 constant_dynamic-update-slice_fusion.5
  84.6 0.6 constant_dynamic-update-slice_fusion.4
  85.3 0.7 constant_dynamic-update-slice_fusion.3
  85.9 0.7 constant_dynamic-update-slice_fusion.2
  86.6 0.8 constant_dynamic-update-slice_fusion.1
  87.4 1.1 collective-permute-done.13
  88.5 3.6 %collective-permute-done.12 = bf16[4,264,128]{2,1,0:T(8,128)(2,1)S(1)} collective-permute-done((bf16[4,264,128]{2,1,0:T(8,128)(2,1)S(1)}, bf16[4,264,128]{2,1,0:T(8,128)(2,1)S(1)}, u32[]{:S(2)}, u32[]{:S(2)}) %collective-permute-start.12) | collective-permute-done | bytes 270368 | tf_op jit(solution)/shard_map/ppermute | solution.py:58
  92.1 0.9 maximum_dynamic-update-slice_fusion
  93.1 0.8 constant_dynamic-update-slice_fusion
  93.9 13.4 %collective-permute-start.15 = (bf16[16,264,256]{2,1,0:T(8,128)(2,1)}, bf16[16,264,256]{2,1,0:T(8,128)(2,1)}, u32[]{:S(2)}, u32[]{:S(2)}) collective-permute-start(bf16[16,264,256]{2,1,0:T(8,128)(2,1)} %constant_dynamic-update-slice_fusion), channel_id=1, source_target_pairs={{0,1},{1,0},{2,3},{3,2},{4,5},{5,4},{6,7},{7,6},{8,9},{9,8},{10,11... | collective-permute-start | bytes 6488072 | tf_op jit(solution)/shard_map/ppermute | solution.py:176
  107.4 0.2 slice_reduce_fusion
  108.1 2.3 %copy.166 = bf16[24,32,8,256]{3,2,0,1:T(8,128)(2,1)S(1)} copy(bf16[24,32,8,256]{3,2,1,0:T(8,128)(2,1)} %bitcast.137) | data formatting | bytes 6291456 | tf_op jit(solution)/shard_map/reshape | solution.py:186
  111.2 2.4 %gather_fusion = bf16[32,192,256]{2,1,0:T(8,128)(2,1)} fusion(bf16[192,32,256]{2,0,1:T(8,128)(2,1)S(1)} %bitcast.136, s32[1024]{0:T(1024)S(1)} %pad_clamp_fusion), kind=kCustom, calls=%fused_computation | custom fusion | bytes 6291584 | tf_op jit(solution)/shard_map/jit(_take)/gather | solution.py:185
  113.8 0.9 slice.238
  114.6 3.4 %fusion.6 = f32[264,192]{0,1:T(8,128)S(1)} fusion(bf16[16,264,256]{2,1,0:T(8,128)(2,1)} %constant_dynamic-update-slice_fusion, bf16[192,32,256]{2,0,1:T(8,128)(2,1)} %bitcast.138), kind=kOutput, calls=%fused_computation.10 | convolution fusion | flops 415236096 | bytes 3938304 | tf_op jit(solution)/shard_map/dot_general | solution.py:189
  118.0 2.8 %fusion.9 = f32[264,192]{0,1:T(8,128)S(1)} fusion(bf16[16,264,256]{2,1,0:T(8,128)(2,1)} %collective-permute-done.15, bf16[192,32,256]{2,0,1:T(8,128)(2,1)S(1)} %bitcast.139), kind=kOutput, calls=%fused_computation.11 | convolution fusion | flops 415236096 | bytes 3938304 | tf_op jit(solution)/shard_map/dot_general | solution.py:194
  120.8 0.4 convolution_convert_fusion
  121.2 1.0 copy.119
  122.2 4.7 %all-to-all-start = ((bf16[32,32,192]{2,1,0:T(8,128)(2,1)}), bf16[32,32,192]{2,1,0:T(8,128)(2,1)S(1)}, u32[]{:S(2)}, u32[]{:S(2)}) async-start(bf16[32,32,192]{2,1,0:T(8,128)(2,1)} %bitcast.20), calls=%async_computation | async-start | bytes 1048576 | tf_op jit(solution)/shard_map/all_to_all | solution.py:224
  126.9 0.9 slice.239
  127.9 0.6 multiply_reduce_fusion.1
  129.3 9.2 %all-to-all-done = bf16[32,32,192]{2,1,0:T(8,128)(2,1)S(1)} async-done(((bf16[32,32,192]{2,1,0:T(8,128)(2,1)}), bf16[32,32,192]{2,1,0:T(8,128)(2,1)S(1)}, u32[]{:S(2)}, u32[]{:S(2)}) %all-to-all-start) | async-done | bytes 393248 | tf_op jit(solution)/shard_map/all_to_all | solution.py:224
  138.5 0.3 copy.120
  138.8 0.5 all_to_all.16
  139.3 0.5 fusion.19
  139.9 1.0 fusion.22
  (93 shorter events, 4.2 us)
Async XLA Ops:
  0.0 10.8 %copy-start = (bf16[256,256]{1,0:T(8,128)(2,1)S(1)}, bf16[256,256]{1,0:T(8,128)(2,1)}, u32[]{:S(2)}) copy-start(bf16[256,256]{1,0:T(8,128)(2,1)} %param.13) | copy-start | bytes 393220
  0.0 12.4 %copy-start.8 = (pred[16]{0:T(512)(128)(4,1)S(1)}, pred[16]{0:T(512)(128)(4,1)}, u32[]{:S(2)}) copy-start(pred[16]{0:T(512)(128)(4,1)} %constant.136.clone) | copy-start | bytes 52
  0.0 12.1 %copy-start.2 = (s32[256,2]{0,1:T(2,128)S(1)}, s32[256,2]{0,1:T(2,128)}, u32[]{:S(2)}) copy-start(s32[256,2]{0,1:T(2,128)} %param.18) | copy-start | bytes 6148
  2.0 12.5 %copy-start.7 = (pred[16]{0:T(512)(128)(4,1)S(1)}, pred[16]{0:T(512)(128)(4,1)}, u32[]{:S(2)}) copy-start(pred[16]{0:T(512)(128)(4,1)} %constant.137.clone) | copy-start | bytes 52
  4.3 5.0 %collective-permute-start = (f32[2,136,128]{2,1,0:T(8,128)S(1)}, f32[2,136,128]{2,1,0:T(8,128)S(1)}, u32[]{:S(2)}, u32[]{:S(2)}) collective-permute-start(f32[2,136,128]{2,1,0:T(8,128)S(1)} %pad_maximum_fusion.1), channel_id=1, source_target_pairs={{0,32},{64,96},{128,160},{192,224},{256,288},{320,352},{384,416},{... | collective-permute-start | bytes 417800 | tf_op jit(solution)/shard_map/ppermute | solution.py:80
  6.9 9.8 %copy-start.3 = (f32[192]{0:T(256)S(1)}, f32[192]{0:T(256)}, u32[]{:S(2)}) copy-start(f32[192]{0:T(256)} %param.20) | copy-start | bytes 2308
  6.9 9.8 %copy-start.6 = (pred[16]{0:T(512)(128)(4,1)S(1)}, pred[16]{0:T(512)(128)(4,1)}, u32[]{:S(2)}) copy-start(pred[16]{0:T(512)(128)(4,1)} %constant.138.clone) | copy-start | bytes 52
  10.1 9.3 %copy-start.5 = (pred[16]{0:T(512)(128)(4,1)S(1)}, pred[16]{0:T(512)(128)(4,1)}, u32[]{:S(2)}) copy-start(pred[16]{0:T(512)(128)(4,1)} %constant.139.clone) | copy-start | bytes 52
  10.1 3.0 %collective-permute-start.1 = (f32[2,136,128]{2,1,0:T(8,128)S(1)}, f32[2,136,128]{2,1,0:T(8,128)S(1)}, u32[]{:S(2)}, u32[]{:S(2)}) collective-permute-start(f32[2,136,128]{2,1,0:T(8,128)S(1)} %maximum_select_fusion), channel_id=1, source_target_pairs={{32,96},{160,224},{288,352},{416,480},{33,97},{161,225},{289,353},... | collective-permute-start | bytes 417800 | tf_op jit(solution)/shard_map/ppermute | solution.py:80
  13.8 1.4 collective-permute-start.2
  16.0 1.4 %collective-permute-start.3 = (f32[2,136,128]{2,1,0:T(8,128)S(1)}, f32[2,136,128]{2,1,0:T(8,128)S(1)}, u32[]{:S(2)}, u32[]{:S(2)}) collective-permute-start(f32[2,136,128]{2,1,0:T(8,128)S(1)} %maximum_select_fusion.2), channel_id=1, source_target_pairs={{224,352},{225,353},{226,354},{227,355},{228,356},{229,357},{230,3... | collective-permute-start | bytes 417800 | tf_op jit(solution)/shard_map/ppermute | solution.py:80
  18.2 1.9 %collective-permute-start.4 = (f32[2,136,128]{2,1,0:T(8,128)S(1)}, f32[2,136,128]{2,1,0:T(8,128)S(1)}, u32[]{:S(2)}, u32[]{:S(2)}) collective-permute-start(f32[2,136,128]{2,1,0:T(8,128)S(1)} %maximum_select_fusion.3), channel_id=1, source_target_pairs={{96,160},{224,288},{352,416},{97,161},{225,289},{353,417},{98,162}... | collective-permute-start | bytes 417800 | tf_op jit(solution)/shard_map/ppermute | solution.py:80
  20.9 3.3 %collective-permute-start.5 = (f32[2,136,128]{2,1,0:T(8,128)S(1)}, f32[2,136,128]{2,1,0:T(8,128)S(1)}, u32[]{:S(2)}, u32[]{:S(2)}) collective-permute-start(f32[2,136,128]{2,1,0:T(8,128)S(1)} %maximum_select_fusion.4), channel_id=1, source_target_pairs={{32,96},{96,160},{160,224},{224,288},{288,352},{352,416},{416,480}... | collective-permute-start | bytes 417800 | tf_op jit(solution)/shard_map/ppermute | solution.py:106
  22.8 30.3 %collective-permute-start.6 = (f32[2,136,128]{2,1,0:T(8,128)S(1)}, f32[2,136,128]{2,1,0:T(8,128)S(1)}, u32[]{:S(2)}, u32[]{:S(2)}) collective-permute-start(f32[2,136,128]{2,1,0:T(8,128)S(1)} %maximum_select_fusion.4), channel_id=1, source_target_pairs={{32,64},{96,128},{160,192},{224,256},{288,320},{352,384},{416,448}... | collective-permute-start | bytes 417800 | tf_op jit(solution)/shard_map/ppermute | solution.py:105
  53.9 16.5 %collective-permute-start.7 = (bf16[1,264,256]{2,1,0:T(8,128)(2,1)S(1)}, bf16[1,264,256]{2,1,0:T(8,128)(2,1)S(1)}, u32[]{:S(2)}, u32[]{:S(2)}) collective-permute-start(bf16[1,264,256]{2,1,0:T(8,128)(2,1)S(1)} %maximum_bitcast_fusion), channel_id=1, source_target_pairs={{0,24},{8,0},{16,8},{24,16},{1,25},{9,1},{17,9},{25,17},{2,26},{10... | collective-permute-start | bytes 405512 | tf_op jit(solution)/shard_map/ppermute | solution.py:58
  58.3 12.1 %collective-permute-start.10 = (bf16[1,264,256]{2,1,0:T(8,128)(2,1)S(1)}, bf16[1,264,256]{2,1,0:T(8,128)(2,1)S(1)}, u32[]{:S(2)}, u32[]{:S(2)}) collective-permute-start(bf16[1,264,256]{2,1,0:T(8,128)(2,1)S(1)} %maximum_bitcast_fusion), channel_id=1, source_target_pairs={{0,8},{8,16},{16,24},{24,0},{1,9},{9,17},{17,25},{25,1},{2,10},{10... | collective-permute-start | bytes 405512 | tf_op jit(solution)/shard_map/ppermute | solution.py:58
  60.2 7.5 %collective-permute-start.8 = (bf16[1,264,128]{2,1,0:T(8,128)(2,1)S(1)}, bf16[1,264,128]{2,1,0:T(8,128)(2,1)S(1)}, u32[]{:S(2)}, u32[]{:S(2)}) collective-permute-start(bf16[1,264,128]{2,1,0:T(8,128)(2,1)S(1)} %get-tuple-element.26), channel_id=1, source_target_pairs={{0,16},{8,24},{16,0},{24,8},{1,17},{9,25},{17,1},{25,9},{2,18},{10... | collective-permute-start | bytes 202760 | tf_op jit(solution)/shard_map/ppermute | solution.py:58
  63.9 6.5 %collective-permute-start.9 = (bf16[1,264,128]{2,1,0:T(8,128)(2,1)S(1)}, bf16[1,264,128]{2,1,0:T(8,128)(2,1)S(1)}, u32[]{:S(2)}, u32[]{:S(2)}) collective-permute-start(bf16[1,264,128]{2,1,0:T(8,128)(2,1)S(1)} %get-tuple-element.25), channel_id=1, source_target_pairs={{0,16},{8,24},{16,0},{24,8},{1,17},{9,25},{17,1},{25,9},{2,18},{10... | collective-permute-start | bytes 202760 | tf_op jit(solution)/shard_map/ppermute | solution.py:58
  70.5 16.1 %collective-permute-start.11 = (bf16[4,264,256]{2,1,0:T(8,128)(2,1)S(1)}, bf16[4,264,256]{2,1,0:T(8,128)(2,1)S(1)}, u32[]{:S(2)}, u32[]{:S(2)}) collective-permute-start(bf16[4,264,256]{2,1,0:T(8,128)(2,1)S(1)} %pad_maximum_fusion), channel_id=1, source_target_pairs={{0,6},{2,0},{4,2},{6,4},{1,7},{3,1},{5,3},{7,5},{8,14},{10,8},{12,... | collective-permute-start | bytes 1622024 | tf_op jit(solution)/shard_map/ppermute | solution.py:58
  75.2 17.9 %collective-permute-start.14 = (bf16[4,264,256]{2,1,0:T(8,128)(2,1)S(1)}, bf16[4,264,256]{2,1,0:T(8,128)(2,1)S(1)}, u32[]{:S(2)}, u32[]{:S(2)}) collective-permute-start(bf16[4,264,256]{2,1,0:T(8,128)(2,1)S(1)} %pad_maximum_fusion), channel_id=1, source_target_pairs={{0,2},{2,4},{4,6},{6,0},{1,3},{3,5},{5,7},{7,1},{8,10},{10,12},{12... | collective-permute-start | bytes 1622024 | tf_op jit(solution)/shard_map/ppermute | solution.py:58
  77.2 11.4 %collective-permute-start.13 = (bf16[4,264,128]{2,1,0:T(8,128)(2,1)S(1)}, bf16[4,264,128]{2,1,0:T(8,128)(2,1)S(1)}, u32[]{:S(2)}, u32[]{:S(2)}) collective-permute-start(bf16[4,264,128]{2,1,0:T(8,128)(2,1)S(1)} %get-tuple-element.24), channel_id=1, source_target_pairs={{0,4},{2,6},{4,0},{6,2},{1,5},{3,7},{5,1},{7,3},{8,12},{10,14},{12... | collective-permute-start | bytes 811016 | tf_op jit(solution)/shard_map/ppermute | solution.py:58
  80.7 11.4 %collective-permute-start.12 = (bf16[4,264,128]{2,1,0:T(8,128)(2,1)S(1)}, bf16[4,264,128]{2,1,0:T(8,128)(2,1)S(1)}, u32[]{:S(2)}, u32[]{:S(2)}) collective-permute-start(bf16[4,264,128]{2,1,0:T(8,128)(2,1)S(1)} %get-tuple-element.23), channel_id=1, source_target_pairs={{0,4},{2,6},{4,0},{6,2},{1,5},{3,7},{5,1},{7,3},{8,12},{10,14},{12... | collective-permute-start | bytes 811016 | tf_op jit(solution)/shard_map/ppermute | solution.py:58
  93.9 24.1 %collective-permute-start.15 = (bf16[16,264,256]{2,1,0:T(8,128)(2,1)}, bf16[16,264,256]{2,1,0:T(8,128)(2,1)}, u32[]{:S(2)}, u32[]{:S(2)}) collective-permute-start(bf16[16,264,256]{2,1,0:T(8,128)(2,1)} %constant_dynamic-update-slice_fusion), channel_id=1, source_target_pairs={{0,1},{1,0},{2,3},{3,2},{4,5},{5,4},{6,7},{7,6},{8,9},{9,8},{10,11... | collective-permute-start | bytes 6488072 | tf_op jit(solution)/shard_map/ppermute | solution.py:176
  108.1 2.6 %copy-start.4 = (s32[64]{0:T(128)S(1)}, s32[64]{0:T(128)}, u32[]{:S(2)}) copy-start(s32[64]{0:T(128)} %param.19) | copy-start | bytes 772
  114.6 3.4 %copy-start.1 = (bf16[32,192,256]{2,1,0:T(8,128)(2,1)S(1)}, bf16[32,192,256]{2,1,0:T(8,128)(2,1)}, u32[]{:S(2)}) copy-start(bf16[32,192,256]{2,1,0:T(8,128)(2,1)} %gather_fusion) | copy-start | bytes 9437188
  122.2 16.3 %all-to-all-start = ((bf16[32,32,192]{2,1,0:T(8,128)(2,1)}), bf16[32,32,192]{2,1,0:T(8,128)(2,1)S(1)}, u32[]{:S(2)}, u32[]{:S(2)}) async-start(bf16[32,32,192]{2,1,0:T(8,128)(2,1)} %bitcast.20), calls=%async_computation | async-start | bytes 1048576 | tf_op jit(solution)/shard_map/all_to_all | solution.py:224

commit v7 on v6

--- a/solution.py
+++ b/solution.py
@@ -64,28 +64,22 @@
     return jnp.concatenate([blocks, from_right, far, from_left], axis=0)
 
 
-def received_by(pairs, count, position):
-    table = [False] * count
-    for _, target in pairs:
-        table[target] = True
-    return jnp.asarray(table)[position]
-
-
 def exclusive_scan(value, axis, count):
     position = lax.axis_index(axis)
     if count == 1:
         return jnp.zeros_like(value)
 
-    def step(current, pairs, merge):
+    def step(current, pairs, chosen, merge):
         arrived = lax.ppermute(current, axis, pairs)
-        return arrived, jnp.where(received_by(pairs, count, position), merge(arrived), current)
+        return arrived, jnp.where(chosen, merge(arrived), current)
 
     segment = value
     left_raw = None
     distance = 1
     while 4 * distance <= count:
         pairs = [(j - distance, j) for j in range(count) if (j + 1) % (2 * distance) == 0]
-        arrived, segment = step(segment, pairs, lambda got, seg=segment: combined(got, seg))
+        chosen = (position + 1) % (2 * distance) == 0
+        arrived, segment = step(segment, pairs, chosen, lambda got, seg=segment: combined(got, seg))
         if left_raw is None:
             left_raw = arrived
         distance *= 2
@@ -96,7 +90,8 @@
             for j in range(count)
             if (j + 1) % (2 * distance) == 0 and j + distance < count
         ]
-        _, segment = step(segment, pairs, lambda got, seg=segment: combined(got, seg))
+        chosen = ((position + 1 - distance) % (2 * distance) == 0) & (position >= 3 * distance - 1)
+        _, segment = step(segment, pairs, chosen, lambda got, seg=segment: combined(got, seg))
         distance //= 2
     if left_raw is None:
         left_raw = lax.ppermute(segment, axis, [(j - 1, j) for j in range(1, count, 2)])
@@ -172,7 +167,8 @@
     attended = normalize(outputs).reshape(block_rows, local_width)
     riders = split_parts(direction, local_width)
     block = jnp.concatenate([attended, riders], axis=0)
-    near = ring_gathered(ring_gathered(block[None], "x"), "y")
+    near = ring_gathered(block[None], "x")
+    near = ring_gathered(near, "y")
     far = lax.ppermute(near, "core", [(0, 1), (1, 0)])
 
     offsets = jnp.arange(RING, dtype=jnp.int32)
@@ -187,17 +183,17 @@
     )
     half = near.shape[0]
     projected = lax.dot_general(
-        near,
+        near[:, :block_rows],
         weight_slots[:, :half],
         (((0, 2), (1, 2)), ((), ())),
         preferred_element_type=jnp.float32,
     ) + lax.dot_general(
-        far,
+        far[:, :block_rows],
         weight_slots[:, half:],
         (((0, 2), (1, 2)), ((), ())),
         preferred_element_type=jnp.float32,
     )
-    projected = projected.astype(jnp.bfloat16)[:block_rows]
+    projected = projected.astype(jnp.bfloat16)
     rider_rows = jnp.concatenate(
         [near[:, block_rows : block_rows + PARTS], far[:, block_rows : block_rows + PARTS]], axis=0
     )

time: 142 us -> 140 us (0.986)
  waiting for transfers between devices: 46.7 us -> 52 us
  other arithmetic: 9.89 us -> 6.69 us
  local copies, waits for them, and re-layouts: 20.6 us -> 17.9 us
    dynamic_slice x5 -> x0, local copies, waits for them, and re-layouts: 3.61 us -> none  [received_by(): return jnp.asarray(table)[position]]
    ppermute x1, waiting for transfers between devices: 28.9 us -> 32.5 us  [exclusive_scan(): from_odd = lax.ppermute(segment, axis, to_even)]
    dot_general x1, matrix products: 0.4 us -> 3.63 us  [local_body(): jnp.dot(chosen.astype(jnp.bfloat16), projected, preferred_element_type=jn...]
    select_n x5, other arithmetic: 3.33 us -> 0.12 us  [step(): return (arrived, jnp.where(chosen, merge(arrived), current))]
    dot_general x2 -> x1, matrix products: 6.16 us -> 3.02 us  [local_body(): lax.dot_general(far[:, :block_rows], weight_slots[:, half:], (((0, 2), (1...]
    unnamed x25 -> x19, local copies, waits for them, and re-layouts: 3.65 us -> 3.63 us
  transfers between devices with their start and end apart: 17 -> 17, of which waited for: 7 -> 6; matrix products, arithmetic and copies ran while one was open for 18% -> 12% of each run, Pallas kernels for 0% -> 0%
where the time goes in v7:
time: 140 us; the launch traced here: 139 us
  waiting for transfers between devices  52 us (37%)
  starting transfers between devices  51.4 us (37%)
  local copies, waits for them, and re-layouts  17.9 us (13%)
  matrix products  9.79 us (7%)
  other arithmetic  6.69 us (5%)
    ppermute x1, waiting for transfers between devices, exclusive_scan(): from_odd = lax.ppermute(segment, axis, to_even)  32.5 us
    ppermute x8, starting transfers between devices, shifted(): lax.ppermute(value, axis, [(i, (i + steps) % RING) for i in range(RING)])  26.4 us
    ppermute x1, starting transfers between devices, local_body(): far = lax.ppermute(near, 'core', [(0, 1), (1, 0)])  13 us
    all_to_all x1, waiting for transfers between devices, local_body(): lax.all_to_all(tile_rows, EP, split_axis=0, concat_axis=2, tiled=True)  9.21 us
    ppermute x8, waiting for transfers between devices, shifted(): lax.ppermute(value, axis, [(i, (i + steps) % RING) for i in range(RING)])  7.93 us
    ppermute x5, starting transfers between devices, step(): arrived = lax.ppermute(current, axis, pairs)  5.33 us
    all_to_all x1, starting transfers between devices, local_body(): lax.all_to_all(tile_rows, EP, split_axis=0, concat_axis=2, tiled=True)  4.67 us
    dot_general x1, matrix products, local_body(): jnp.dot(chosen.astype(jnp.bfloat16), projected, preferred_element_type=jn...  3.63 us
  transfers between devices with their start and end apart: 17, of which 6 were waited for; matrix products, arithmetic and copies ran while one was open for 12% of the time, Pallas kernels for 0%

profile of v7, /device:TPU:385, one launch (start us, length us, event | category | flops | bytes accessed | tf_op | source)
XLA Modules:
  0.0 139.1 jit_solution(5841469535641485164)
XLA Ops:
  0.0 0.7 reshape.306
  0.7 0.6 reduce-window.16
  1.4 0.2 slice_reduce_fusion.1
  1.5 0.2 reduce-window.19
  1.8 0.2 slice_reduce_fusion.2
  2.0 1.0 copy.119
  3.1 1.1 convolution_add_fusion
  4.2 2.7 %collective-permute-start = (f32[2,136,128]{2,1,0:T(8,128)S(1)}, f32[2,136,128]{2,1,0:T(8,128)S(1)}, u32[]{:S(2)}, u32[]{:S(2)}) collective-permute-start(f32[2,136,128]{2,1,0:T(8,128)S(1)} %pad_maximum_fusion.1), channel_id=1, source_target_pairs={{0,32},{64,96},{128,160},{192,224},{256,288},{320,352},{384,416},{... | collective-permute-start | bytes 417800 | tf_op jit(solution)/shard_map/ppermute | solution.py:73
  6.9 2.3 %collective-permute-done = f32[2,136,128]{2,1,0:T(8,128)S(1)} collective-permute-done((f32[2,136,128]{2,1,0:T(8,128)S(1)}, f32[2,136,128]{2,1,0:T(8,128)S(1)}, u32[]{:S(2)}, u32[]{:S(2)}) %collective-permute-start) | collective-permute-done | bytes 139296 | tf_op jit(solution)/shard_map/ppermute | solution.py:73
  9.4 0.7 collective-permute-start.1
  10.4 0.7 collective-permute-start.2
  11.1 0.4 fusion.11
  11.7 0.7 collective-permute-start.3
  12.7 0.7 collective-permute-start.4
  13.3 0.5 fusion.10
  14.1 0.7 collective-permute-start.5
  14.9 1.3 collective-permute-start.6
  16.3 32.5 %collective-permute-done.6 = f32[2,136,128]{2,1,0:T(8,128)S(1)} collective-permute-done((f32[2,136,128]{2,1,0:T(8,128)S(1)}, f32[2,136,128]{2,1,0:T(8,128)S(1)}, u32[]{:S(2)}, u32[]{:S(2)}) %collective-permute-start.6) | collective-permute-done | bytes 139296 | tf_op jit(solution)/shard_map/ppermute | solution.py:100
  48.8 0.5 multiply_reduce_fusion
  49.5 4.4 %collective-permute-start.7 = (bf16[1,264,256]{2,1,0:T(8,128)(2,1)S(1)}, bf16[1,264,256]{2,1,0:T(8,128)(2,1)S(1)}, u32[]{:S(2)}, u32[]{:S(2)}) collective-permute-start(bf16[1,264,256]{2,1,0:T(8,128)(2,1)S(1)} %maximum_bitcast_fusion), channel_id=1, source_target_pairs={{0,24},{8,0},{16,8},{24,16},{1,25},{9,1},{17,9},{25,17},{2,26},{10... | collective-permute-start | bytes 405512 | tf_op jit(solution)/shard_map/ppermute | solution.py:58
  53.9 1.9 %collective-permute-start.10 = (bf16[1,264,256]{2,1,0:T(8,128)(2,1)S(1)}, bf16[1,264,256]{2,1,0:T(8,128)(2,1)S(1)}, u32[]{:S(2)}, u32[]{:S(2)}) collective-permute-start(bf16[1,264,256]{2,1,0:T(8,128)(2,1)S(1)} %maximum_bitcast_fusion), channel_id=1, source_target_pairs={{0,8},{8,16},{16,24},{24,0},{1,9},{9,17},{17,25},{25,1},{2,10},{10... | collective-permute-start | bytes 405512 | tf_op jit(solution)/shard_map/ppermute | solution.py:58
  55.9 3.6 %collective-permute-start.8 = (bf16[1,264,128]{2,1,0:T(8,128)(2,1)S(1)}, bf16[1,264,128]{2,1,0:T(8,128)(2,1)S(1)}, u32[]{:S(2)}, u32[]{:S(2)}) collective-permute-start(bf16[1,264,128]{2,1,0:T(8,128)(2,1)S(1)} %get-tuple-element.26), channel_id=1, source_target_pairs={{0,16},{8,24},{16,0},{24,8},{1,17},{9,25},{17,1},{25,9},{2,18},{10... | collective-permute-start | bytes 202760 | tf_op jit(solution)/shard_map/ppermute | solution.py:58
  59.5 3.2 %collective-permute-start.9 = (bf16[1,264,128]{2,1,0:T(8,128)(2,1)S(1)}, bf16[1,264,128]{2,1,0:T(8,128)(2,1)S(1)}, u32[]{:S(2)}, u32[]{:S(2)}) collective-permute-start(bf16[1,264,128]{2,1,0:T(8,128)(2,1)S(1)} %get-tuple-element.25), channel_id=1, source_target_pairs={{0,16},{8,24},{16,0},{24,8},{1,17},{9,25},{17,1},{25,9},{2,18},{10... | collective-permute-start | bytes 202760 | tf_op jit(solution)/shard_map/ppermute | solution.py:58
  62.7 0.6 constant_dynamic-update-slice_fusion.6
  63.3 2.7 %collective-permute-done.9 = bf16[1,264,128]{2,1,0:T(8,128)(2,1)S(1)} collective-permute-done((bf16[1,264,128]{2,1,0:T(8,128)(2,1)S(1)}, bf16[1,264,128]{2,1,0:T(8,128)(2,1)S(1)}, u32[]{:S(2)}, u32[]{:S(2)}) %collective-permute-start.9) | collective-permute-done | bytes 67616 | tf_op jit(solution)/shard_map/ppermute | solution.py:58
  66.1 4.6 %collective-permute-start.11 = (bf16[4,264,256]{2,1,0:T(8,128)(2,1)S(1)}, bf16[4,264,256]{2,1,0:T(8,128)(2,1)S(1)}, u32[]{:S(2)}, u32[]{:S(2)}) collective-permute-start(bf16[4,264,256]{2,1,0:T(8,128)(2,1)S(1)} %pad_maximum_fusion), channel_id=1, source_target_pairs={{0,6},{2,0},{4,2},{6,4},{1,7},{3,1},{5,3},{7,5},{8,14},{10,8},{12,... | collective-permute-start | bytes 1622024 | tf_op jit(solution)/shard_map/ppermute | solution.py:58
  70.9 1.9 %collective-permute-start.14 = (bf16[4,264,256]{2,1,0:T(8,128)(2,1)S(1)}, bf16[4,264,256]{2,1,0:T(8,128)(2,1)S(1)}, u32[]{:S(2)}, u32[]{:S(2)}) collective-permute-start(bf16[4,264,256]{2,1,0:T(8,128)(2,1)S(1)} %pad_maximum_fusion), channel_id=1, source_target_pairs={{0,2},{2,4},{4,6},{6,0},{1,3},{3,5},{5,7},{7,1},{8,10},{10,12},{12... | collective-permute-start | bytes 1622024 | tf_op jit(solution)/shard_map/ppermute | solution.py:58
  72.8 3.5 %collective-permute-start.13 = (bf16[4,264,128]{2,1,0:T(8,128)(2,1)S(1)}, bf16[4,264,128]{2,1,0:T(8,128)(2,1)S(1)}, u32[]{:S(2)}, u32[]{:S(2)}) collective-permute-start(bf16[4,264,128]{2,1,0:T(8,128)(2,1)S(1)} %get-tuple-element.24), channel_id=1, source_target_pairs={{0,4},{2,6},{4,0},{6,2},{1,5},{3,7},{5,1},{7,3},{8,12},{10,14},{12... | collective-permute-start | bytes 811016 | tf_op jit(solution)/shard_map/ppermute | solution.py:58
  76.4 3.2 %collective-permute-start.12 = (bf16[4,264,128]{2,1,0:T(8,128)(2,1)S(1)}, bf16[4,264,128]{2,1,0:T(8,128)(2,1)S(1)}, u32[]{:S(2)}, u32[]{:S(2)}) collective-permute-start(bf16[4,264,128]{2,1,0:T(8,128)(2,1)S(1)} %get-tuple-element.23), channel_id=1, source_target_pairs={{0,4},{2,6},{4,0},{6,2},{1,5},{3,7},{5,1},{7,3},{8,12},{10,14},{12... | collective-permute-start | bytes 811016 | tf_op jit(solution)/shard_map/ppermute | solution.py:58
  79.6 0.7 constant_dynamic-update-slice_fusion.5
  80.3 0.6 constant_dynamic-update-slice_fusion.4
  80.9 0.7 constant_dynamic-update-slice_fusion.3
  81.6 0.7 constant_dynamic-update-slice_fusion.2
  82.2 0.8 constant_dynamic-update-slice_fusion.1
  83.1 1.1 collective-permute-done.13
  84.2 4.1 %collective-permute-done.12 = bf16[4,264,128]{2,1,0:T(8,128)(2,1)S(1)} collective-permute-done((bf16[4,264,128]{2,1,0:T(8,128)(2,1)S(1)}, bf16[4,264,128]{2,1,0:T(8,128)(2,1)S(1)}, u32[]{:S(2)}, u32[]{:S(2)}) %collective-permute-start.12) | collective-permute-done | bytes 270368 | tf_op jit(solution)/shard_map/ppermute | solution.py:58
  88.3 0.9 maximum_dynamic-update-slice_fusion
  89.2 0.8 constant_dynamic-update-slice_fusion
  90.0 13.0 %collective-permute-start.15 = (bf16[16,264,256]{2,1,0:T(8,128)(2,1)}, bf16[16,264,256]{2,1,0:T(8,128)(2,1)}, u32[]{:S(2)}, u32[]{:S(2)}) collective-permute-start(bf16[16,264,256]{2,1,0:T(8,128)(2,1)} %constant_dynamic-update-slice_fusion), channel_id=1, source_target_pairs={{0,1},{1,0},{2,3},{3,2},{4,5},{5,4},{6,7},{7,6},{8,9},{9,8},{10,11... | collective-permute-start | bytes 6488072 | tf_op jit(solution)/shard_map/ppermute | solution.py:172
  103.0 0.1 copy.101
  103.2 0.1 eq.138
  103.3 0.1 eq.142
  103.5 2.3 %copy.161 = bf16[24,32,8,256]{3,2,0,1:T(8,128)(2,1)S(1)} copy(bf16[24,32,8,256]{3,2,1,0:T(8,128)(2,1)} %bitcast.136) | data formatting | bytes 6291456 | tf_op jit(solution)/shard_map/reshape | solution.py:182
  106.0 1.2 reduce-window.14
  107.2 0.2 slice_reduce_fusion
  107.5 0.1 fusion.77
  107.6 0.1 reduce_sum.30
  107.9 0.2 copy.100
  108.1 0.2 and.85
  108.4 2.4 %gather_fusion = bf16[32,192,256]{2,1,0:T(8,128)(2,1)} fusion(bf16[192,32,256]{2,0,1:T(8,128)(2,1)S(1)} %bitcast.135, s32[1024]{0:T(1024)S(1)} %pad_clamp_fusion), kind=kCustom, calls=%fused_computation | custom fusion | bytes 6291584 | tf_op jit(solution)/shard_map/jit(_take)/gather | solution.py:181
  110.8 0.1 fusion.83
  110.9 0.9 slice.242
  111.8 3.0 %fusion.18 = f32[256,192]{0,1:T(8,128)S(1)} fusion(bf16[192,32,256]{2,0,1:T(8,128)(2,1)} %bitcast.137, bf16[16,264,256]{2,1,0:T(8,128)(2,1)} %collective-permute-done.15), kind=kOutput, calls=%fused_computation.20 | convolution fusion | flops 402653184 | bytes 3866624 | tf_op jit(solution)/shard_map/dot_general | solution.py:190
  114.8 3.6 %convolution_convert_fusion = bf16[1024,192]{0,1:T(8,128)(2,1)} fusion(f32[256,192]{0,1:T(8,128)S(1)} %fusion.18, bf16[192,32,256]{2,0,1:T(8,128)(2,1)S(1)} %bitcast.138, bf16[16,264,256]{2,1,0:T(8,128)(2,1)} %constant_dynamic-update-slice_fusion, s32[256]{0:T(256)S(1)} %bitcast.149, s32[256]{0:T(256)S(1)} %bitcast.148), kind=kOutput, calls=%fused_computation.8 | convolution fusion | flops 504397824 | bytes 4261888 | tf_op jit(solution)/shard_map/dot_general | solution.py:216
  118.5 2.0 %copy.114 = bf16[1024,192]{1,0:T(8,128)(2,1)} copy(bf16[1024,192]{0,1:T(8,128)(2,1)} %convolution_convert_fusion) | data formatting | bytes 786432 | tf_op jit(solution)/shard_map/convert_element_type | solution.py:218
  120.5 4.7 %all-to-all-start = ((bf16[32,32,192]{2,1,0:T(8,128)(2,1)}), bf16[32,32,192]{2,1,0:T(8,128)(2,1)S(1)}, u32[]{:S(2)}, u32[]{:S(2)}) async-start(bf16[32,32,192]{2,1,0:T(8,128)(2,1)} %bitcast.15), calls=%async_computation | async-start | bytes 1048576 | tf_op jit(solution)/shard_map/all_to_all | solution.py:220
  125.1 0.9 slice.243
  126.1 0.1 fusion.38
  126.2 0.6 multiply_reduce_fusion.1
  127.5 9.2 %all-to-all-done = bf16[32,32,192]{2,1,0:T(8,128)(2,1)S(1)} async-done(((bf16[32,32,192]{2,1,0:T(8,128)(2,1)}), bf16[32,32,192]{2,1,0:T(8,128)(2,1)S(1)}, u32[]{:S(2)}, u32[]{:S(2)}) %all-to-all-start) | async-done | bytes 393248 | tf_op jit(solution)/shard_map/all_to_all | solution.py:220
  136.7 0.3 copy.115
  137.0 0.5 all_to_all.16
  137.6 0.5 fusion.39
  138.1 1.0 fusion.42
  (81 shorter events, 2.6 us)
Async XLA Ops:
  0.0 11.1 %copy-start = (bf16[256,256]{1,0:T(8,128)(2,1)S(1)}, bf16[256,256]{1,0:T(8,128)(2,1)}, u32[]{:S(2)}) copy-start(bf16[256,256]{1,0:T(8,128)(2,1)} %param.8) | copy-start | bytes 393220
  0.0 11.1 %copy-start.2 = (bf16[256,256]{1,0:T(8,128)(2,1)S(1)}, bf16[256,256]{1,0:T(8,128)(2,1)}, u32[]{:S(2)}) copy-start(bf16[256,256]{1,0:T(8,128)(2,1)} %param.10) | copy-start | bytes 393220
  4.1 8.2 %copy-start.4 = (f32[192]{0:T(256)S(1)}, f32[192]{0:T(256)}, u32[]{:S(2)}) copy-start(f32[192]{0:T(256)} %param.15) | copy-start | bytes 2308
  4.2 5.0 %collective-permute-start = (f32[2,136,128]{2,1,0:T(8,128)S(1)}, f32[2,136,128]{2,1,0:T(8,128)S(1)}, u32[]{:S(2)}, u32[]{:S(2)}) collective-permute-start(f32[2,136,128]{2,1,0:T(8,128)S(1)} %pad_maximum_fusion.1), channel_id=1, source_target_pairs={{0,32},{64,96},{128,160},{192,224},{256,288},{320,352},{384,416},{... | collective-permute-start | bytes 417800 | tf_op jit(solution)/shard_map/ppermute | solution.py:73
  9.4 0.8 collective-permute-start.1
  10.4 1.2 collective-permute-start.2
  11.7 0.8 collective-permute-start.3
  12.7 1.4 collective-permute-start.4
  14.1 2.1 %collective-permute-start.5 = (f32[2,136,128]{2,1,0:T(8,128)S(1)}, f32[2,136,128]{2,1,0:T(8,128)S(1)}, u32[]{:S(2)}, u32[]{:S(2)}) collective-permute-start(f32[2,136,128]{2,1,0:T(8,128)S(1)} %maximum_select_fusion.4), channel_id=1, source_target_pairs={{32,96},{96,160},{160,224},{224,288},{288,352},{352,416},{416,480}... | collective-permute-start | bytes 417800 | tf_op jit(solution)/shard_map/ppermute | solution.py:101
  14.9 33.9 %collective-permute-start.6 = (f32[2,136,128]{2,1,0:T(8,128)S(1)}, f32[2,136,128]{2,1,0:T(8,128)S(1)}, u32[]{:S(2)}, u32[]{:S(2)}) collective-permute-start(f32[2,136,128]{2,1,0:T(8,128)S(1)} %maximum_select_fusion.4), channel_id=1, source_target_pairs={{32,64},{96,128},{160,192},{224,256},{288,320},{352,384},{416,448}... | collective-permute-start | bytes 417800 | tf_op jit(solution)/shard_map/ppermute | solution.py:100
  49.5 16.5 %collective-permute-start.7 = (bf16[1,264,256]{2,1,0:T(8,128)(2,1)S(1)}, bf16[1,264,256]{2,1,0:T(8,128)(2,1)S(1)}, u32[]{:S(2)}, u32[]{:S(2)}) collective-permute-start(bf16[1,264,256]{2,1,0:T(8,128)(2,1)S(1)} %maximum_bitcast_fusion), channel_id=1, source_target_pairs={{0,24},{8,0},{16,8},{24,16},{1,25},{9,1},{17,9},{25,17},{2,26},{10... | collective-permute-start | bytes 405512 | tf_op jit(solution)/shard_map/ppermute | solution.py:58
  53.9 12.1 %collective-permute-start.10 = (bf16[1,264,256]{2,1,0:T(8,128)(2,1)S(1)}, bf16[1,264,256]{2,1,0:T(8,128)(2,1)S(1)}, u32[]{:S(2)}, u32[]{:S(2)}) collective-permute-start(bf16[1,264,256]{2,1,0:T(8,128)(2,1)S(1)} %maximum_bitcast_fusion), channel_id=1, source_target_pairs={{0,8},{8,16},{16,24},{24,0},{1,9},{9,17},{17,25},{25,1},{2,10},{10... | collective-permute-start | bytes 405512 | tf_op jit(solution)/shard_map/ppermute | solution.py:58
  55.9 7.5 %collective-permute-start.8 = (bf16[1,264,128]{2,1,0:T(8,128)(2,1)S(1)}, bf16[1,264,128]{2,1,0:T(8,128)(2,1)S(1)}, u32[]{:S(2)}, u32[]{:S(2)}) collective-permute-start(bf16[1,264,128]{2,1,0:T(8,128)(2,1)S(1)} %get-tuple-element.26), channel_id=1, source_target_pairs={{0,16},{8,24},{16,0},{24,8},{1,17},{9,25},{17,1},{25,9},{2,18},{10... | collective-permute-start | bytes 202760 | tf_op jit(solution)/shard_map/ppermute | solution.py:58
  59.5 6.5 %collective-permute-start.9 = (bf16[1,264,128]{2,1,0:T(8,128)(2,1)S(1)}, bf16[1,264,128]{2,1,0:T(8,128)(2,1)S(1)}, u32[]{:S(2)}, u32[]{:S(2)}) collective-permute-start(bf16[1,264,128]{2,1,0:T(8,128)(2,1)S(1)} %get-tuple-element.25), channel_id=1, source_target_pairs={{0,16},{8,24},{16,0},{24,8},{1,17},{9,25},{17,1},{25,9},{2,18},{10... | collective-permute-start | bytes 202760 | tf_op jit(solution)/shard_map/ppermute | solution.py:58
  66.1 16.1 %collective-permute-start.11 = (bf16[4,264,256]{2,1,0:T(8,128)(2,1)S(1)}, bf16[4,264,256]{2,1,0:T(8,128)(2,1)S(1)}, u32[]{:S(2)}, u32[]{:S(2)}) collective-permute-start(bf16[4,264,256]{2,1,0:T(8,128)(2,1)S(1)} %pad_maximum_fusion), channel_id=1, source_target_pairs={{0,6},{2,0},{4,2},{6,4},{1,7},{3,1},{5,3},{7,5},{8,14},{10,8},{12,... | collective-permute-start | bytes 1622024 | tf_op jit(solution)/shard_map/ppermute | solution.py:58
  70.9 32.2 %copy-start.3 = (s32[256,2]{0,1:T(2,128)S(1)}, s32[256,2]{0,1:T(2,128)}, u32[]{:S(2)}) copy-start(s32[256,2]{0,1:T(2,128)} %param.13) | copy-start | bytes 6148
  70.9 18.3 %collective-permute-start.14 = (bf16[4,264,256]{2,1,0:T(8,128)(2,1)S(1)}, bf16[4,264,256]{2,1,0:T(8,128)(2,1)S(1)}, u32[]{:S(2)}, u32[]{:S(2)}) collective-permute-start(bf16[4,264,256]{2,1,0:T(8,128)(2,1)S(1)} %pad_maximum_fusion), channel_id=1, source_target_pairs={{0,2},{2,4},{4,6},{6,0},{1,3},{3,5},{5,7},{7,1},{8,10},{10,12},{12... | collective-permute-start | bytes 1622024 | tf_op jit(solution)/shard_map/ppermute | solution.py:58
  72.8 11.4 %collective-permute-start.13 = (bf16[4,264,128]{2,1,0:T(8,128)(2,1)S(1)}, bf16[4,264,128]{2,1,0:T(8,128)(2,1)S(1)}, u32[]{:S(2)}, u32[]{:S(2)}) collective-permute-start(bf16[4,264,128]{2,1,0:T(8,128)(2,1)S(1)} %get-tuple-element.24), channel_id=1, source_target_pairs={{0,4},{2,6},{4,0},{6,2},{1,5},{3,7},{5,1},{7,3},{8,12},{10,14},{12... | collective-permute-start | bytes 811016 | tf_op jit(solution)/shard_map/ppermute | solution.py:58
  76.4 11.9 %collective-permute-start.12 = (bf16[4,264,128]{2,1,0:T(8,128)(2,1)S(1)}, bf16[4,264,128]{2,1,0:T(8,128)(2,1)S(1)}, u32[]{:S(2)}, u32[]{:S(2)}) collective-permute-start(bf16[4,264,128]{2,1,0:T(8,128)(2,1)S(1)} %get-tuple-element.23), channel_id=1, source_target_pairs={{0,4},{2,6},{4,0},{6,2},{1,5},{3,7},{5,1},{7,3},{8,12},{10,14},{12... | collective-permute-start | bytes 811016 | tf_op jit(solution)/shard_map/ppermute | solution.py:58
  90.0 21.8 %collective-permute-start.15 = (bf16[16,264,256]{2,1,0:T(8,128)(2,1)}, bf16[16,264,256]{2,1,0:T(8,128)(2,1)}, u32[]{:S(2)}, u32[]{:S(2)}) collective-permute-start(bf16[16,264,256]{2,1,0:T(8,128)(2,1)} %constant_dynamic-update-slice_fusion), channel_id=1, source_target_pairs={{0,1},{1,0},{2,3},{3,2},{4,5},{5,4},{6,7},{7,6},{8,9},{9,8},{10,11... | collective-permute-start | bytes 6488072 | tf_op jit(solution)/shard_map/ppermute | solution.py:172
  103.5 4.3 %copy-start.5 = (s32[64]{0:T(128)S(1)}, s32[64]{0:T(128)}, u32[]{:S(2)}) copy-start(s32[64]{0:T(128)} %param.14) | copy-start | bytes 772
  111.8 3.0 %copy-start.1 = (bf16[32,192,256]{2,1,0:T(8,128)(2,1)S(1)}, bf16[32,192,256]{2,1,0:T(8,128)(2,1)}, u32[]{:S(2)}) copy-start(bf16[32,192,256]{2,1,0:T(8,128)(2,1)} %gather_fusion) | copy-start | bytes 9437188
  120.5 16.3 %all-to-all-start = ((bf16[32,32,192]{2,1,0:T(8,128)(2,1)}), bf16[32,32,192]{2,1,0:T(8,128)(2,1)S(1)}, u32[]{:S(2)}, u32[]{:S(2)}) async-start(bf16[32,32,192]{2,1,0:T(8,128)(2,1)} %bitcast.15), calls=%async_computation | async-start | bytes 1048576 | tf_op jit(solution)/shard_map/all_to_all | solution.py:220

commit v8 on v7

--- a/solution.py
+++ b/solution.py
@@ -169,34 +169,45 @@
     block = jnp.concatenate([attended, riders], axis=0)
     near = ring_gathered(block[None], "x")
     near = ring_gathered(near, "y")
-    far = lax.ppermute(near, "core", [(0, 1), (1, 0)])
+
+    core_index = lax.axis_index("core")
+    chips = RING * RING
+    own_weight = out_weight.reshape(model_cols, chips, 2, local_width)
+    partner_all = lax.ppermute(out_weight, "core", [(0, 1), (1, 0)])
+    partner_weight = lax.dynamic_index_in_dim(
+        partner_all.reshape(own_weight.shape), core_index, axis=2, keepdims=False
+    )
 
     offsets = jnp.arange(RING, dtype=jnp.int32)
     origin_x = (lax.axis_index("x") + offsets) % RING
     origin_y = (lax.axis_index("y") + offsets) % RING
-    near_origin = ((origin_x[None, :] * RING + origin_y[:, None]) * 2).reshape(-1)
-    core_index = lax.axis_index("core")
+    chip_origin = (origin_x[None, :] * RING + origin_y[:, None]).reshape(-1)
+    mine = lax.dynamic_index_in_dim(own_weight, core_index, axis=2, keepdims=False)
+    both = jnp.concatenate([mine, partner_weight], axis=0)
+    weight_slots = jnp.take(both, chip_origin, axis=1, mode="clip")
+    partial = lax.dot_general(
+        near,
+        weight_slots,
+        (((0, 2), (1, 2)), ((), ())),
+        preferred_element_type=jnp.float32,
+    )
+    own_riders = near[:, block_rows : block_rows + PARTS]
+    outgoing = jnp.concatenate(
+        [
+            partial[:block_rows, model_cols:],
+            own_riders.astype(jnp.float32).reshape(-1, model_cols),
+        ],
+        axis=0,
+    )
+    incoming_partial = lax.ppermute(outgoing, "core", [(0, 1), (1, 0)])
+    projected = (partial[:block_rows, :model_cols] + incoming_partial[:block_rows]).astype(
+        jnp.bfloat16
+    )
+    partner_riders = incoming_partial[block_rows:].reshape(own_riders.shape).astype(jnp.bfloat16)
+    near_origin = chip_origin * 2
     origin = jnp.concatenate([near_origin + core_index, near_origin + (1 - core_index)])
     slots = origin.shape[0]
-    weight_slots = jnp.take(
-        out_weight.reshape(model_cols, slots, local_width), origin, axis=1, mode="clip"
-    )
-    half = near.shape[0]
-    projected = lax.dot_general(
-        near[:, :block_rows],
-        weight_slots[:, :half],
-        (((0, 2), (1, 2)), ((), ())),
-        preferred_element_type=jnp.float32,
-    ) + lax.dot_general(
-        far[:, :block_rows],
-        weight_slots[:, half:],
-        (((0, 2), (1, 2)), ((), ())),
-        preferred_element_type=jnp.float32,
-    )
-    projected = projected.astype(jnp.bfloat16)
-    rider_rows = jnp.concatenate(
-        [near[:, block_rows : block_rows + PARTS], far[:, block_rows : block_rows + PARTS]], axis=0
-    )
+    rider_rows = jnp.concatenate([own_riders, partner_riders], axis=0)
     reorder = (origin[None, :] == jnp.arange(slots, dtype=jnp.int32)[:, None]).astype(jnp.bfloat16)
     ordered = jnp.einsum("os,spk->pok", reorder, rider_rows, preferred_element_type=jnp.float32)
     direction_full = joined_parts(ordered.astype(jnp.bfloat16), local_width, model_cols)

time: 140 us -> 181 us (1.29)
  local copies, waits for them, and re-layouts: 17.9 us -> 41.9 us
  other arithmetic: 6.69 us -> 20.2 us
  waiting for transfers between devices: 52 us -> 54 us
    dynamic_slice x0 -> x2, local copies, waits for them, and re-layouts: none -> 9.38 us  [the longest x1 5.73 us: local_body(): lax.dynamic_index_in_dim(own_weight, core_index, axis=2, keepdims=False)]
    reshape x1 -> x3, local copies, waits for them, and re-layouts: 2.27 us -> 9.6 us  [the longest x1 4.75 us: local_body(): partner_all.reshape(own_weight.shape)]
    ppermute x8, waiting for transfers between devices: 7.93 us -> 13.7 us  [shifted(): lax.ppermute(value, axis, [(i, (i + steps) % RING) for i in range(RING)])]
    another operation x5, other arithmetic: 2 us -> 5.96 us
    ppermute x1, waiting for transfers between devices: 32.5 us -> 28.9 us  [exclusive_scan(): from_odd = lax.ppermute(segment, axis, to_even)]
    squeeze x0 -> x1, local copies, waits for them, and re-layouts: none -> 3.39 us  [local_body(): lax.dynamic_index_in_dim(partner_all.reshape(own_weight.shape), core_inde...]
    dot_general x1, matrix products: 3.63 us -> 0.42 us  [local_body(): jnp.dot(chosen.astype(jnp.bfloat16), projected, preferred_element_type=jn...]
    eq x2, local copies, waits for them, and re-layouts: 0.28 us -> 3.25 us  [local_body(): flat_ids[:, None] == jnp.arange(experts_all, dtype=jnp.int32)[None, :]]
  transfers between devices with their start and end apart: 17 -> 18, of which waited for: 6 -> 7; matrix products, arithmetic and copies ran while one was open for 12% -> 24% of each run, Pallas kernels for 0% -> 0%
where the time goes in v8:
time: 181 us; the launch traced here: 180 us
  waiting for transfers between devices  54 us (30%)
  starting transfers between devices  52.5 us (29%)
  local copies, waits for them, and re-layouts  41.9 us (23%)
  other arithmetic  20.2 us (11%)
  matrix products  10.1 us (6%)
    ppermute x1, waiting for transfers between devices, exclusive_scan(): from_odd = lax.ppermute(segment, axis, to_even)  28.9 us
    ppermute x8, starting transfers between devices, shifted(): lax.ppermute(value, axis, [(i, (i + steps) % RING) for i in range(RING)])  26.8 us
    ppermute x8, waiting for transfers between devices, shifted(): lax.ppermute(value, axis, [(i, (i + steps) % RING) for i in range(RING)])  13.7 us
    ppermute x1, starting transfers between devices, local_body(): incoming_partial = lax.ppermute(outgoing, 'core', [(0, 1), (1, 0)])  11.6 us
    all_to_all x1, waiting for transfers between devices, local_body(): lax.all_to_all(tile_rows, EP, split_axis=0, concat_axis=2, tiled=True)  10.2 us
    another operation x5, other arithmetic  5.96 us
    dynamic_slice x1, local copies, waits for them, and re-layouts, local_body(): lax.dynamic_index_in_dim(own_weight, core_index, axis=2, keepdims=False)  5.73 us
    ppermute x5, starting transfers between devices, step(): arrived = lax.ppermute(current, axis, pairs)  5.31 us
  transfers between devices with their start and end apart: 18, of which 7 were waited for; matrix products, arithmetic and copies ran while one was open for 24% of the time, Pallas kernels for 0%

profile of v8, /device:TPU:385, one launch (start us, length us, event | category | flops | bytes accessed | tf_op | source)
XLA Modules:
  0.0 180.0 jit_solution(17921289389481509654)
XLA Ops:
  0.0 0.7 reshape.340
  0.7 0.6 reduce-window.16
  1.9 0.6 subtract_exponential_fusion
  3.1 1.0 copy.123
  4.2 1.1 convolution_add_fusion
  5.4 0.7 pad_maximum_fusion.3
  6.0 2.6 %collective-permute-start = (f32[2,136,128]{2,1,0:T(8,128)}, f32[2,136,128]{2,1,0:T(8,128)S(1)}, u32[]{:S(2)}, u32[]{:S(2)}) collective-permute-start(f32[2,136,128]{2,1,0:T(8,128)} %pad_maximum_fusion.3), channel_id=1, source_target_pairs={{0,32},{64,96},{128,160},{192,224},{256,288},{320,352},{384,416},{... | collective-permute-start | bytes 417800 | tf_op jit(solution)/shard_map/ppermute | solution.py:73
  8.7 2.9 %collective-permute-start.15 = (bf16[192,8192]{1,0:T(8,128)(2,1)}, bf16[192,8192]{1,0:T(8,128)(2,1)}, u32[]{:S(2)}, u32[]{:S(2)}) collective-permute-start(bf16[192,8192]{1,0:T(8,128)(2,1)} %param.12), channel_id=1, source_target_pairs={{0,1},{1,0},{2,3},{3,2},{4,5},{5,4},{6,7},{7,6},{8,9},{9,8},{10,11... | collective-permute-start | bytes 9437192 | tf_op jit(solution)/shard_map/ppermute | solution.py:176
  11.6 0.6 iota_compare_fusion.3
  12.2 4.8 %reshape.343 = bf16[192,16,2,256]{3,2,1,0:T(2,128)(2,1)S(1)} reshape(bf16[192,8192]{1,0:T(8,128)(2,1)} %param.12) | data formatting | bytes 6291456 | tf_op jit(solution)/shard_map/reshape | solution.py:175
  17.0 1.5 copy.102
  18.4 1.6 eq.142
  20.1 1.6 eq.138
  21.7 0.6 and_select_fusion
  22.3 1.3 fusion.58
  23.6 3.2 %reduce-window.14 = s32[32,4,128]{2,0,1:T(8,128)} reduce-window(s32[32,4,128]{2,0,1:T(8,128)} %fusion.58, s32[]{:T(128)} %constant.149.clone.1), window={size=1x1x128 pad=0_0x0_0x127_0}, to_apply=%region_1.2 | reduce-window | flops 2080768 | bytes 131076 | tf_op jit(solution)/shard_map/reduce-window
  26.8 1.7 slice_reduce_fusion
  28.5 1.3 reduce-window.15
  29.7 0.7 slice.153
  30.4 1.5 fusion.54
  32.0 1.5 reduce_sum.30
  33.4 1.6 copy.105
  35.0 1.3 multiply_add_fusion.1
  36.3 0.7 broadcast_subtract_fusion
  36.9 0.6 fusion.57
  37.5 2.1 %fusion.10 = f32[256,2,128]{0,2,1:T(8,128)} fusion(bf16[256,2,128]{0,2,1:T(8,128)(2,1)} %bitcast.135, f32[2,256]{1,0:T(2,128)} %bitcast.140, pred[256,256]{1,0:T(8,128)(4,1)} %iota_compare_fusion.3, bf16[256,256]{1,0:T(8,128)(2,1)} %param.10, bf16[256,256]{1,0:T(8,128)(2,1)S(1)} %copy-done), kind=kOutput, calls=%fused_computation.16 | convolution fusion | flops 67764224 | bytes 722944 | tf_op jit(solution)/shard_map/while/body/eval_jaxpr/hts,shd->thd/dot_general | solution.py:31
  39.6 5.7 %constant_dynamic-slice_fusion.1 = bf16[192,16,1,256]{3,2,1,0:T(2,128)(2,1)} fusion(bf16[192,16,2,256]{3,2,1,0:T(2,128)(2,1)S(1)} %reshape.343, s32[]{:T(128)S(6)} %select_n.148), kind=kLoop, calls=%fused_computation.178 | loop fusion | bytes 3145732 | tf_op jit(solution)/shard_map/jit(dynamic_index_in_dim)/dynamic_slice | solution.py:185
  45.4 0.8 multiply_add_fusion.3
  46.1 0.7 compare_and_fusion
  46.8 0.7 slice_add_fusion.12
  47.5 0.8 multiply_add_fusion
  48.3 0.7 collective-permute-start.1
  48.9 0.7 reduce-precision_convert_fusion.1
  49.9 0.7 collective-permute-start.2
  50.5 1.4 fusion.9
  52.6 0.7 collective-permute-start.3
  53.7 0.7 collective-permute-start.4
  54.7 0.7 collective-permute-start.5
  55.7 1.3 collective-permute-start.6
  57.1 28.9 %collective-permute-done.6 = f32[2,136,128]{2,1,0:T(8,128)S(1)} collective-permute-done((f32[2,136,128]{2,1,0:T(8,128)S(1)}, f32[2,136,128]{2,1,0:T(8,128)S(1)}, u32[]{:S(2)}, u32[]{:S(2)}) %collective-permute-start.6) | collective-permute-done | bytes 139296 | tf_op jit(solution)/shard_map/ppermute | solution.py:100
  86.7 3.1 %collective-permute-start.10 = (bf16[1,264,256]{2,1,0:T(8,128)(2,1)S(1)}, bf16[1,264,256]{2,1,0:T(8,128)(2,1)S(1)}, u32[]{:S(2)}, u32[]{:S(2)}) collective-permute-start(bf16[1,264,256]{2,1,0:T(8,128)(2,1)S(1)} %maximum_bitcast_fusion), channel_id=1, source_target_pairs={{0,8},{8,16},{16,24},{24,0},{1,9},{9,17},{17,25},{25,1},{2,10},{10... | collective-permute-start | bytes 405512 | tf_op jit(solution)/shard_map/ppermute | solution.py:58
  89.9 3.4 %collective-permute-start.7 = (bf16[1,264,256]{2,1,0:T(8,128)(2,1)S(1)}, bf16[1,264,256]{2,1,0:T(8,128)(2,1)S(1)}, u32[]{:S(2)}, u32[]{:S(2)}) collective-permute-start(bf16[1,264,256]{2,1,0:T(8,128)(2,1)S(1)} %maximum_bitcast_fusion), channel_id=1, source_target_pairs={{0,24},{8,0},{16,8},{24,16},{1,25},{9,1},{17,9},{25,17},{2,26},{10... | collective-permute-start | bytes 405512 | tf_op jit(solution)/shard_map/ppermute | solution.py:58
  93.3 3.4 %collective-permute-start.8 = (bf16[1,264,128]{2,1,0:T(8,128)(2,1)S(1)}, bf16[1,264,128]{2,1,0:T(8,128)(2,1)S(1)}, u32[]{:S(2)}, u32[]{:S(2)}) collective-permute-start(bf16[1,264,128]{2,1,0:T(8,128)(2,1)S(1)} %get-tuple-element.38), channel_id=1, source_target_pairs={{0,16},{8,24},{16,0},{24,8},{1,17},{9,25},{17,1},{25,9},{2,18},{10... | collective-permute-start | bytes 202760 | tf_op jit(solution)/shard_map/ppermute | solution.py:58
  96.7 3.3 %collective-permute-start.9 = (bf16[1,264,128]{2,1,0:T(8,128)(2,1)S(1)}, bf16[1,264,128]{2,1,0:T(8,128)(2,1)S(1)}, u32[]{:S(2)}, u32[]{:S(2)}) collective-permute-start(bf16[1,264,128]{2,1,0:T(8,128)(2,1)S(1)} %get-tuple-element.36), channel_id=1, source_target_pairs={{0,16},{8,24},{16,0},{24,8},{1,17},{9,25},{17,1},{25,9},{2,18},{10... | collective-permute-start | bytes 202760 | tf_op jit(solution)/shard_map/ppermute | solution.py:58
  100.5 2.8 %collective-permute-done.9 = bf16[1,264,128]{2,1,0:T(8,128)(2,1)S(1)} collective-permute-done((bf16[1,264,128]{2,1,0:T(8,128)(2,1)S(1)}, bf16[1,264,128]{2,1,0:T(8,128)(2,1)S(1)}, u32[]{:S(2)}, u32[]{:S(2)}) %collective-permute-start.9) | collective-permute-done | bytes 67616 | tf_op jit(solution)/shard_map/ppermute | solution.py:58
  103.3 4.6 %collective-permute-start.11 = (bf16[4,264,256]{2,1,0:T(8,128)(2,1)S(1)}, bf16[4,264,256]{2,1,0:T(8,128)(2,1)S(1)}, u32[]{:S(2)}, u32[]{:S(2)}) collective-permute-start(bf16[4,264,256]{2,1,0:T(8,128)(2,1)S(1)} %pad_maximum_fusion.1), channel_id=1, source_target_pairs={{0,6},{2,0},{4,2},{6,4},{1,7},{3,1},{5,3},{7,5},{8,14},{10,8},{12,... | collective-permute-start | bytes 1622024 | tf_op jit(solution)/shard_map/ppermute | solution.py:58
  108.1 1.9 %collective-permute-start.14 = (bf16[4,264,256]{2,1,0:T(8,128)(2,1)S(1)}, bf16[4,264,256]{2,1,0:T(8,128)(2,1)S(1)}, u32[]{:S(2)}, u32[]{:S(2)}) collective-permute-start(bf16[4,264,256]{2,1,0:T(8,128)(2,1)S(1)} %pad_maximum_fusion.1), channel_id=1, source_target_pairs={{0,2},{2,4},{4,6},{6,0},{1,3},{3,5},{5,7},{7,1},{8,10},{10,12},{12... | collective-permute-start | bytes 1622024 | tf_op jit(solution)/shard_map/ppermute | solution.py:58
  110.0 3.5 %collective-permute-start.12 = (bf16[4,264,128]{2,1,0:T(8,128)(2,1)S(1)}, bf16[4,264,128]{2,1,0:T(8,128)(2,1)S(1)}, u32[]{:S(2)}, u32[]{:S(2)}) collective-permute-start(bf16[4,264,128]{2,1,0:T(8,128)(2,1)S(1)} %get-tuple-element.25), channel_id=1, source_target_pairs={{0,4},{2,6},{4,0},{6,2},{1,5},{3,7},{5,1},{7,3},{8,12},{10,14},{12... | collective-permute-start | bytes 811016 | tf_op jit(solution)/shard_map/ppermute | solution.py:58
  113.5 3.4 %collective-permute-start.13 = (bf16[4,264,128]{2,1,0:T(8,128)(2,1)S(1)}, bf16[4,264,128]{2,1,0:T(8,128)(2,1)S(1)}, u32[]{:S(2)}, u32[]{:S(2)}) collective-permute-start(bf16[4,264,128]{2,1,0:T(8,128)(2,1)S(1)} %get-tuple-element.26), channel_id=1, source_target_pairs={{0,4},{2,6},{4,0},{6,2},{1,5},{3,7},{5,1},{7,3},{8,12},{10,14},{12... | collective-permute-start | bytes 811016 | tf_op jit(solution)/shard_map/ppermute | solution.py:58
  117.1 4.8 %collective-permute-done.12 = bf16[4,264,128]{2,1,0:T(8,128)(2,1)S(1)} collective-permute-done((bf16[4,264,128]{2,1,0:T(8,128)(2,1)S(1)}, bf16[4,264,128]{2,1,0:T(8,128)(2,1)S(1)}, u32[]{:S(2)}, u32[]{:S(2)}) %collective-permute-start.12) | collective-permute-done | bytes 270368 | tf_op jit(solution)/shard_map/ppermute | solution.py:58
  121.9 5.8 %collective-permute-done.13 = bf16[4,264,128]{2,1,0:T(8,128)(2,1)S(1)} collective-permute-done((bf16[4,264,128]{2,1,0:T(8,128)(2,1)S(1)}, bf16[4,264,128]{2,1,0:T(8,128)(2,1)S(1)}, u32[]{:S(2)}, u32[]{:S(2)}) %collective-permute-start.13) | collective-permute-done | bytes 270368 | tf_op jit(solution)/shard_map/ppermute | solution.py:58
  127.9 1.2 copy-done.5
  129.2 4.8 %reshape.344 = bf16[192,16,2,256]{3,2,1,0:T(2,128)(2,1)S(1)} reshape(bf16[192,8192]{1,0:T(8,128)(2,1)} %collective-permute-done.15) | data formatting | bytes 6291456 | tf_op jit(solution)/shard_map/reshape | solution.py:178
  133.9 3.7 %constant_dynamic-slice_fusion = bf16[192,16,1,256]{3,2,1,0:T(2,128)(2,1)S(1)} fusion(bf16[192,16,2,256]{3,2,1,0:T(2,128)(2,1)S(1)} %reshape.344, s32[]{:T(128)S(6)} %select_n.148), kind=kLoop, calls=%fused_computation.177 | loop fusion | bytes 3145732 | tf_op jit(solution)/shard_map/jit(dynamic_index_in_dim)/dynamic_slice | solution.py:177
  137.6 3.4 %copy_bitcast_fusion = (bf16[192,16,256]{2,0,1:T(8,128)(2,1)S(1)}, bf16[192,16,256]{2,0,1:T(8,128)(2,1)S(1)}) fusion(bf16[192,16,1,256]{3,2,1,0:T(2,128)(2,1)S(1)} %constant_dynamic-slice_fusion, bf16[192,16,1,256]{3,2,1,0:T(2,128)(2,1)S(1)} %copy-done.1), kind=kLoop, calls=%fused_computation.4 | loop fusion | bytes 6291456 | tf_op jit(solution)/shard_map/jit(dynamic_index_in_dim)/squeeze | solution.py:177
  141.2 2.4 %gather_fusion = bf16[16,384,256]{2,1,0:T(8,128)(2,1)} fusion(bf16[384,16,256]{2,0,1:T(8,128)(2,1)S(1)} %pad_maximum_fusion, s32[1024]{0:T(1024)S(1)} %pad_clamp_fusion), kind=kCustom, calls=%fused_computation | custom fusion | bytes 6291520 | tf_op jit(solution)/shard_map/jit(_take)/gather | solution.py:187
  143.6 3.8 %fusion.3 = f32[264,384]{1,0:T(8,128)S(1)} fusion(bf16[16,264,256]{2,1,0:T(8,128)(2,1)} %copy-done.5, bf16[16,384,256]{2,1,0:T(8,128)(2,1)} %gather_fusion), kind=kOutput, calls=%fused_computation.9 | convolution fusion | flops 830472192 | bytes 5713920 | tf_op jit(solution)/shard_map/dot_general | solution.py:188
  147.6 11.6 %collective-permute-start.16 = (f32[320,192]{1,0:T(8,128)S(1)}, f32[320,192]{1,0:T(8,128)S(1)}, u32[]{:S(2)}, u32[]{:S(2)}) collective-permute-start(f32[320,192]{1,0:T(8,128)S(1)} %pad_maximum_fusion.2), channel_id=1, source_target_pairs={{0,1},{1,0},{2,3},{3,2},{4,5},{5,4},{6,7},{7,6},{8,9},{9,8},{10,11... | collective-permute-start | bytes 737288 | tf_op jit(solution)/shard_map/ppermute | solution.py:202
  159.3 1.2 collective-permute-done.16
  161.0 1.0 copy.116
  162.0 3.9 %all-to-all-start = ((bf16[32,32,192]{2,1,0:T(8,128)(2,1)}), bf16[32,32,192]{2,1,0:T(8,128)(2,1)S(1)}, u32[]{:S(2)}, u32[]{:S(2)}) async-start(bf16[32,32,192]{2,1,0:T(8,128)(2,1)} %bitcast.16), calls=%async_computation | async-start | bytes 1048576 | tf_op jit(solution)/shard_map/all_to_all | solution.py:231
  166.1 0.6 multiply_reduce_fusion.1
  167.5 10.2 %all-to-all-done = bf16[32,32,192]{2,1,0:T(8,128)(2,1)S(1)} async-done(((bf16[32,32,192]{2,1,0:T(8,128)(2,1)}), bf16[32,32,192]{2,1,0:T(8,128)(2,1)S(1)}, u32[]{:S(2)}, u32[]{:S(2)}) %all-to-all-start) | async-done | bytes 393248 | tf_op jit(solution)/shard_map/all_to_all | solution.py:231
  179.0 1.0 fusion.17
  (99 shorter events, 7.3 us)
Async XLA Ops:
  0.0 37.5 %copy-start = (bf16[256,256]{1,0:T(8,128)(2,1)S(1)}, bf16[256,256]{1,0:T(8,128)(2,1)}, u32[]{:S(2)}) copy-start(bf16[256,256]{1,0:T(8,128)(2,1)} %param.8) | copy-start | bytes 393220
  1.8 0.8 copy-start.8
  1.9 3.4 %copy-start.7 = (f32[2]{0:T(128)}, f32[2]{0:T(128)S(1)}, u32[]{:S(2)}) copy-start(f32[2]{0:T(128)S(1)} %slice_reduce_fusion.2) | copy-start | bytes 28
  4.2 1.2 copy-start.2
  6.0 40.8 %collective-permute-start = (f32[2,136,128]{2,1,0:T(8,128)}, f32[2,136,128]{2,1,0:T(8,128)S(1)}, u32[]{:S(2)}, u32[]{:S(2)}) collective-permute-start(f32[2,136,128]{2,1,0:T(8,128)} %pad_maximum_fusion.3), channel_id=1, source_target_pairs={{0,32},{64,96},{128,160},{192,224},{256,288},{320,352},{384,416},{... | collective-permute-start | bytes 417800 | tf_op jit(solution)/shard_map/ppermute | solution.py:73
  8.7 120.5 %collective-permute-start.15 = (bf16[192,8192]{1,0:T(8,128)(2,1)}, bf16[192,8192]{1,0:T(8,128)(2,1)}, u32[]{:S(2)}, u32[]{:S(2)}) collective-permute-start(bf16[192,8192]{1,0:T(8,128)(2,1)} %param.12), channel_id=1, source_target_pairs={{0,1},{1,0},{2,3},{3,2},{4,5},{5,4},{6,7},{7,6},{8,9},{9,8},{10,11... | collective-permute-start | bytes 9437192 | tf_op jit(solution)/shard_map/ppermute | solution.py:176
  45.4 7.9 %copy-start.4 = (s32[512]{0:T(512)S(1)}, s32[512]{0:T(512)}, u32[]{:S(2)}) copy-start(s32[512]{0:T(512)} %fusion.54) | copy-start | bytes 6148
  48.3 1.5 collective-permute-start.1
  49.8 36.2 %copy-start.3 = (f32[256,2]{0,1:T(2,128)S(1)}, f32[256,2]{0,1:T(2,128)}, u32[]{:S(2)}) copy-start(f32[256,2]{0,1:T(2,128)} %get-tuple-element.41) | copy-start | bytes 6148
  49.9 2.6 %collective-permute-start.2 = (f32[2,136,128]{2,1,0:T(8,128)S(1)}, f32[2,136,128]{2,1,0:T(8,128)S(1)}, u32[]{:S(2)}, u32[]{:S(2)}) collective-permute-start(f32[2,136,128]{2,1,0:T(8,128)S(1)} %maximum_select_fusion.1), channel_id=1, source_target_pairs={{96,224},{352,480},{97,225},{353,481},{98,226},{354,482},{99,227},... | collective-permute-start | bytes 417800 | tf_op jit(solution)/shard_map/ppermute | solution.py:73
  52.6 1.0 collective-permute-start.3
  53.7 0.9 collective-permute-start.4
  54.7 2.3 %collective-permute-start.5 = (f32[2,136,128]{2,1,0:T(8,128)S(1)}, f32[2,136,128]{2,1,0:T(8,128)S(1)}, u32[]{:S(2)}, u32[]{:S(2)}) collective-permute-start(f32[2,136,128]{2,1,0:T(8,128)S(1)} %maximum_select_fusion.4), channel_id=1, source_target_pairs={{32,96},{96,160},{160,224},{224,288},{288,352},{352,416},{416,480}... | collective-permute-start | bytes 417800 | tf_op jit(solution)/shard_map/ppermute | solution.py:101
  55.7 30.3 %collective-permute-start.6 = (f32[2,136,128]{2,1,0:T(8,128)S(1)}, f32[2,136,128]{2,1,0:T(8,128)S(1)}, u32[]{:S(2)}, u32[]{:S(2)}) collective-permute-start(f32[2,136,128]{2,1,0:T(8,128)S(1)} %maximum_select_fusion.4), channel_id=1, source_target_pairs={{32,64},{96,128},{160,192},{224,256},{288,320},{352,384},{416,448}... | collective-permute-start | bytes 417800 | tf_op jit(solution)/shard_map/ppermute | solution.py:100
  86.7 16.5 %collective-permute-start.10 = (bf16[1,264,256]{2,1,0:T(8,128)(2,1)S(1)}, bf16[1,264,256]{2,1,0:T(8,128)(2,1)S(1)}, u32[]{:S(2)}, u32[]{:S(2)}) collective-permute-start(bf16[1,264,256]{2,1,0:T(8,128)(2,1)S(1)} %maximum_bitcast_fusion), channel_id=1, source_target_pairs={{0,8},{8,16},{16,24},{24,0},{1,9},{9,17},{17,25},{25,1},{2,10},{10... | collective-permute-start | bytes 405512 | tf_op jit(solution)/shard_map/ppermute | solution.py:58
  89.9 13.4 %collective-permute-start.7 = (bf16[1,264,256]{2,1,0:T(8,128)(2,1)S(1)}, bf16[1,264,256]{2,1,0:T(8,128)(2,1)S(1)}, u32[]{:S(2)}, u32[]{:S(2)}) collective-permute-start(bf16[1,264,256]{2,1,0:T(8,128)(2,1)S(1)} %maximum_bitcast_fusion), channel_id=1, source_target_pairs={{0,24},{8,0},{16,8},{24,16},{1,25},{9,1},{17,9},{25,17},{2,26},{10... | collective-permute-start | bytes 405512 | tf_op jit(solution)/shard_map/ppermute | solution.py:58
  93.3 7.2 %collective-permute-start.8 = (bf16[1,264,128]{2,1,0:T(8,128)(2,1)S(1)}, bf16[1,264,128]{2,1,0:T(8,128)(2,1)S(1)}, u32[]{:S(2)}, u32[]{:S(2)}) collective-permute-start(bf16[1,264,128]{2,1,0:T(8,128)(2,1)S(1)} %get-tuple-element.38), channel_id=1, source_target_pairs={{0,16},{8,24},{16,0},{24,8},{1,17},{9,25},{17,1},{25,9},{2,18},{10... | collective-permute-start | bytes 202760 | tf_op jit(solution)/shard_map/ppermute | solution.py:58
  96.7 6.5 %collective-permute-start.9 = (bf16[1,264,128]{2,1,0:T(8,128)(2,1)S(1)}, bf16[1,264,128]{2,1,0:T(8,128)(2,1)S(1)}, u32[]{:S(2)}, u32[]{:S(2)}) collective-permute-start(bf16[1,264,128]{2,1,0:T(8,128)(2,1)S(1)} %get-tuple-element.36), channel_id=1, source_target_pairs={{0,16},{8,24},{16,0},{24,8},{1,17},{9,25},{17,1},{25,9},{2,18},{10... | collective-permute-start | bytes 202760 | tf_op jit(solution)/shard_map/ppermute | solution.py:58
  103.3 13.8 %collective-permute-start.11 = (bf16[4,264,256]{2,1,0:T(8,128)(2,1)S(1)}, bf16[4,264,256]{2,1,0:T(8,128)(2,1)S(1)}, u32[]{:S(2)}, u32[]{:S(2)}) collective-permute-start(bf16[4,264,256]{2,1,0:T(8,128)(2,1)S(1)} %pad_maximum_fusion.1), channel_id=1, source_target_pairs={{0,6},{2,0},{4,2},{6,4},{1,7},{3,1},{5,3},{7,5},{8,14},{10,8},{12,... | collective-permute-start | bytes 1622024 | tf_op jit(solution)/shard_map/ppermute | solution.py:58
  108.1 19.7 %collective-permute-start.14 = (bf16[4,264,256]{2,1,0:T(8,128)(2,1)S(1)}, bf16[4,264,256]{2,1,0:T(8,128)(2,1)S(1)}, u32[]{:S(2)}, u32[]{:S(2)}) collective-permute-start(bf16[4,264,256]{2,1,0:T(8,128)(2,1)S(1)} %pad_maximum_fusion.1), channel_id=1, source_target_pairs={{0,2},{2,4},{4,6},{6,0},{1,3},{3,5},{5,7},{7,1},{8,10},{10,12},{12... | collective-permute-start | bytes 1622024 | tf_op jit(solution)/shard_map/ppermute | solution.py:58
  110.0 11.9 %collective-permute-start.12 = (bf16[4,264,128]{2,1,0:T(8,128)(2,1)S(1)}, bf16[4,264,128]{2,1,0:T(8,128)(2,1)S(1)}, u32[]{:S(2)}, u32[]{:S(2)}) collective-permute-start(bf16[4,264,128]{2,1,0:T(8,128)(2,1)S(1)} %get-tuple-element.25), channel_id=1, source_target_pairs={{0,4},{2,6},{4,0},{6,2},{1,5},{3,7},{5,1},{7,3},{8,12},{10,14},{12... | collective-permute-start | bytes 811016 | tf_op jit(solution)/shard_map/ppermute | solution.py:58
  113.5 14.1 %collective-permute-start.13 = (bf16[4,264,128]{2,1,0:T(8,128)(2,1)S(1)}, bf16[4,264,128]{2,1,0:T(8,128)(2,1)S(1)}, u32[]{:S(2)}, u32[]{:S(2)}) collective-permute-start(bf16[4,264,128]{2,1,0:T(8,128)(2,1)S(1)} %get-tuple-element.26), channel_id=1, source_target_pairs={{0,4},{2,6},{4,0},{6,2},{1,5},{3,7},{5,1},{7,3},{8,12},{10,14},{12... | collective-permute-start | bytes 811016 | tf_op jit(solution)/shard_map/ppermute | solution.py:58
  127.8 1.4 copy-start.5
  133.9 3.7 %copy-start.1 = (bf16[192,16,1,256]{3,2,1,0:T(2,128)(2,1)S(1)}, bf16[192,16,1,256]{3,2,1,0:T(2,128)(2,1)}, u32[]{:S(2)}) copy-start(bf16[192,16,1,256]{3,2,1,0:T(2,128)(2,1)} %constant_dynamic-slice_fusion.1) | copy-start | bytes 4718596
  143.6 15.7 %copy-start.6 = (s32[256,2]{0,1:T(2,128)S(1)}, s32[256,2]{0,1:T(2,128)}, u32[]{:S(2)}) copy-start(s32[256,2]{0,1:T(2,128)} %multiply_add_fusion.1) | copy-start | bytes 6148
  147.6 12.8 %collective-permute-start.16 = (f32[320,192]{1,0:T(8,128)S(1)}, f32[320,192]{1,0:T(8,128)S(1)}, u32[]{:S(2)}, u32[]{:S(2)}) collective-permute-start(f32[320,192]{1,0:T(8,128)S(1)} %pad_maximum_fusion.2), channel_id=1, source_target_pairs={{0,1},{1,0},{2,3},{3,2},{4,5},{5,4},{6,7},{7,6},{8,9},{9,8},{10,11... | collective-permute-start | bytes 737288 | tf_op jit(solution)/shard_map/ppermute | solution.py:202
  162.0 15.6 %all-to-all-start = ((bf16[32,32,192]{2,1,0:T(8,128)(2,1)}), bf16[32,32,192]{2,1,0:T(8,128)(2,1)S(1)}, u32[]{:S(2)}, u32[]{:S(2)}) async-start(bf16[32,32,192]{2,1,0:T(8,128)(2,1)} %bitcast.16), calls=%async_computation | async-start | bytes 1048576 | tf_op jit(solution)/shard_map/all_to_all | solution.py:231

commit v9 on v7

--- a/solution.py
+++ b/solution.py
@@ -57,10 +57,16 @@
     def shifted(value, steps):
         return lax.ppermute(value, axis, [(i, (i + steps) % RING) for i in range(RING)])
 
-    half = blocks.shape[-1] // 2
     from_right = shifted(blocks, -1)
     from_left = shifted(blocks, 1)
-    far = jnp.concatenate([shifted(blocks[..., :half], 2), shifted(blocks[..., half:], -2)], axis=-1)
+    if blocks.shape[0] % 2 == 0:
+        half = blocks.shape[0] // 2
+        far = jnp.concatenate([shifted(blocks[:half], 2), shifted(blocks[half:], -2)], axis=0)
+    else:
+        half = blocks.shape[-1] // 2
+        far = jnp.concatenate(
+            [shifted(blocks[..., :half], 2), shifted(blocks[..., half:], -2)], axis=-1
+        )
     return jnp.concatenate([blocks, from_right, far, from_left], axis=0)
 
 
@@ -183,17 +189,17 @@
     )
     half = near.shape[0]
     projected = lax.dot_general(
-        near[:, :block_rows],
+        near,
         weight_slots[:, :half],
         (((0, 2), (1, 2)), ((), ())),
         preferred_element_type=jnp.float32,
     ) + lax.dot_general(
-        far[:, :block_rows],
+        far,
         weight_slots[:, half:],
         (((0, 2), (1, 2)), ((), ())),
         preferred_element_type=jnp.float32,
     )
-    projected = projected.astype(jnp.bfloat16)
+    projected = projected.astype(jnp.bfloat16)[:block_rows]
     rider_rows = jnp.concatenate(
         [near[:, block_rows : block_rows + PARTS], far[:, block_rows : block_rows + PARTS]], axis=0
     )

time: 140 us -> 140 us (level)
    dot_general x1, matrix products: 3.63 us -> 0.4 us  [local_body(): jnp.dot(chosen.astype(jnp.bfloat16), projected, preferred_element_type=jn...]
    dot_general x1 -> x2, matrix products: 3.02 us -> 6.15 us  [the longest x1 3.37 us: local_body(): lax.dot_general(near, weight_slots[:, :half], (((0, 2), (1, 2)), ((), ())...]
    unnamed x19 -> x20, local copies, waits for them, and re-layouts: 3.63 us -> 4.45 us
  transfers between devices with their start and end apart: 17 -> 17, of which waited for: 6 -> 6; matrix products, arithmetic and copies ran while one was open for 12% -> 15% of each run, Pallas kernels for 0% -> 0%
where the time goes in v9:
time: 140 us; the launch traced here: 139 us
  starting transfers between devices  52.1 us (37%)
  waiting for transfers between devices  51.7 us (37%)
  local copies, waits for them, and re-layouts  18.4 us (13%)
  matrix products  9.68 us (7%)
  other arithmetic  5.85 us (4%)
    ppermute x1, waiting for transfers between devices, exclusive_scan(): from_odd = lax.ppermute(segment, axis, to_even)  32.4 us
    ppermute x8, starting transfers between devices, shifted(): lax.ppermute(value, axis, [(i, (i + steps) % RING) for i in range(RING)])  26.4 us
    ppermute x1, starting transfers between devices, local_body(): far = lax.ppermute(near, 'core', [(0, 1), (1, 0)])  13.1 us
    all_to_all x1, waiting for transfers between devices, local_body(): lax.all_to_all(tile_rows, EP, split_axis=0, concat_axis=2, tiled=True)  9.21 us
    ppermute x8, waiting for transfers between devices, shifted(): lax.ppermute(value, axis, [(i, (i + steps) % RING) for i in range(RING)])  7.77 us
    ppermute x5, starting transfers between devices, step(): arrived = lax.ppermute(current, axis, pairs)  5.33 us
    all_to_all x1, starting transfers between devices, local_body(): lax.all_to_all(tile_rows, EP, split_axis=0, concat_axis=2, tiled=True)  5.29 us
    unnamed x20, local copies, waits for them, and re-layouts  4.45 us
  transfers between devices with their start and end apart: 17, of which 6 were waited for; matrix products, arithmetic and copies ran while one was open for 15% of the time, Pallas kernels for 0%

profile of v9, /device:TPU:385, one launch (start us, length us, event | category | flops | bytes accessed | tf_op | source)
XLA Modules:
  0.0 139.1 jit_solution(5286056529640706866)
XLA Ops:
  0.0 0.7 reshape.306
  0.7 0.6 reduce-window.16
  1.4 0.2 slice_reduce_fusion.1
  1.5 0.2 reduce-window.19
  1.8 0.2 slice_reduce_fusion.2
  2.0 1.0 copy.120
  3.1 1.1 convolution_add_fusion
  4.2 2.7 %collective-permute-start = (f32[2,136,128]{2,1,0:T(8,128)S(1)}, f32[2,136,128]{2,1,0:T(8,128)S(1)}, u32[]{:S(2)}, u32[]{:S(2)}) collective-permute-start(f32[2,136,128]{2,1,0:T(8,128)S(1)} %pad_maximum_fusion.3), channel_id=1, source_target_pairs={{0,32},{64,96},{128,160},{192,224},{256,288},{320,352},{384,416},{... | collective-permute-start | bytes 417800 | tf_op jit(solution)/shard_map/ppermute | solution.py:79
  6.9 2.3 %collective-permute-done = f32[2,136,128]{2,1,0:T(8,128)S(1)} collective-permute-done((f32[2,136,128]{2,1,0:T(8,128)S(1)}, f32[2,136,128]{2,1,0:T(8,128)S(1)}, u32[]{:S(2)}, u32[]{:S(2)}) %collective-permute-start) | collective-permute-done | bytes 139296 | tf_op jit(solution)/shard_map/ppermute | solution.py:79
  9.4 0.7 collective-permute-start.1
  10.4 0.7 collective-permute-start.2
  11.1 0.4 fusion.15
  11.7 0.7 collective-permute-start.3
  12.7 0.7 collective-permute-start.4
  13.3 0.5 fusion.14
  14.1 0.7 collective-permute-start.5
  14.9 0.1 copy.102
  15.0 0.1 eq.142
  15.3 1.3 collective-permute-start.6
  16.7 32.4 %collective-permute-done.6 = f32[2,136,128]{2,1,0:T(8,128)S(1)} collective-permute-done((f32[2,136,128]{2,1,0:T(8,128)S(1)}, f32[2,136,128]{2,1,0:T(8,128)S(1)}, u32[]{:S(2)}, u32[]{:S(2)}) %collective-permute-start.6) | collective-permute-done | bytes 139296 | tf_op jit(solution)/shard_map/ppermute | solution.py:106
  49.1 0.5 multiply_reduce_fusion
  49.8 4.4 %collective-permute-start.7 = (bf16[1,264,256]{2,1,0:T(8,128)(2,1)S(1)}, bf16[1,264,256]{2,1,0:T(8,128)(2,1)S(1)}, u32[]{:S(2)}, u32[]{:S(2)}) collective-permute-start(bf16[1,264,256]{2,1,0:T(8,128)(2,1)S(1)} %maximum_bitcast_fusion), channel_id=1, source_target_pairs={{0,24},{8,0},{16,8},{24,16},{1,25},{9,1},{17,9},{25,17},{2,26},{10... | collective-permute-start | bytes 405512 | tf_op jit(solution)/shard_map/ppermute | solution.py:58
  54.2 1.9 %collective-permute-start.10 = (bf16[1,264,256]{2,1,0:T(8,128)(2,1)S(1)}, bf16[1,264,256]{2,1,0:T(8,128)(2,1)S(1)}, u32[]{:S(2)}, u32[]{:S(2)}) collective-permute-start(bf16[1,264,256]{2,1,0:T(8,128)(2,1)S(1)} %maximum_bitcast_fusion), channel_id=1, source_target_pairs={{0,8},{8,16},{16,24},{24,0},{1,9},{9,17},{17,25},{25,1},{2,10},{10... | collective-permute-start | bytes 405512 | tf_op jit(solution)/shard_map/ppermute | solution.py:58
  56.1 3.6 %collective-permute-start.8 = (bf16[1,264,128]{2,1,0:T(8,128)(2,1)S(1)}, bf16[1,264,128]{2,1,0:T(8,128)(2,1)S(1)}, u32[]{:S(2)}, u32[]{:S(2)}) collective-permute-start(bf16[1,264,128]{2,1,0:T(8,128)(2,1)S(1)} %get-tuple-element.24), channel_id=1, source_target_pairs={{0,16},{8,24},{16,0},{24,8},{1,17},{9,25},{17,1},{25,9},{2,18},{10... | collective-permute-start | bytes 202760 | tf_op jit(solution)/shard_map/ppermute | solution.py:58
  59.8 3.2 %collective-permute-start.9 = (bf16[1,264,128]{2,1,0:T(8,128)(2,1)S(1)}, bf16[1,264,128]{2,1,0:T(8,128)(2,1)S(1)}, u32[]{:S(2)}, u32[]{:S(2)}) collective-permute-start(bf16[1,264,128]{2,1,0:T(8,128)(2,1)S(1)} %get-tuple-element.23), channel_id=1, source_target_pairs={{0,16},{8,24},{16,0},{24,8},{1,17},{9,25},{17,1},{25,9},{2,18},{10... | collective-permute-start | bytes 202760 | tf_op jit(solution)/shard_map/ppermute | solution.py:58
  63.0 0.6 constant_dynamic-update-slice_fusion.10
  63.6 0.7 constant_dynamic-update-slice_fusion.9
  64.3 0.7 constant_dynamic-update-slice_fusion.1
  64.9 1.4 collective-permute-done.9
  66.3 0.7 constant_dynamic-update-slice_fusion
  67.1 4.6 %collective-permute-start.11 = (bf16[4,264,256]{2,1,0:T(8,128)(2,1)S(1)}, bf16[4,264,256]{2,1,0:T(8,128)(2,1)S(1)}, u32[]{:S(2)}, u32[]{:S(2)}) collective-permute-start(bf16[4,264,256]{2,1,0:T(8,128)(2,1)S(1)} %pad_maximum_fusion), channel_id=1, source_target_pairs={{0,6},{2,0},{4,2},{6,4},{1,7},{3,1},{5,3},{7,5},{8,14},{10,8},{12,... | collective-permute-start | bytes 1622024 | tf_op jit(solution)/shard_map/ppermute | solution.py:58
  71.7 1.2 reduce-window.14
  72.9 1.9 %collective-permute-start.14 = (bf16[4,264,256]{2,1,0:T(8,128)(2,1)S(1)}, bf16[4,264,256]{2,1,0:T(8,128)(2,1)S(1)}, u32[]{:S(2)}, u32[]{:S(2)}) collective-permute-start(bf16[4,264,256]{2,1,0:T(8,128)(2,1)S(1)} %pad_maximum_fusion), channel_id=1, source_target_pairs={{0,2},{2,4},{4,6},{6,0},{1,3},{3,5},{5,7},{7,1},{8,10},{10,12},{12... | collective-permute-start | bytes 1622024 | tf_op jit(solution)/shard_map/ppermute | solution.py:58
  74.9 3.5 %collective-permute-start.12 = (bf16[2,264,256]{2,1,0:T(8,128)(2,1)S(1)}, bf16[2,264,256]{2,1,0:T(8,128)(2,1)S(1)}, u32[]{:S(2)}, u32[]{:S(2)}) collective-permute-start(bf16[2,264,256]{2,1,0:T(8,128)(2,1)S(1)} %pad_maximum_fusion.1), channel_id=1, source_target_pairs={{0,4},{2,6},{4,0},{6,2},{1,5},{3,7},{5,1},{7,3},{8,12},{10,14},{12... | collective-permute-start | bytes 811016 | tf_op jit(solution)/shard_map/ppermute | solution.py:58
  78.4 3.2 %collective-permute-start.13 = (bf16[2,264,256]{2,1,0:T(8,128)(2,1)S(1)}, bf16[2,264,256]{2,1,0:T(8,128)(2,1)S(1)}, u32[]{:S(2)}, u32[]{:S(2)}) collective-permute-start(bf16[2,264,256]{2,1,0:T(8,128)(2,1)S(1)} %pad_maximum_fusion.2), channel_id=1, source_target_pairs={{0,4},{2,6},{4,0},{6,2},{1,5},{3,7},{5,1},{7,3},{8,12},{10,14},{12... | collective-permute-start | bytes 811016 | tf_op jit(solution)/shard_map/ppermute | solution.py:58
  81.7 0.7 constant_dynamic-update-slice_fusion.6
  82.4 0.8 constant_dynamic-update-slice_fusion.5
  83.2 3.0 %collective-permute-done.12 = bf16[2,264,256]{2,1,0:T(8,128)(2,1)S(1)} collective-permute-done((bf16[2,264,256]{2,1,0:T(8,128)(2,1)S(1)}, bf16[2,264,256]{2,1,0:T(8,128)(2,1)S(1)}, u32[]{:S(2)}, u32[]{:S(2)}) %collective-permute-start.12) | collective-permute-done | bytes 270368 | tf_op jit(solution)/shard_map/ppermute | solution.py:58
  86.2 0.7 constant_dynamic-update-slice_fusion.4
  86.9 3.4 %collective-permute-done.13 = bf16[2,264,256]{2,1,0:T(8,128)(2,1)S(1)} collective-permute-done((bf16[2,264,256]{2,1,0:T(8,128)(2,1)S(1)}, bf16[2,264,256]{2,1,0:T(8,128)(2,1)S(1)}, u32[]{:S(2)}, u32[]{:S(2)}) %collective-permute-start.13) | collective-permute-done | bytes 270368 | tf_op jit(solution)/shard_map/ppermute | solution.py:58
  90.3 0.7 constant_dynamic-update-slice_fusion.3
  91.0 0.8 constant_dynamic-update-slice_fusion.2
  91.9 13.1 %collective-permute-start.15 = (bf16[16,264,256]{2,1,0:T(8,128)(2,1)}, bf16[16,264,256]{2,1,0:T(8,128)(2,1)}, u32[]{:S(2)}, u32[]{:S(2)}) collective-permute-start(bf16[16,264,256]{2,1,0:T(8,128)(2,1)} %constant_dynamic-update-slice_fusion.2), channel_id=1, source_target_pairs={{0,1},{1,0},{2,3},{3,2},{4,5},{5,4},{6,7},{7,6},{8,9},{9,8},{10,11... | collective-permute-start | bytes 6488072 | tf_op jit(solution)/shard_map/ppermute | solution.py:178
  105.0 0.2 slice_reduce_fusion
  105.2 0.1 eq.138
  105.5 0.1 reduce_sum.30
  105.8 2.3 %copy.162 = bf16[24,32,8,256]{3,2,0,1:T(8,128)(2,1)S(1)} copy(bf16[24,32,8,256]{3,2,1,0:T(8,128)(2,1)} %bitcast.132) | data formatting | bytes 6291456 | tf_op jit(solution)/shard_map/reshape | solution.py:188
  108.4 0.2 copy.101
  108.6 0.2 and.85
  108.9 2.4 %gather_fusion = bf16[32,192,256]{2,1,0:T(8,128)(2,1)} fusion(bf16[192,32,256]{2,0,1:T(8,128)(2,1)S(1)} %bitcast.131, s32[1024]{0:T(1024)S(1)} %pad_clamp_fusion), kind=kCustom, calls=%fused_computation | custom fusion | bytes 6291584 | tf_op jit(solution)/shard_map/jit(_take)/gather | solution.py:187
  111.4 0.9 slice.232
  112.3 3.4 %fusion.6 = f32[264,192]{0,1:T(8,128)S(1)} fusion(bf16[16,264,256]{2,1,0:T(8,128)(2,1)} %constant_dynamic-update-slice_fusion.2, bf16[192,32,256]{2,0,1:T(8,128)(2,1)} %bitcast.133), kind=kOutput, calls=%fused_computation.10 | convolution fusion | flops 415236096 | bytes 3938304 | tf_op jit(solution)/shard_map/dot_general | solution.py:191
  115.7 2.8 %fusion.9 = f32[264,192]{0,1:T(8,128)S(1)} fusion(bf16[16,264,256]{2,1,0:T(8,128)(2,1)} %collective-permute-done.15, bf16[192,32,256]{2,0,1:T(8,128)(2,1)S(1)} %bitcast.134), kind=kOutput, calls=%fused_computation.11 | convolution fusion | flops 415236096 | bytes 3938304 | tf_op jit(solution)/shard_map/dot_general | solution.py:196
  118.5 0.4 convolution_convert_fusion
  118.9 1.0 copy.115
  119.9 5.3 %all-to-all-start = ((bf16[32,32,192]{2,1,0:T(8,128)(2,1)}), bf16[32,32,192]{2,1,0:T(8,128)(2,1)S(1)}, u32[]{:S(2)}, u32[]{:S(2)}) async-start(bf16[32,32,192]{2,1,0:T(8,128)(2,1)} %bitcast.15), calls=%async_computation | async-start | bytes 1048576 | tf_op jit(solution)/shard_map/all_to_all | solution.py:226
  125.2 0.9 slice.233
  126.1 0.1 fusion.18
  126.2 0.6 multiply_reduce_fusion.1
  127.6 9.2 %all-to-all-done = bf16[32,32,192]{2,1,0:T(8,128)(2,1)S(1)} async-done(((bf16[32,32,192]{2,1,0:T(8,128)(2,1)}), bf16[32,32,192]{2,1,0:T(8,128)(2,1)S(1)}, u32[]{:S(2)}, u32[]{:S(2)}) %all-to-all-start) | async-done | bytes 393248 | tf_op jit(solution)/shard_map/all_to_all | solution.py:226
  136.8 0.3 copy.116
  137.1 0.6 all_to_all.16
  137.6 0.5 fusion.19
  138.1 1.0 fusion.22
  (84 shorter events, 2.8 us)
Async XLA Ops:
  0.0 11.1 %copy-start = (bf16[256,256]{1,0:T(8,128)(2,1)S(1)}, bf16[256,256]{1,0:T(8,128)(2,1)}, u32[]{:S(2)}) copy-start(bf16[256,256]{1,0:T(8,128)(2,1)} %param.8) | copy-start | bytes 393220
  0.0 11.1 %copy-start.2 = (bf16[256,256]{1,0:T(8,128)(2,1)S(1)}, bf16[256,256]{1,0:T(8,128)(2,1)}, u32[]{:S(2)}) copy-start(bf16[256,256]{1,0:T(8,128)(2,1)} %param.10) | copy-start | bytes 393220
  4.1 8.3 %copy-start.4 = (f32[192]{0:T(256)S(1)}, f32[192]{0:T(256)}, u32[]{:S(2)}) copy-start(f32[192]{0:T(256)} %param.15) | copy-start | bytes 2308
  4.2 5.0 %collective-permute-start = (f32[2,136,128]{2,1,0:T(8,128)S(1)}, f32[2,136,128]{2,1,0:T(8,128)S(1)}, u32[]{:S(2)}, u32[]{:S(2)}) collective-permute-start(f32[2,136,128]{2,1,0:T(8,128)S(1)} %pad_maximum_fusion.3), channel_id=1, source_target_pairs={{0,32},{64,96},{128,160},{192,224},{256,288},{320,352},{384,416},{... | collective-permute-start | bytes 417800 | tf_op jit(solution)/shard_map/ppermute | solution.py:79
  9.4 0.8 collective-permute-start.1
  10.4 4.5 %copy-start.3 = (s32[256,2]{0,1:T(2,128)S(1)}, s32[256,2]{0,1:T(2,128)}, u32[]{:S(2)}) copy-start(s32[256,2]{0,1:T(2,128)} %param.13) | copy-start | bytes 6148
  10.4 1.2 collective-permute-start.2
  11.7 0.8 collective-permute-start.3
  12.7 1.4 collective-permute-start.4
  14.1 2.4 %collective-permute-start.5 = (f32[2,136,128]{2,1,0:T(8,128)S(1)}, f32[2,136,128]{2,1,0:T(8,128)S(1)}, u32[]{:S(2)}, u32[]{:S(2)}) collective-permute-start(f32[2,136,128]{2,1,0:T(8,128)S(1)} %maximum_select_fusion.4), channel_id=1, source_target_pairs={{32,96},{96,160},{160,224},{224,288},{288,352},{352,416},{416,480}... | collective-permute-start | bytes 417800 | tf_op jit(solution)/shard_map/ppermute | solution.py:107
  15.3 33.8 %collective-permute-start.6 = (f32[2,136,128]{2,1,0:T(8,128)S(1)}, f32[2,136,128]{2,1,0:T(8,128)S(1)}, u32[]{:S(2)}, u32[]{:S(2)}) collective-permute-start(f32[2,136,128]{2,1,0:T(8,128)S(1)} %maximum_select_fusion.4), channel_id=1, source_target_pairs={{32,64},{96,128},{160,192},{224,256},{288,320},{352,384},{416,448}... | collective-permute-start | bytes 417800 | tf_op jit(solution)/shard_map/ppermute | solution.py:106
  49.8 13.8 %collective-permute-start.7 = (bf16[1,264,256]{2,1,0:T(8,128)(2,1)S(1)}, bf16[1,264,256]{2,1,0:T(8,128)(2,1)S(1)}, u32[]{:S(2)}, u32[]{:S(2)}) collective-permute-start(bf16[1,264,256]{2,1,0:T(8,128)(2,1)S(1)} %maximum_bitcast_fusion), channel_id=1, source_target_pairs={{0,24},{8,0},{16,8},{24,16},{1,25},{9,1},{17,9},{25,17},{2,26},{10... | collective-permute-start | bytes 405512 | tf_op jit(solution)/shard_map/ppermute | solution.py:58
  54.2 12.8 %collective-permute-start.10 = (bf16[1,264,256]{2,1,0:T(8,128)(2,1)S(1)}, bf16[1,264,256]{2,1,0:T(8,128)(2,1)S(1)}, u32[]{:S(2)}, u32[]{:S(2)}) collective-permute-start(bf16[1,264,256]{2,1,0:T(8,128)(2,1)S(1)} %maximum_bitcast_fusion), channel_id=1, source_target_pairs={{0,8},{8,16},{16,24},{24,0},{1,9},{9,17},{17,25},{25,1},{2,10},{10... | collective-permute-start | bytes 405512 | tf_op jit(solution)/shard_map/ppermute | solution.py:58
  56.1 8.1 %collective-permute-start.8 = (bf16[1,264,128]{2,1,0:T(8,128)(2,1)S(1)}, bf16[1,264,128]{2,1,0:T(8,128)(2,1)S(1)}, u32[]{:S(2)}, u32[]{:S(2)}) collective-permute-start(bf16[1,264,128]{2,1,0:T(8,128)(2,1)S(1)} %get-tuple-element.24), channel_id=1, source_target_pairs={{0,16},{8,24},{16,0},{24,8},{1,17},{9,25},{17,1},{25,9},{2,18},{10... | collective-permute-start | bytes 202760 | tf_op jit(solution)/shard_map/ppermute | solution.py:58
  59.8 6.5 %collective-permute-start.9 = (bf16[1,264,128]{2,1,0:T(8,128)(2,1)S(1)}, bf16[1,264,128]{2,1,0:T(8,128)(2,1)S(1)}, u32[]{:S(2)}, u32[]{:S(2)}) collective-permute-start(bf16[1,264,128]{2,1,0:T(8,128)(2,1)S(1)} %get-tuple-element.23), channel_id=1, source_target_pairs={{0,16},{8,24},{16,0},{24,8},{1,17},{9,25},{17,1},{25,9},{2,18},{10... | collective-permute-start | bytes 202760 | tf_op jit(solution)/shard_map/ppermute | solution.py:58
  67.1 15.3 %collective-permute-start.11 = (bf16[4,264,256]{2,1,0:T(8,128)(2,1)S(1)}, bf16[4,264,256]{2,1,0:T(8,128)(2,1)S(1)}, u32[]{:S(2)}, u32[]{:S(2)}) collective-permute-start(bf16[4,264,256]{2,1,0:T(8,128)(2,1)S(1)} %pad_maximum_fusion), channel_id=1, source_target_pairs={{0,6},{2,0},{4,2},{6,4},{1,7},{3,1},{5,3},{7,5},{8,14},{10,8},{12,... | collective-permute-start | bytes 1622024 | tf_op jit(solution)/shard_map/ppermute | solution.py:58
  72.9 18.1 %collective-permute-start.14 = (bf16[4,264,256]{2,1,0:T(8,128)(2,1)S(1)}, bf16[4,264,256]{2,1,0:T(8,128)(2,1)S(1)}, u32[]{:S(2)}, u32[]{:S(2)}) collective-permute-start(bf16[4,264,256]{2,1,0:T(8,128)(2,1)S(1)} %pad_maximum_fusion), channel_id=1, source_target_pairs={{0,2},{2,4},{4,6},{6,0},{1,3},{3,5},{5,7},{7,1},{8,10},{10,12},{12... | collective-permute-start | bytes 1622024 | tf_op jit(solution)/shard_map/ppermute | solution.py:58
  74.9 11.3 %collective-permute-start.12 = (bf16[2,264,256]{2,1,0:T(8,128)(2,1)S(1)}, bf16[2,264,256]{2,1,0:T(8,128)(2,1)S(1)}, u32[]{:S(2)}, u32[]{:S(2)}) collective-permute-start(bf16[2,264,256]{2,1,0:T(8,128)(2,1)S(1)} %pad_maximum_fusion.1), channel_id=1, source_target_pairs={{0,4},{2,6},{4,0},{6,2},{1,5},{3,7},{5,1},{7,3},{8,12},{10,14},{12... | collective-permute-start | bytes 811016 | tf_op jit(solution)/shard_map/ppermute | solution.py:58
  78.4 11.9 %collective-permute-start.13 = (bf16[2,264,256]{2,1,0:T(8,128)(2,1)S(1)}, bf16[2,264,256]{2,1,0:T(8,128)(2,1)S(1)}, u32[]{:S(2)}, u32[]{:S(2)}) collective-permute-start(bf16[2,264,256]{2,1,0:T(8,128)(2,1)S(1)} %pad_maximum_fusion.2), channel_id=1, source_target_pairs={{0,4},{2,6},{4,0},{6,2},{1,5},{3,7},{5,1},{7,3},{8,12},{10,14},{12... | collective-permute-start | bytes 811016 | tf_op jit(solution)/shard_map/ppermute | solution.py:58
  91.9 23.8 %collective-permute-start.15 = (bf16[16,264,256]{2,1,0:T(8,128)(2,1)}, bf16[16,264,256]{2,1,0:T(8,128)(2,1)}, u32[]{:S(2)}, u32[]{:S(2)}) collective-permute-start(bf16[16,264,256]{2,1,0:T(8,128)(2,1)} %constant_dynamic-update-slice_fusion.2), channel_id=1, source_target_pairs={{0,1},{1,0},{2,3},{3,2},{4,5},{5,4},{6,7},{7,6},{8,9},{9,8},{10,11... | collective-permute-start | bytes 6488072 | tf_op jit(solution)/shard_map/ppermute | solution.py:178
  105.8 2.6 %copy-start.5 = (s32[64]{0:T(128)S(1)}, s32[64]{0:T(128)}, u32[]{:S(2)}) copy-start(s32[64]{0:T(128)} %param.14) | copy-start | bytes 772
  112.3 3.4 %copy-start.1 = (bf16[32,192,256]{2,1,0:T(8,128)(2,1)S(1)}, bf16[32,192,256]{2,1,0:T(8,128)(2,1)}, u32[]{:S(2)}) copy-start(bf16[32,192,256]{2,1,0:T(8,128)(2,1)} %gather_fusion) | copy-start | bytes 9437188
  119.9 16.9 %all-to-all-start = ((bf16[32,32,192]{2,1,0:T(8,128)(2,1)}), bf16[32,32,192]{2,1,0:T(8,128)(2,1)S(1)}, u32[]{:S(2)}, u32[]{:S(2)}) async-start(bf16[32,32,192]{2,1,0:T(8,128)(2,1)} %bitcast.15), calls=%async_computation | async-start | bytes 1048576 | tf_op jit(solution)/shard_map/all_to_all | solution.py:226

commit v10 on v7

--- a/solution.py
+++ b/solution.py
@@ -183,17 +183,17 @@
     )
     half = near.shape[0]
     projected = lax.dot_general(
-        near[:, :block_rows],
+        near,
         weight_slots[:, :half],
         (((0, 2), (1, 2)), ((), ())),
         preferred_element_type=jnp.float32,
     ) + lax.dot_general(
-        far[:, :block_rows],
+        far,
         weight_slots[:, half:],
         (((0, 2), (1, 2)), ((), ())),
         preferred_element_type=jnp.float32,
     )
-    projected = projected.astype(jnp.bfloat16)
+    projected = projected.astype(jnp.bfloat16)[:block_rows]
     rider_rows = jnp.concatenate(
         [near[:, block_rows : block_rows + PARTS], far[:, block_rows : block_rows + PARTS]], axis=0
     )
@@ -213,10 +213,12 @@
     chosen = (position[None, :, 0] == places) | (position[None, :, 1] == places)
     for pick in range(2, TOP):
         chosen = chosen | (position[None, :, pick] == places)
-    tile_rows = jnp.dot(
-        chosen.astype(jnp.bfloat16), projected, preferred_element_type=jnp.float32
+    tile_rows = jnp.einsum(
+        "est,tm->esm",
+        chosen.astype(jnp.bfloat16).reshape(experts_all, capacity, block_rows),
+        projected,
+        preferred_element_type=jnp.float32,
     ).astype(jnp.bfloat16)
-    tile_rows = tile_rows.reshape(experts_all, capacity, model_cols)
     received = lax.all_to_all(tile_rows, EP, split_axis=0, concat_axis=2, tiled=True)
 
     local_flags = flagged - ctx_index * block_rows

time: 140 us -> 137 us (0.979)
  waiting for transfers between devices: 52 us -> 48.6 us
  matrix products: 9.79 us -> 11.4 us
    ppermute x5, waiting for transfers between devices: 2.33 us -> 0.01 us  [step(): arrived = lax.ppermute(current, axis, pairs)]
    convert_element_type x1 -> x0, local copies, waits for them, and re-layouts: 1.99 us -> none  [local_body(): tile_rows = jnp.dot(chosen.astype(jnp.bfloat16), projected, preferred_ele...]
    dot_general x2 -> x3, matrix products: 6.66 us -> 7.32 us  [the longest x1 3.37 us: local_body(): lax.dot_general(near, weight_slots[:, :half], (((0, 2), (1, 2)), ((), ())...]
  transfers between devices with their start and end apart: 17 -> 17, of which waited for: 6 -> 5; matrix products, arithmetic and copies ran while one was open for 12% -> 16% of each run, Pallas kernels for 0% -> 0%
where the time goes in v10:
time: 137 us; the launch traced here: 136 us
  starting transfers between devices  51.4 us (38%)
  waiting for transfers between devices  48.6 us (35%)
  local copies, waits for them, and re-layouts  16.6 us (12%)
  matrix products  11.4 us (8%)
  other arithmetic  6.68 us (5%)
    ppermute x1, waiting for transfers between devices, exclusive_scan(): from_odd = lax.ppermute(segment, axis, to_even)  31.5 us
    ppermute x8, starting transfers between devices, shifted(): lax.ppermute(value, axis, [(i, (i + steps) % RING) for i in range(RING)])  26.4 us
    ppermute x1, starting transfers between devices, local_body(): far = lax.ppermute(near, 'core', [(0, 1), (1, 0)])  13 us
    all_to_all x1, waiting for transfers between devices, local_body(): lax.all_to_all(tile_rows, EP, split_axis=0, concat_axis=2, tiled=True)  9.21 us
    ppermute x8, waiting for transfers between devices, shifted(): lax.ppermute(value, axis, [(i, (i + steps) % RING) for i in range(RING)])  7.93 us
    ppermute x5, starting transfers between devices, step(): arrived = lax.ppermute(current, axis, pairs)  5.33 us
    all_to_all x1, starting transfers between devices, local_body(): lax.all_to_all(tile_rows, EP, split_axis=0, concat_axis=2, tiled=True)  4.66 us
    unnamed x19, local copies, waits for them, and re-layouts  4.3 us
  transfers between devices with their start and end apart: 17, of which 5 were waited for; matrix products, arithmetic and copies ran while one was open for 16% of the time, Pallas kernels for 0%

profile of v10, /device:TPU:385, one launch (start us, length us, event | category | flops | bytes accessed | tf_op | source)
XLA Modules:
  0.0 136.0 jit_solution(8701063980966994860)
XLA Ops:
  0.0 0.7 reshape.326
  0.7 0.6 reduce-window.16
  1.3 0.2 slice_reduce_fusion.1
  1.5 0.2 reduce-window.19
  1.8 0.2 slice_reduce_fusion.2
  2.0 1.0 copy.114
  3.1 1.1 convolution_add_fusion
  4.2 2.6 %collective-permute-start = (f32[2,136,128]{2,1,0:T(8,128)S(1)}, f32[2,136,128]{2,1,0:T(8,128)S(1)}, u32[]{:S(2)}, u32[]{:S(2)}) collective-permute-start(f32[2,136,128]{2,1,0:T(8,128)S(1)} %pad_maximum_fusion.1), channel_id=1, source_target_pairs={{0,32},{64,96},{128,160},{192,224},{256,288},{320,352},{384,416},{... | collective-permute-start | bytes 417800 | tf_op jit(solution)/shard_map/ppermute | solution.py:73
  6.9 0.8 copy.97
  7.8 0.1 eq.154
  7.9 1.3 fusion.15
  9.4 0.7 collective-permute-start.1
  10.1 0.1 fusion.91
  10.4 0.7 collective-permute-start.2
  11.3 0.7 collective-permute-start.3
  12.0 0.5 fusion.14
  12.5 1.2 reduce-window.14
  13.9 0.7 collective-permute-start.4
  14.6 0.2 slice_reduce_fusion
  15.1 0.7 collective-permute-start.5
  15.8 0.1 eq.150
  16.0 0.1 fusion.90
  16.1 1.3 collective-permute-start.6
  17.5 31.5 %collective-permute-done.6 = f32[2,136,128]{2,1,0:T(8,128)S(1)} collective-permute-done((f32[2,136,128]{2,1,0:T(8,128)S(1)}, f32[2,136,128]{2,1,0:T(8,128)S(1)}, u32[]{:S(2)}, u32[]{:S(2)}) %collective-permute-start.6) | collective-permute-done | bytes 139296 | tf_op jit(solution)/shard_map/ppermute | solution.py:100
  48.9 0.5 multiply_reduce_fusion
  49.7 4.4 %collective-permute-start.7 = (bf16[1,264,256]{2,1,0:T(8,128)(2,1)S(1)}, bf16[1,264,256]{2,1,0:T(8,128)(2,1)S(1)}, u32[]{:S(2)}, u32[]{:S(2)}) collective-permute-start(bf16[1,264,256]{2,1,0:T(8,128)(2,1)S(1)} %maximum_bitcast_fusion), channel_id=1, source_target_pairs={{0,24},{8,0},{16,8},{24,16},{1,25},{9,1},{17,9},{25,17},{2,26},{10... | collective-permute-start | bytes 405512 | tf_op jit(solution)/shard_map/ppermute | solution.py:58
  54.0 1.9 %collective-permute-start.10 = (bf16[1,264,256]{2,1,0:T(8,128)(2,1)S(1)}, bf16[1,264,256]{2,1,0:T(8,128)(2,1)S(1)}, u32[]{:S(2)}, u32[]{:S(2)}) collective-permute-start(bf16[1,264,256]{2,1,0:T(8,128)(2,1)S(1)} %maximum_bitcast_fusion), channel_id=1, source_target_pairs={{0,8},{8,16},{16,24},{24,0},{1,9},{9,17},{17,25},{25,1},{2,10},{10... | collective-permute-start | bytes 405512 | tf_op jit(solution)/shard_map/ppermute | solution.py:58
  56.0 3.6 %collective-permute-start.8 = (bf16[1,264,128]{2,1,0:T(8,128)(2,1)S(1)}, bf16[1,264,128]{2,1,0:T(8,128)(2,1)S(1)}, u32[]{:S(2)}, u32[]{:S(2)}) collective-permute-start(bf16[1,264,128]{2,1,0:T(8,128)(2,1)S(1)} %get-tuple-element.26), channel_id=1, source_target_pairs={{0,16},{8,24},{16,0},{24,8},{1,17},{9,25},{17,1},{25,9},{2,18},{10... | collective-permute-start | bytes 202760 | tf_op jit(solution)/shard_map/ppermute | solution.py:58
  59.6 3.2 %collective-permute-start.9 = (bf16[1,264,128]{2,1,0:T(8,128)(2,1)S(1)}, bf16[1,264,128]{2,1,0:T(8,128)(2,1)S(1)}, u32[]{:S(2)}, u32[]{:S(2)}) collective-permute-start(bf16[1,264,128]{2,1,0:T(8,128)(2,1)S(1)} %get-tuple-element.25), channel_id=1, source_target_pairs={{0,16},{8,24},{16,0},{24,8},{1,17},{9,25},{17,1},{25,9},{2,18},{10... | collective-permute-start | bytes 202760 | tf_op jit(solution)/shard_map/ppermute | solution.py:58
  62.8 0.6 constant_dynamic-update-slice_fusion.6
  63.4 2.7 %collective-permute-done.9 = bf16[1,264,128]{2,1,0:T(8,128)(2,1)S(1)} collective-permute-done((bf16[1,264,128]{2,1,0:T(8,128)(2,1)S(1)}, bf16[1,264,128]{2,1,0:T(8,128)(2,1)S(1)}, u32[]{:S(2)}, u32[]{:S(2)}) %collective-permute-start.9) | collective-permute-done | bytes 67616 | tf_op jit(solution)/shard_map/ppermute | solution.py:58
  66.2 4.6 %collective-permute-start.11 = (bf16[4,264,256]{2,1,0:T(8,128)(2,1)S(1)}, bf16[4,264,256]{2,1,0:T(8,128)(2,1)S(1)}, u32[]{:S(2)}, u32[]{:S(2)}) collective-permute-start(bf16[4,264,256]{2,1,0:T(8,128)(2,1)S(1)} %pad_maximum_fusion), channel_id=1, source_target_pairs={{0,6},{2,0},{4,2},{6,4},{1,7},{3,1},{5,3},{7,5},{8,14},{10,8},{12,... | collective-permute-start | bytes 1622024 | tf_op jit(solution)/shard_map/ppermute | solution.py:58
  71.0 1.9 %collective-permute-start.14 = (bf16[4,264,256]{2,1,0:T(8,128)(2,1)S(1)}, bf16[4,264,256]{2,1,0:T(8,128)(2,1)S(1)}, u32[]{:S(2)}, u32[]{:S(2)}) collective-permute-start(bf16[4,264,256]{2,1,0:T(8,128)(2,1)S(1)} %pad_maximum_fusion), channel_id=1, source_target_pairs={{0,2},{2,4},{4,6},{6,0},{1,3},{3,5},{5,7},{7,1},{8,10},{10,12},{12... | collective-permute-start | bytes 1622024 | tf_op jit(solution)/shard_map/ppermute | solution.py:58
  72.9 3.5 %collective-permute-start.13 = (bf16[4,264,128]{2,1,0:T(8,128)(2,1)S(1)}, bf16[4,264,128]{2,1,0:T(8,128)(2,1)S(1)}, u32[]{:S(2)}, u32[]{:S(2)}) collective-permute-start(bf16[4,264,128]{2,1,0:T(8,128)(2,1)S(1)} %get-tuple-element.24), channel_id=1, source_target_pairs={{0,4},{2,6},{4,0},{6,2},{1,5},{3,7},{5,1},{7,3},{8,12},{10,14},{12... | collective-permute-start | bytes 811016 | tf_op jit(solution)/shard_map/ppermute | solution.py:58
  76.5 3.2 %collective-permute-start.12 = (bf16[4,264,128]{2,1,0:T(8,128)(2,1)S(1)}, bf16[4,264,128]{2,1,0:T(8,128)(2,1)S(1)}, u32[]{:S(2)}, u32[]{:S(2)}) collective-permute-start(bf16[4,264,128]{2,1,0:T(8,128)(2,1)S(1)} %get-tuple-element.23), channel_id=1, source_target_pairs={{0,4},{2,6},{4,0},{6,2},{1,5},{3,7},{5,1},{7,3},{8,12},{10,14},{12... | collective-permute-start | bytes 811016 | tf_op jit(solution)/shard_map/ppermute | solution.py:58
  79.7 0.7 constant_dynamic-update-slice_fusion.5
  80.4 0.6 constant_dynamic-update-slice_fusion.4
  81.0 0.7 constant_dynamic-update-slice_fusion.3
  81.7 0.7 constant_dynamic-update-slice_fusion.2
  82.4 0.8 constant_dynamic-update-slice_fusion.1
  83.2 1.1 collective-permute-done.13
  84.3 4.1 %collective-permute-done.12 = bf16[4,264,128]{2,1,0:T(8,128)(2,1)S(1)} collective-permute-done((bf16[4,264,128]{2,1,0:T(8,128)(2,1)S(1)}, bf16[4,264,128]{2,1,0:T(8,128)(2,1)S(1)}, u32[]{:S(2)}, u32[]{:S(2)}) %collective-permute-start.12) | collective-permute-done | bytes 270368 | tf_op jit(solution)/shard_map/ppermute | solution.py:58
  88.4 0.9 maximum_dynamic-update-slice_fusion
  89.3 0.8 constant_dynamic-update-slice_fusion
  90.1 13.0 %collective-permute-start.15 = (bf16[16,264,256]{2,1,0:T(8,128)(2,1)}, bf16[16,264,256]{2,1,0:T(8,128)(2,1)}, u32[]{:S(2)}, u32[]{:S(2)}) collective-permute-start(bf16[16,264,256]{2,1,0:T(8,128)(2,1)} %constant_dynamic-update-slice_fusion), channel_id=1, source_target_pairs={{0,1},{1,0},{2,3},{3,2},{4,5},{5,4},{6,7},{7,6},{8,9},{9,8},{10,11... | collective-permute-start | bytes 6488072 | tf_op jit(solution)/shard_map/ppermute | solution.py:172
  103.2 0.1 reduce_sum.30
  103.5 2.3 %copy.156 = bf16[24,32,8,256]{3,2,0,1:T(8,128)(2,1)S(1)} copy(bf16[24,32,8,256]{3,2,1,0:T(8,128)(2,1)} %bitcast.134) | data formatting | bytes 6291456 | tf_op jit(solution)/shard_map/reshape | solution.py:182
  106.2 0.2 copy.96
  106.4 0.2 and.85
  106.6 2.4 %gather_fusion = bf16[32,192,256]{2,1,0:T(8,128)(2,1)} fusion(bf16[192,32,256]{2,0,1:T(8,128)(2,1)S(1)} %bitcast.133, s32[1024]{0:T(1024)S(1)} %pad_clamp_fusion), kind=kCustom, calls=%fused_computation | custom fusion | bytes 6291584 | tf_op jit(solution)/shard_map/jit(_take)/gather | solution.py:181
  109.0 0.1 fusion.68
  109.2 0.9 slice.238
  110.0 3.4 %fusion.6 = f32[264,192]{0,1:T(8,128)S(1)} fusion(bf16[16,264,256]{2,1,0:T(8,128)(2,1)} %constant_dynamic-update-slice_fusion, bf16[192,32,256]{2,0,1:T(8,128)(2,1)} %bitcast.135), kind=kOutput, calls=%fused_computation.10 | convolution fusion | flops 415236096 | bytes 3938304 | tf_op jit(solution)/shard_map/dot_general | solution.py:185
  113.4 2.8 %fusion.9 = f32[264,192]{0,1:T(8,128)S(1)} fusion(bf16[16,264,256]{2,1,0:T(8,128)(2,1)} %collective-permute-done.15, bf16[192,32,256]{2,0,1:T(8,128)(2,1)S(1)} %bitcast.136), kind=kOutput, calls=%fused_computation.11 | convolution fusion | flops 415236096 | bytes 3938304 | tf_op jit(solution)/shard_map/dot_general | solution.py:190
  116.2 1.2 convolution_convert_fusion
  117.4 4.7 %all-to-all-start = ((bf16[32,32,192]{2,1,0:T(8,128)(2,1)}), bf16[32,32,192]{2,1,0:T(8,128)(2,1)S(1)}, u32[]{:S(2)}, u32[]{:S(2)}) async-start(bf16[32,32,192]{2,1,0:T(8,128)(2,1)} %convolution_convert_fusion), calls=%async_computation | async-start | bytes 1048576 | tf_op jit(solution)/shard_map/all_to_all | solution.py:222
  122.1 0.9 slice.239
  123.0 0.1 fusion.18
  123.1 0.6 multiply_reduce_fusion.1
  124.4 9.2 %all-to-all-done = bf16[32,32,192]{2,1,0:T(8,128)(2,1)S(1)} async-done(((bf16[32,32,192]{2,1,0:T(8,128)(2,1)}), bf16[32,32,192]{2,1,0:T(8,128)(2,1)S(1)}, u32[]{:S(2)}, u32[]{:S(2)}) %all-to-all-start) | async-done | bytes 393248 | tf_op jit(solution)/shard_map/all_to_all | solution.py:222
  133.7 0.3 copy.110
  134.0 0.5 all_to_all.16
  134.5 0.5 fusion.19
  135.0 1.0 fusion.23
  (83 shorter events, 2.5 us)
Async XLA Ops:
  0.0 7.9 %copy-start = (bf16[256,256]{1,0:T(8,128)(2,1)S(1)}, bf16[256,256]{1,0:T(8,128)(2,1)}, u32[]{:S(2)}) copy-start(bf16[256,256]{1,0:T(8,128)(2,1)} %param.8) | copy-start | bytes 393220
  3.0 8.0 %copy-start.4 = (f32[192]{0:T(256)S(1)}, f32[192]{0:T(256)}, u32[]{:S(2)}) copy-start(f32[192]{0:T(256)} %param.15) | copy-start | bytes 2308
  4.2 5.0 %collective-permute-start = (f32[2,136,128]{2,1,0:T(8,128)S(1)}, f32[2,136,128]{2,1,0:T(8,128)S(1)}, u32[]{:S(2)}, u32[]{:S(2)}) collective-permute-start(f32[2,136,128]{2,1,0:T(8,128)S(1)} %pad_maximum_fusion.1), channel_id=1, source_target_pairs={{0,32},{64,96},{128,160},{192,224},{256,288},{320,352},{384,416},{... | collective-permute-start | bytes 417800 | tf_op jit(solution)/shard_map/ppermute | solution.py:73
  9.4 0.8 collective-permute-start.1
  10.4 0.8 collective-permute-start.2
  11.3 2.5 %collective-permute-start.3 = (f32[2,136,128]{2,1,0:T(8,128)S(1)}, f32[2,136,128]{2,1,0:T(8,128)S(1)}, u32[]{:S(2)}, u32[]{:S(2)}) collective-permute-start(f32[2,136,128]{2,1,0:T(8,128)S(1)} %maximum_select_fusion.2), channel_id=1, source_target_pairs={{224,352},{225,353},{226,354},{227,355},{228,356},{229,357},{230,3... | collective-permute-start | bytes 417800 | tf_op jit(solution)/shard_map/ppermute | solution.py:73
  13.9 1.1 collective-permute-start.4
  15.1 2.3 %collective-permute-start.5 = (f32[2,136,128]{2,1,0:T(8,128)S(1)}, f32[2,136,128]{2,1,0:T(8,128)S(1)}, u32[]{:S(2)}, u32[]{:S(2)}) collective-permute-start(f32[2,136,128]{2,1,0:T(8,128)S(1)} %maximum_select_fusion.4), channel_id=1, source_target_pairs={{32,96},{96,160},{160,224},{224,288},{288,352},{352,416},{416,480}... | collective-permute-start | bytes 417800 | tf_op jit(solution)/shard_map/ppermute | solution.py:101
  16.0 55.0 %copy-start.3 = (s32[32,5]{0,1:T(8,128)}, s32[32,5]{0,1:T(8,128)S(1)}, u32[]{:S(2)}) copy-start(s32[32,5]{0,1:T(8,128)S(1)} %reduce-window.15) | copy-start | bytes 1924
  16.1 32.9 %collective-permute-start.6 = (f32[2,136,128]{2,1,0:T(8,128)S(1)}, f32[2,136,128]{2,1,0:T(8,128)S(1)}, u32[]{:S(2)}, u32[]{:S(2)}) collective-permute-start(f32[2,136,128]{2,1,0:T(8,128)S(1)} %maximum_select_fusion.4), channel_id=1, source_target_pairs={{32,64},{96,128},{160,192},{224,256},{288,320},{352,384},{416,448}... | collective-permute-start | bytes 417800 | tf_op jit(solution)/shard_map/ppermute | solution.py:100
  49.7 16.5 %collective-permute-start.7 = (bf16[1,264,256]{2,1,0:T(8,128)(2,1)S(1)}, bf16[1,264,256]{2,1,0:T(8,128)(2,1)S(1)}, u32[]{:S(2)}, u32[]{:S(2)}) collective-permute-start(bf16[1,264,256]{2,1,0:T(8,128)(2,1)S(1)} %maximum_bitcast_fusion), channel_id=1, source_target_pairs={{0,24},{8,0},{16,8},{24,16},{1,25},{9,1},{17,9},{25,17},{2,26},{10... | collective-permute-start | bytes 405512 | tf_op jit(solution)/shard_map/ppermute | solution.py:58
  54.0 12.1 %collective-permute-start.10 = (bf16[1,264,256]{2,1,0:T(8,128)(2,1)S(1)}, bf16[1,264,256]{2,1,0:T(8,128)(2,1)S(1)}, u32[]{:S(2)}, u32[]{:S(2)}) collective-permute-start(bf16[1,264,256]{2,1,0:T(8,128)(2,1)S(1)} %maximum_bitcast_fusion), channel_id=1, source_target_pairs={{0,8},{8,16},{16,24},{24,0},{1,9},{9,17},{17,25},{25,1},{2,10},{10... | collective-permute-start | bytes 405512 | tf_op jit(solution)/shard_map/ppermute | solution.py:58
  56.0 7.5 %collective-permute-start.8 = (bf16[1,264,128]{2,1,0:T(8,128)(2,1)S(1)}, bf16[1,264,128]{2,1,0:T(8,128)(2,1)S(1)}, u32[]{:S(2)}, u32[]{:S(2)}) collective-permute-start(bf16[1,264,128]{2,1,0:T(8,128)(2,1)S(1)} %get-tuple-element.26), channel_id=1, source_target_pairs={{0,16},{8,24},{16,0},{24,8},{1,17},{9,25},{17,1},{25,9},{2,18},{10... | collective-permute-start | bytes 202760 | tf_op jit(solution)/shard_map/ppermute | solution.py:58
  59.6 6.5 %collective-permute-start.9 = (bf16[1,264,128]{2,1,0:T(8,128)(2,1)S(1)}, bf16[1,264,128]{2,1,0:T(8,128)(2,1)S(1)}, u32[]{:S(2)}, u32[]{:S(2)}) collective-permute-start(bf16[1,264,128]{2,1,0:T(8,128)(2,1)S(1)} %get-tuple-element.25), channel_id=1, source_target_pairs={{0,16},{8,24},{16,0},{24,8},{1,17},{9,25},{17,1},{25,9},{2,18},{10... | collective-permute-start | bytes 202760 | tf_op jit(solution)/shard_map/ppermute | solution.py:58
  66.2 16.1 %collective-permute-start.11 = (bf16[4,264,256]{2,1,0:T(8,128)(2,1)S(1)}, bf16[4,264,256]{2,1,0:T(8,128)(2,1)S(1)}, u32[]{:S(2)}, u32[]{:S(2)}) collective-permute-start(bf16[4,264,256]{2,1,0:T(8,128)(2,1)S(1)} %pad_maximum_fusion), channel_id=1, source_target_pairs={{0,6},{2,0},{4,2},{6,4},{1,7},{3,1},{5,3},{7,5},{8,14},{10,8},{12,... | collective-permute-start | bytes 1622024 | tf_op jit(solution)/shard_map/ppermute | solution.py:58
  71.0 18.3 %collective-permute-start.14 = (bf16[4,264,256]{2,1,0:T(8,128)(2,1)S(1)}, bf16[4,264,256]{2,1,0:T(8,128)(2,1)S(1)}, u32[]{:S(2)}, u32[]{:S(2)}) collective-permute-start(bf16[4,264,256]{2,1,0:T(8,128)(2,1)S(1)} %pad_maximum_fusion), channel_id=1, source_target_pairs={{0,2},{2,4},{4,6},{6,0},{1,3},{3,5},{5,7},{7,1},{8,10},{10,12},{12... | collective-permute-start | bytes 1622024 | tf_op jit(solution)/shard_map/ppermute | solution.py:58
  72.9 30.2 %slice-start = ((s32[32,5]{0,1:T(8,128)}), s32[32,4]{0,1:T(4,128)S(1)}, s32[]{:S(2)}) async-start(s32[32,5]{0,1:T(8,128)} %copy-done.3), calls=%async_computation.1 | async-start | bytes 4096 | tf_op jit(solution)/shard_map/slice.3
  72.9 11.3 %collective-permute-start.13 = (bf16[4,264,128]{2,1,0:T(8,128)(2,1)S(1)}, bf16[4,264,128]{2,1,0:T(8,128)(2,1)S(1)}, u32[]{:S(2)}, u32[]{:S(2)}) collective-permute-start(bf16[4,264,128]{2,1,0:T(8,128)(2,1)S(1)} %get-tuple-element.24), channel_id=1, source_target_pairs={{0,4},{2,6},{4,0},{6,2},{1,5},{3,7},{5,1},{7,3},{8,12},{10,14},{12... | collective-permute-start | bytes 811016 | tf_op jit(solution)/shard_map/ppermute | solution.py:58
  76.5 11.9 %collective-permute-start.12 = (bf16[4,264,128]{2,1,0:T(8,128)(2,1)S(1)}, bf16[4,264,128]{2,1,0:T(8,128)(2,1)S(1)}, u32[]{:S(2)}, u32[]{:S(2)}) collective-permute-start(bf16[4,264,128]{2,1,0:T(8,128)(2,1)S(1)} %get-tuple-element.23), channel_id=1, source_target_pairs={{0,4},{2,6},{4,0},{6,2},{1,5},{3,7},{5,1},{7,3},{8,12},{10,14},{12... | collective-permute-start | bytes 811016 | tf_op jit(solution)/shard_map/ppermute | solution.py:58
  90.1 23.3 %collective-permute-start.15 = (bf16[16,264,256]{2,1,0:T(8,128)(2,1)}, bf16[16,264,256]{2,1,0:T(8,128)(2,1)}, u32[]{:S(2)}, u32[]{:S(2)}) collective-permute-start(bf16[16,264,256]{2,1,0:T(8,128)(2,1)} %constant_dynamic-update-slice_fusion), channel_id=1, source_target_pairs={{0,1},{1,0},{2,3},{3,2},{4,5},{5,4},{6,7},{7,6},{8,9},{9,8},{10,11... | collective-permute-start | bytes 6488072 | tf_op jit(solution)/shard_map/ppermute | solution.py:172
  103.5 2.6 %copy-start.5 = (s32[64]{0:T(128)S(1)}, s32[64]{0:T(128)}, u32[]{:S(2)}) copy-start(s32[64]{0:T(128)} %param.14) | copy-start | bytes 772
  103.5 2.7 %copy-start.2 = (s32[256,2]{0,1:T(2,128)S(1)}, s32[256,2]{0,1:T(2,128)}, u32[]{:S(2)}) copy-start(s32[256,2]{0,1:T(2,128)} %param.13) | copy-start | bytes 6148
  110.0 3.4 %copy-start.1 = (bf16[32,192,256]{2,1,0:T(8,128)(2,1)S(1)}, bf16[32,192,256]{2,1,0:T(8,128)(2,1)}, u32[]{:S(2)}) copy-start(bf16[32,192,256]{2,1,0:T(8,128)(2,1)} %gather_fusion) | copy-start | bytes 9437188
  117.4 16.3 %all-to-all-start = ((bf16[32,32,192]{2,1,0:T(8,128)(2,1)}), bf16[32,32,192]{2,1,0:T(8,128)(2,1)S(1)}, u32[]{:S(2)}, u32[]{:S(2)}) async-start(bf16[32,32,192]{2,1,0:T(8,128)(2,1)} %convolution_convert_fusion), calls=%async_computation | async-start | bytes 1048576 | tf_op jit(solution)/shard_map/all_to_all | solution.py:222

commit v11 on v7

--- a/solution.py
+++ b/solution.py
@@ -19,7 +19,9 @@
     kv_state, offset = carried_in
     query_sub, key_sub, value_sub, decay_sub = pieces
     sub_rows = query_sub.shape[0]
-    cumulated = jnp.cumsum(decay_sub, axis=0)
+    rows = jnp.arange(sub_rows, dtype=jnp.int32)
+    lower = (rows[:, None] >= rows[None, :]).astype(jnp.float32)
+    cumulated = jnp.dot(lower, decay_sub, precision=lax.Precision.HIGHEST)
     scores = jnp.einsum("thd,shd->hts", query_sub, key_sub, preferred_element_type=jnp.float32)
     spread = jnp.transpose(cumulated)
     decay_gaps = jnp.minimum(spread[:, :, None] - spread[:, None, :], 0.0)
@@ -183,17 +185,17 @@
     )
     half = near.shape[0]
     projected = lax.dot_general(
-        near[:, :block_rows],
+        near,
         weight_slots[:, :half],
         (((0, 2), (1, 2)), ((), ())),
         preferred_element_type=jnp.float32,
     ) + lax.dot_general(
-        far[:, :block_rows],
+        far,
         weight_slots[:, half:],
         (((0, 2), (1, 2)), ((), ())),
         preferred_element_type=jnp.float32,
     )
-    projected = projected.astype(jnp.bfloat16)
+    projected = projected.astype(jnp.bfloat16)[:block_rows]
     rider_rows = jnp.concatenate(
         [near[:, block_rows : block_rows + PARTS], far[:, block_rows : block_rows + PARTS]], axis=0
     )

time: 140 us -> 138 us (0.986)
  local copies, waits for them, and re-layouts: 17.9 us -> 16.1 us
  matrix products: 9.79 us -> 11.5 us
    dot_general x1 -> x3, matrix products: 3.02 us -> 7.06 us  [the longest x1 3.38 us: local_body(): lax.dot_general(near, weight_slots[:, :half], (((0, 2), (1, 2)), ((), ())...]
    dot_general x1, matrix products: 3.63 us -> 0.4 us  [local_body(): jnp.dot(chosen.astype(jnp.bfloat16), projected, preferred_element_type=jn...]
    unnamed x19 -> x16, local copies, waits for them, and re-layouts: 3.63 us -> 3.62 us
  transfers between devices with their start and end apart: 17 -> 17, of which waited for: 6 -> 6; matrix products, arithmetic and copies ran while one was open for 12% -> 16% of each run, Pallas kernels for 0% -> 0%
where the time goes in v11:
time: 138 us; the launch traced here: 137 us
  starting transfers between devices  51.4 us (37%)
  waiting for transfers between devices  50.7 us (37%)
  local copies, waits for them, and re-layouts  16.1 us (12%)
  matrix products  11.5 us (8%)
  other arithmetic  5.81 us (4%)
    ppermute x1, waiting for transfers between devices, exclusive_scan(): from_odd = lax.ppermute(segment, axis, to_even)  31.2 us
    ppermute x8, starting transfers between devices, shifted(): lax.ppermute(value, axis, [(i, (i + steps) % RING) for i in range(RING)])  26.4 us
    ppermute x1, starting transfers between devices, local_body(): far = lax.ppermute(near, 'core', [(0, 1), (1, 0)])  13 us
    all_to_all x1, waiting for transfers between devices, local_body(): lax.all_to_all(tile_rows, EP, split_axis=0, concat_axis=2, tiled=True)  9.21 us
    ppermute x8, waiting for transfers between devices, shifted(): lax.ppermute(value, axis, [(i, (i + steps) % RING) for i in range(RING)])  7.93 us
    ppermute x5, starting transfers between devices, step(): arrived = lax.ppermute(current, axis, pairs)  5.33 us
    all_to_all x1, starting transfers between devices, local_body(): lax.all_to_all(tile_rows, EP, split_axis=0, concat_axis=2, tiled=True)  4.67 us
    unnamed x16, local copies, waits for them, and re-layouts  3.62 us
  transfers between devices with their start and end apart: 17, of which 6 were waited for; matrix products, arithmetic and copies ran while one was open for 16% of the time, Pallas kernels for 0%

profile of v11, /device:TPU:385, one launch (start us, length us, event | category | flops | bytes accessed | tf_op | source)
XLA Modules:
  0.0 136.8 jit_solution(13070579669975344866)
XLA Ops:
  0.0 0.9 fusion.57
  0.9 0.2 slice_reduce_fusion.1
  1.2 1.0 copy.90
  2.3 1.1 convolution_add_fusion
  3.4 2.7 %collective-permute-start = (f32[2,136,128]{2,1,0:T(8,128)S(1)}, f32[2,136,128]{2,1,0:T(8,128)S(1)}, u32[]{:S(2)}, u32[]{:S(2)}) collective-permute-start(f32[2,136,128]{2,1,0:T(8,128)S(1)} %pad_maximum_fusion.1), channel_id=1, source_target_pairs={{0,32},{64,96},{128,160},{192,224},{256,288},{320,352},{384,416},{... | collective-permute-start | bytes 417800 | tf_op jit(solution)/shard_map/ppermute | solution.py:75
  6.2 2.3 %collective-permute-done = f32[2,136,128]{2,1,0:T(8,128)S(1)} collective-permute-done((f32[2,136,128]{2,1,0:T(8,128)S(1)}, f32[2,136,128]{2,1,0:T(8,128)S(1)}, u32[]{:S(2)}, u32[]{:S(2)}) %collective-permute-start) | collective-permute-done | bytes 139296 | tf_op jit(solution)/shard_map/ppermute | solution.py:75
  8.6 0.7 collective-permute-start.1
  9.3 1.3 fusion.15
  10.6 0.1 copy.72
  10.8 0.1 eq.142
  10.9 0.1 fusion.89
  11.1 0.7 collective-permute-start.2
  11.8 0.1 fusion.90
  12.1 0.7 collective-permute-start.3
  12.8 0.1 fusion.91
  13.0 0.7 collective-permute-start.4
  13.7 0.5 fusion.14
  14.5 0.7 collective-permute-start.5
  15.2 1.2 reduce-window.6
  16.5 1.3 collective-permute-start.6
  17.9 31.2 %collective-permute-done.6 = f32[2,136,128]{2,1,0:T(8,128)S(1)} collective-permute-done((f32[2,136,128]{2,1,0:T(8,128)S(1)}, f32[2,136,128]{2,1,0:T(8,128)S(1)}, u32[]{:S(2)}, u32[]{:S(2)}) %collective-permute-start.6) | collective-permute-done | bytes 139296 | tf_op jit(solution)/shard_map/ppermute | solution.py:102
  49.1 0.5 multiply_reduce_fusion
  49.8 4.4 %collective-permute-start.7 = (bf16[1,264,256]{2,1,0:T(8,128)(2,1)S(1)}, bf16[1,264,256]{2,1,0:T(8,128)(2,1)S(1)}, u32[]{:S(2)}, u32[]{:S(2)}) collective-permute-start(bf16[1,264,256]{2,1,0:T(8,128)(2,1)S(1)} %maximum_bitcast_fusion), channel_id=1, source_target_pairs={{0,24},{8,0},{16,8},{24,16},{1,25},{9,1},{17,9},{25,17},{2,26},{10... | collective-permute-start | bytes 405512 | tf_op jit(solution)/shard_map/ppermute | solution.py:60
  54.2 1.9 %collective-permute-start.10 = (bf16[1,264,256]{2,1,0:T(8,128)(2,1)S(1)}, bf16[1,264,256]{2,1,0:T(8,128)(2,1)S(1)}, u32[]{:S(2)}, u32[]{:S(2)}) collective-permute-start(bf16[1,264,256]{2,1,0:T(8,128)(2,1)S(1)} %maximum_bitcast_fusion), channel_id=1, source_target_pairs={{0,8},{8,16},{16,24},{24,0},{1,9},{9,17},{17,25},{25,1},{2,10},{10... | collective-permute-start | bytes 405512 | tf_op jit(solution)/shard_map/ppermute | solution.py:60
  56.2 3.6 %collective-permute-start.8 = (bf16[1,264,128]{2,1,0:T(8,128)(2,1)S(1)}, bf16[1,264,128]{2,1,0:T(8,128)(2,1)S(1)}, u32[]{:S(2)}, u32[]{:S(2)}) collective-permute-start(bf16[1,264,128]{2,1,0:T(8,128)(2,1)S(1)} %get-tuple-element.26), channel_id=1, source_target_pairs={{0,16},{8,24},{16,0},{24,8},{1,17},{9,25},{17,1},{25,9},{2,18},{10... | collective-permute-start | bytes 202760 | tf_op jit(solution)/shard_map/ppermute | solution.py:60
  59.8 3.2 %collective-permute-start.9 = (bf16[1,264,128]{2,1,0:T(8,128)(2,1)S(1)}, bf16[1,264,128]{2,1,0:T(8,128)(2,1)S(1)}, u32[]{:S(2)}, u32[]{:S(2)}) collective-permute-start(bf16[1,264,128]{2,1,0:T(8,128)(2,1)S(1)} %get-tuple-element.25), channel_id=1, source_target_pairs={{0,16},{8,24},{16,0},{24,8},{1,17},{9,25},{17,1},{25,9},{2,18},{10... | collective-permute-start | bytes 202760 | tf_op jit(solution)/shard_map/ppermute | solution.py:60
  63.0 0.6 constant_dynamic-update-slice_fusion.6
  63.6 2.7 %collective-permute-done.9 = bf16[1,264,128]{2,1,0:T(8,128)(2,1)S(1)} collective-permute-done((bf16[1,264,128]{2,1,0:T(8,128)(2,1)S(1)}, bf16[1,264,128]{2,1,0:T(8,128)(2,1)S(1)}, u32[]{:S(2)}, u32[]{:S(2)}) %collective-permute-start.9) | collective-permute-done | bytes 67616 | tf_op jit(solution)/shard_map/ppermute | solution.py:60
  66.4 4.6 %collective-permute-start.11 = (bf16[4,264,256]{2,1,0:T(8,128)(2,1)S(1)}, bf16[4,264,256]{2,1,0:T(8,128)(2,1)S(1)}, u32[]{:S(2)}, u32[]{:S(2)}) collective-permute-start(bf16[4,264,256]{2,1,0:T(8,128)(2,1)S(1)} %pad_maximum_fusion), channel_id=1, source_target_pairs={{0,6},{2,0},{4,2},{6,4},{1,7},{3,1},{5,3},{7,5},{8,14},{10,8},{12,... | collective-permute-start | bytes 1622024 | tf_op jit(solution)/shard_map/ppermute | solution.py:60
  71.2 1.9 %collective-permute-start.14 = (bf16[4,264,256]{2,1,0:T(8,128)(2,1)S(1)}, bf16[4,264,256]{2,1,0:T(8,128)(2,1)S(1)}, u32[]{:S(2)}, u32[]{:S(2)}) collective-permute-start(bf16[4,264,256]{2,1,0:T(8,128)(2,1)S(1)} %pad_maximum_fusion), channel_id=1, source_target_pairs={{0,2},{2,4},{4,6},{6,0},{1,3},{3,5},{5,7},{7,1},{8,10},{10,12},{12... | collective-permute-start | bytes 1622024 | tf_op jit(solution)/shard_map/ppermute | solution.py:60
  73.1 3.5 %collective-permute-start.13 = (bf16[4,264,128]{2,1,0:T(8,128)(2,1)S(1)}, bf16[4,264,128]{2,1,0:T(8,128)(2,1)S(1)}, u32[]{:S(2)}, u32[]{:S(2)}) collective-permute-start(bf16[4,264,128]{2,1,0:T(8,128)(2,1)S(1)} %get-tuple-element.24), channel_id=1, source_target_pairs={{0,4},{2,6},{4,0},{6,2},{1,5},{3,7},{5,1},{7,3},{8,12},{10,14},{12... | collective-permute-start | bytes 811016 | tf_op jit(solution)/shard_map/ppermute | solution.py:60
  76.7 3.2 %collective-permute-start.12 = (bf16[4,264,128]{2,1,0:T(8,128)(2,1)S(1)}, bf16[4,264,128]{2,1,0:T(8,128)(2,1)S(1)}, u32[]{:S(2)}, u32[]{:S(2)}) collective-permute-start(bf16[4,264,128]{2,1,0:T(8,128)(2,1)S(1)} %get-tuple-element.23), channel_id=1, source_target_pairs={{0,4},{2,6},{4,0},{6,2},{1,5},{3,7},{5,1},{7,3},{8,12},{10,14},{12... | collective-permute-start | bytes 811016 | tf_op jit(solution)/shard_map/ppermute | solution.py:60
  79.9 0.7 constant_dynamic-update-slice_fusion.5
  80.6 0.6 constant_dynamic-update-slice_fusion.4
  81.2 0.7 constant_dynamic-update-slice_fusion.3
  81.9 0.7 constant_dynamic-update-slice_fusion.2
  82.5 0.8 constant_dynamic-update-slice_fusion.1
  83.4 1.1 collective-permute-done.13
  84.5 4.1 %collective-permute-done.12 = bf16[4,264,128]{2,1,0:T(8,128)(2,1)S(1)} collective-permute-done((bf16[4,264,128]{2,1,0:T(8,128)(2,1)S(1)}, bf16[4,264,128]{2,1,0:T(8,128)(2,1)S(1)}, u32[]{:S(2)}, u32[]{:S(2)}) %collective-permute-start.12) | collective-permute-done | bytes 270368 | tf_op jit(solution)/shard_map/ppermute | solution.py:60
  88.6 0.9 maximum_dynamic-update-slice_fusion
  89.5 0.8 constant_dynamic-update-slice_fusion
  90.3 13.0 %collective-permute-start.15 = (bf16[16,264,256]{2,1,0:T(8,128)(2,1)}, bf16[16,264,256]{2,1,0:T(8,128)(2,1)}, u32[]{:S(2)}, u32[]{:S(2)}) collective-permute-start(bf16[16,264,256]{2,1,0:T(8,128)(2,1)} %constant_dynamic-update-slice_fusion), channel_id=1, source_target_pairs={{0,1},{1,0},{2,3},{3,2},{4,5},{5,4},{6,7},{7,6},{8,9},{9,8},{10,11... | collective-permute-start | bytes 6488072 | tf_op jit(solution)/shard_map/ppermute | solution.py:174
  103.3 0.2 slice_reduce_fusion
  103.5 0.1 eq.138
  103.8 0.1 reduce_sum.30
  104.0 2.3 %copy.124 = bf16[24,32,8,256]{3,2,0,1:T(8,128)(2,1)S(1)} copy(bf16[24,32,8,256]{3,2,1,0:T(8,128)(2,1)} %bitcast.116) | data formatting | bytes 6291456 | tf_op jit(solution)/shard_map/reshape | solution.py:184
  106.7 0.2 copy.71
  106.9 0.2 and.85
  107.2 2.4 %gather_fusion = bf16[32,192,256]{2,1,0:T(8,128)(2,1)} fusion(bf16[192,32,256]{2,0,1:T(8,128)(2,1)S(1)} %bitcast.115, s32[1024]{0:T(1024)S(1)} %pad_clamp_fusion), kind=kCustom, calls=%fused_computation | custom fusion | bytes 6291584 | tf_op jit(solution)/shard_map/jit(_take)/gather | solution.py:183
  109.6 0.1 fusion.66
  109.7 0.9 slice.229
  110.6 3.4 %fusion.6 = f32[264,192]{0,1:T(8,128)S(1)} fusion(bf16[16,264,256]{2,1,0:T(8,128)(2,1)} %constant_dynamic-update-slice_fusion, bf16[192,32,256]{2,0,1:T(8,128)(2,1)} %bitcast.117), kind=kOutput, calls=%fused_computation.10 | convolution fusion | flops 415236096 | bytes 3938304 | tf_op jit(solution)/shard_map/dot_general | solution.py:187
  114.0 2.8 %fusion.9 = f32[264,192]{0,1:T(8,128)S(1)} fusion(bf16[16,264,256]{2,1,0:T(8,128)(2,1)} %collective-permute-done.15, bf16[192,32,256]{2,0,1:T(8,128)(2,1)S(1)} %bitcast.118), kind=kOutput, calls=%fused_computation.11 | convolution fusion | flops 415236096 | bytes 3938304 | tf_op jit(solution)/shard_map/dot_general | solution.py:192
  116.8 0.4 convolution_convert_fusion
  117.2 1.0 copy.85
  118.2 4.7 %all-to-all-start = ((bf16[32,32,192]{2,1,0:T(8,128)(2,1)}), bf16[32,32,192]{2,1,0:T(8,128)(2,1)S(1)}, u32[]{:S(2)}, u32[]{:S(2)}) async-start(bf16[32,32,192]{2,1,0:T(8,128)(2,1)} %bitcast.14), calls=%async_computation | async-start | bytes 1048576 | tf_op jit(solution)/shard_map/all_to_all | solution.py:222
  122.9 0.9 slice.230
  123.8 0.1 fusion.18
  123.9 0.6 multiply_reduce_fusion.1
  125.2 9.2 %all-to-all-done = bf16[32,32,192]{2,1,0:T(8,128)(2,1)S(1)} async-done(((bf16[32,32,192]{2,1,0:T(8,128)(2,1)}), bf16[32,32,192]{2,1,0:T(8,128)(2,1)S(1)}, u32[]{:S(2)}, u32[]{:S(2)}) %all-to-all-start) | async-done | bytes 393248 | tf_op jit(solution)/shard_map/all_to_all | solution.py:222
  134.5 0.3 copy.86
  134.8 0.5 all_to_all.16
  135.3 0.5 fusion.19
  135.8 1.0 fusion.22
  (75 shorter events, 2.3 us)
Async XLA Ops:
  0.0 9.3 %copy-start = (bf16[256,256]{1,0:T(8,128)(2,1)S(1)}, bf16[256,256]{1,0:T(8,128)(2,1)}, u32[]{:S(2)}) copy-start(bf16[256,256]{1,0:T(8,128)(2,1)} %param.8) | copy-start | bytes 393220
  0.0 10.6 %copy-start.2 = (s32[256,2]{0,1:T(2,128)S(1)}, s32[256,2]{0,1:T(2,128)}, u32[]{:S(2)}) copy-start(s32[256,2]{0,1:T(2,128)} %param.13) | copy-start | bytes 6148
  3.4 5.0 %collective-permute-start = (f32[2,136,128]{2,1,0:T(8,128)S(1)}, f32[2,136,128]{2,1,0:T(8,128)S(1)}, u32[]{:S(2)}, u32[]{:S(2)}) collective-permute-start(f32[2,136,128]{2,1,0:T(8,128)S(1)} %pad_maximum_fusion.1), channel_id=1, source_target_pairs={{0,32},{64,96},{128,160},{192,224},{256,288},{320,352},{384,416},{... | collective-permute-start | bytes 417800 | tf_op jit(solution)/shard_map/ppermute | solution.py:75
  6.1 6.6 %copy-start.3 = (f32[192]{0:T(256)S(1)}, f32[192]{0:T(256)}, u32[]{:S(2)}) copy-start(f32[192]{0:T(256)} %param.15) | copy-start | bytes 2308
  8.6 2.4 %collective-permute-start.1 = (f32[2,136,128]{2,1,0:T(8,128)S(1)}, f32[2,136,128]{2,1,0:T(8,128)S(1)}, u32[]{:S(2)}, u32[]{:S(2)}) collective-permute-start(f32[2,136,128]{2,1,0:T(8,128)S(1)} %maximum_select_fusion), channel_id=1, source_target_pairs={{32,96},{160,224},{288,352},{416,480},{33,97},{161,225},{289,353},... | collective-permute-start | bytes 417800 | tf_op jit(solution)/shard_map/ppermute | solution.py:75
  11.1 0.8 collective-permute-start.2
  12.1 0.8 collective-permute-start.3
  13.0 1.4 collective-permute-start.4
  14.5 3.3 %collective-permute-start.5 = (f32[2,136,128]{2,1,0:T(8,128)S(1)}, f32[2,136,128]{2,1,0:T(8,128)S(1)}, u32[]{:S(2)}, u32[]{:S(2)}) collective-permute-start(f32[2,136,128]{2,1,0:T(8,128)S(1)} %maximum_select_fusion.4), channel_id=1, source_target_pairs={{32,96},{96,160},{160,224},{224,288},{288,352},{352,416},{416,480}... | collective-permute-start | bytes 417800 | tf_op jit(solution)/shard_map/ppermute | solution.py:103
  16.5 32.7 %collective-permute-start.6 = (f32[2,136,128]{2,1,0:T(8,128)S(1)}, f32[2,136,128]{2,1,0:T(8,128)S(1)}, u32[]{:S(2)}, u32[]{:S(2)}) collective-permute-start(f32[2,136,128]{2,1,0:T(8,128)S(1)} %maximum_select_fusion.4), channel_id=1, source_target_pairs={{32,64},{96,128},{160,192},{224,256},{288,320},{352,384},{416,448}... | collective-permute-start | bytes 417800 | tf_op jit(solution)/shard_map/ppermute | solution.py:102
  49.8 16.5 %collective-permute-start.7 = (bf16[1,264,256]{2,1,0:T(8,128)(2,1)S(1)}, bf16[1,264,256]{2,1,0:T(8,128)(2,1)S(1)}, u32[]{:S(2)}, u32[]{:S(2)}) collective-permute-start(bf16[1,264,256]{2,1,0:T(8,128)(2,1)S(1)} %maximum_bitcast_fusion), channel_id=1, source_target_pairs={{0,24},{8,0},{16,8},{24,16},{1,25},{9,1},{17,9},{25,17},{2,26},{10... | collective-permute-start | bytes 405512 | tf_op jit(solution)/shard_map/ppermute | solution.py:60
  54.2 12.1 %collective-permute-start.10 = (bf16[1,264,256]{2,1,0:T(8,128)(2,1)S(1)}, bf16[1,264,256]{2,1,0:T(8,128)(2,1)S(1)}, u32[]{:S(2)}, u32[]{:S(2)}) collective-permute-start(bf16[1,264,256]{2,1,0:T(8,128)(2,1)S(1)} %maximum_bitcast_fusion), channel_id=1, source_target_pairs={{0,8},{8,16},{16,24},{24,0},{1,9},{9,17},{17,25},{25,1},{2,10},{10... | collective-permute-start | bytes 405512 | tf_op jit(solution)/shard_map/ppermute | solution.py:60
  56.2 7.5 %collective-permute-start.8 = (bf16[1,264,128]{2,1,0:T(8,128)(2,1)S(1)}, bf16[1,264,128]{2,1,0:T(8,128)(2,1)S(1)}, u32[]{:S(2)}, u32[]{:S(2)}) collective-permute-start(bf16[1,264,128]{2,1,0:T(8,128)(2,1)S(1)} %get-tuple-element.26), channel_id=1, source_target_pairs={{0,16},{8,24},{16,0},{24,8},{1,17},{9,25},{17,1},{25,9},{2,18},{10... | collective-permute-start | bytes 202760 | tf_op jit(solution)/shard_map/ppermute | solution.py:60
  59.8 6.5 %collective-permute-start.9 = (bf16[1,264,128]{2,1,0:T(8,128)(2,1)S(1)}, bf16[1,264,128]{2,1,0:T(8,128)(2,1)S(1)}, u32[]{:S(2)}, u32[]{:S(2)}) collective-permute-start(bf16[1,264,128]{2,1,0:T(8,128)(2,1)S(1)} %get-tuple-element.25), channel_id=1, source_target_pairs={{0,16},{8,24},{16,0},{24,8},{1,17},{9,25},{17,1},{25,9},{2,18},{10... | collective-permute-start | bytes 202760 | tf_op jit(solution)/shard_map/ppermute | solution.py:60
  66.4 16.1 %collective-permute-start.11 = (bf16[4,264,256]{2,1,0:T(8,128)(2,1)S(1)}, bf16[4,264,256]{2,1,0:T(8,128)(2,1)S(1)}, u32[]{:S(2)}, u32[]{:S(2)}) collective-permute-start(bf16[4,264,256]{2,1,0:T(8,128)(2,1)S(1)} %pad_maximum_fusion), channel_id=1, source_target_pairs={{0,6},{2,0},{4,2},{6,4},{1,7},{3,1},{5,3},{7,5},{8,14},{10,8},{12,... | collective-permute-start | bytes 1622024 | tf_op jit(solution)/shard_map/ppermute | solution.py:60
  71.2 18.3 %collective-permute-start.14 = (bf16[4,264,256]{2,1,0:T(8,128)(2,1)S(1)}, bf16[4,264,256]{2,1,0:T(8,128)(2,1)S(1)}, u32[]{:S(2)}, u32[]{:S(2)}) collective-permute-start(bf16[4,264,256]{2,1,0:T(8,128)(2,1)S(1)} %pad_maximum_fusion), channel_id=1, source_target_pairs={{0,2},{2,4},{4,6},{6,0},{1,3},{3,5},{5,7},{7,1},{8,10},{10,12},{12... | collective-permute-start | bytes 1622024 | tf_op jit(solution)/shard_map/ppermute | solution.py:60
  73.1 11.4 %collective-permute-start.13 = (bf16[4,264,128]{2,1,0:T(8,128)(2,1)S(1)}, bf16[4,264,128]{2,1,0:T(8,128)(2,1)S(1)}, u32[]{:S(2)}, u32[]{:S(2)}) collective-permute-start(bf16[4,264,128]{2,1,0:T(8,128)(2,1)S(1)} %get-tuple-element.24), channel_id=1, source_target_pairs={{0,4},{2,6},{4,0},{6,2},{1,5},{3,7},{5,1},{7,3},{8,12},{10,14},{12... | collective-permute-start | bytes 811016 | tf_op jit(solution)/shard_map/ppermute | solution.py:60
  76.7 11.9 %collective-permute-start.12 = (bf16[4,264,128]{2,1,0:T(8,128)(2,1)S(1)}, bf16[4,264,128]{2,1,0:T(8,128)(2,1)S(1)}, u32[]{:S(2)}, u32[]{:S(2)}) collective-permute-start(bf16[4,264,128]{2,1,0:T(8,128)(2,1)S(1)} %get-tuple-element.23), channel_id=1, source_target_pairs={{0,4},{2,6},{4,0},{6,2},{1,5},{3,7},{5,1},{7,3},{8,12},{10,14},{12... | collective-permute-start | bytes 811016 | tf_op jit(solution)/shard_map/ppermute | solution.py:60
  90.3 23.7 %collective-permute-start.15 = (bf16[16,264,256]{2,1,0:T(8,128)(2,1)}, bf16[16,264,256]{2,1,0:T(8,128)(2,1)}, u32[]{:S(2)}, u32[]{:S(2)}) collective-permute-start(bf16[16,264,256]{2,1,0:T(8,128)(2,1)} %constant_dynamic-update-slice_fusion), channel_id=1, source_target_pairs={{0,1},{1,0},{2,3},{3,2},{4,5},{5,4},{6,7},{7,6},{8,9},{9,8},{10,11... | collective-permute-start | bytes 6488072 | tf_op jit(solution)/shard_map/ppermute | solution.py:174
  104.0 2.6 %copy-start.4 = (s32[64]{0:T(128)S(1)}, s32[64]{0:T(128)}, u32[]{:S(2)}) copy-start(s32[64]{0:T(128)} %param.14) | copy-start | bytes 772
  110.6 3.4 %copy-start.1 = (bf16[32,192,256]{2,1,0:T(8,128)(2,1)S(1)}, bf16[32,192,256]{2,1,0:T(8,128)(2,1)}, u32[]{:S(2)}) copy-start(bf16[32,192,256]{2,1,0:T(8,128)(2,1)} %gather_fusion) | copy-start | bytes 9437188
  118.2 16.3 %all-to-all-start = ((bf16[32,32,192]{2,1,0:T(8,128)(2,1)}), bf16[32,32,192]{2,1,0:T(8,128)(2,1)S(1)}, u32[]{:S(2)}, u32[]{:S(2)}) async-start(bf16[32,32,192]{2,1,0:T(8,128)(2,1)} %bitcast.14), calls=%async_computation | async-start | bytes 1048576 | tf_op jit(solution)/shard_map/all_to_all | solution.py:222

commit v12 on v10

--- a/solution.py
+++ b/solution.py
@@ -19,7 +19,9 @@
     kv_state, offset = carried_in
     query_sub, key_sub, value_sub, decay_sub = pieces
     sub_rows = query_sub.shape[0]
-    cumulated = jnp.cumsum(decay_sub, axis=0)
+    rows = jnp.arange(sub_rows, dtype=jnp.int32)
+    lower = (rows[:, None] >= rows[None, :]).astype(jnp.float32)
+    cumulated = jnp.dot(lower, decay_sub, precision=lax.Precision.HIGHEST)
     scores = jnp.einsum("thd,shd->hts", query_sub, key_sub, preferred_element_type=jnp.float32)
     spread = jnp.transpose(cumulated)
     decay_gaps = jnp.minimum(spread[:, :, None] - spread[:, None, :], 0.0)
@@ -100,8 +102,7 @@
     from_odd = lax.ppermute(segment, axis, to_even)
     from_odd_far = lax.ppermute(segment, axis, to_odd)
     odd_result = jnp.where(position >= 3, combined(from_odd_far, left_raw), left_raw)
-    result = jnp.where(position % 2 == 1, odd_result, from_odd)
-    return jnp.where(position == 0, jnp.zeros_like(value), result)
+    return jnp.where(position % 2 == 1, odd_result, from_odd)
 
 
 def split_parts(values, width):

time: 137 us -> 136 us (level)
    unnamed x19 -> x18, local copies, waits for them, and re-layouts: 4.3 us -> 4.3 us
where the time goes in v12:
time: 136 us; the launch traced here: 135 us
  starting transfers between devices  51.4 us (38%)
  waiting for transfers between devices  48.6 us (36%)
  local copies, waits for them, and re-layouts  15.8 us (12%)
  matrix products  12.2 us (9%)
  other arithmetic  5.82 us (4%)
    ppermute x1, waiting for transfers between devices, exclusive_scan(): from_odd = lax.ppermute(segment, axis, to_even)  31.5 us
    ppermute x8, starting transfers between devices, shifted(): lax.ppermute(value, axis, [(i, (i + steps) % RING) for i in range(RING)])  26.4 us
    ppermute x1, starting transfers between devices, local_body(): far = lax.ppermute(near, 'core', [(0, 1), (1, 0)])  13 us
    all_to_all x1, waiting for transfers between devices, local_body(): lax.all_to_all(tile_rows, EP, split_axis=0, concat_axis=2, tiled=True)  9.21 us
    ppermute x8, waiting for transfers between devices, shifted(): lax.ppermute(value, axis, [(i, (i + steps) % RING) for i in range(RING)])  7.93 us
    ppermute x5, starting transfers between devices, step(): arrived = lax.ppermute(current, axis, pairs)  5.33 us
    all_to_all x1, starting transfers between devices, local_body(): lax.all_to_all(tile_rows, EP, split_axis=0, concat_axis=2, tiled=True)  4.68 us
    unnamed x18, local copies, waits for them, and re-layouts  4.3 us
  transfers between devices with their start and end apart: 17, of which 5 were waited for; matrix products, arithmetic and copies ran while one was open for 16% of the time, Pallas kernels for 0%

profile of v12, /device:TPU:385, one launch (start us, length us, event | category | flops | bytes accessed | tf_op | source)
XLA Modules:
  0.0 135.2 jit_solution(16357525659643115796)
XLA Ops:
  0.0 0.9 fusion.58
  0.9 0.2 slice_reduce_fusion.1
  1.2 1.0 copy.86
  2.3 1.1 convolution_add_fusion
  3.5 2.7 %collective-permute-start = (f32[2,136,128]{2,1,0:T(8,128)S(1)}, f32[2,136,128]{2,1,0:T(8,128)S(1)}, u32[]{:S(2)}, u32[]{:S(2)}) collective-permute-start(f32[2,136,128]{2,1,0:T(8,128)S(1)} %pad_maximum_fusion.1), channel_id=1, source_target_pairs={{0,32},{64,96},{128,160},{192,224},{256,288},{320,352},{384,416},{... | collective-permute-start | bytes 417800 | tf_op jit(solution)/shard_map/ppermute | solution.py:75
  6.2 0.8 copy.69
  7.0 0.1 eq.151
  7.1 1.3 fusion.15
  8.6 0.7 collective-permute-start.1
  9.3 0.1 fusion.88
  9.6 0.7 collective-permute-start.2
  10.3 0.1 fusion.89
  10.5 0.7 collective-permute-start.3
  11.2 0.5 fusion.14
  11.7 1.2 reduce-window.6
  12.9 0.1 fusion.90
  13.1 0.7 collective-permute-start.4
  13.8 0.2 slice_reduce_fusion
  14.1 0.1 fusion.91
  14.3 0.7 collective-permute-start.5
  15.0 0.1 eq.147
  15.2 0.1 fusion.87
  15.3 1.3 collective-permute-start.6
  16.7 31.5 %collective-permute-done.6 = f32[2,136,128]{2,1,0:T(8,128)S(1)} collective-permute-done((f32[2,136,128]{2,1,0:T(8,128)S(1)}, f32[2,136,128]{2,1,0:T(8,128)S(1)}, u32[]{:S(2)}, u32[]{:S(2)}) %collective-permute-start.6) | collective-permute-done | bytes 139296 | tf_op jit(solution)/shard_map/ppermute | solution.py:102
  48.2 0.5 multiply_reduce_fusion
  48.9 4.4 %collective-permute-start.7 = (bf16[1,264,256]{2,1,0:T(8,128)(2,1)S(1)}, bf16[1,264,256]{2,1,0:T(8,128)(2,1)S(1)}, u32[]{:S(2)}, u32[]{:S(2)}) collective-permute-start(bf16[1,264,256]{2,1,0:T(8,128)(2,1)S(1)} %maximum_bitcast_fusion), channel_id=1, source_target_pairs={{0,24},{8,0},{16,8},{24,16},{1,25},{9,1},{17,9},{25,17},{2,26},{10... | collective-permute-start | bytes 405512 | tf_op jit(solution)/shard_map/ppermute | solution.py:60
  53.3 1.9 %collective-permute-start.10 = (bf16[1,264,256]{2,1,0:T(8,128)(2,1)S(1)}, bf16[1,264,256]{2,1,0:T(8,128)(2,1)S(1)}, u32[]{:S(2)}, u32[]{:S(2)}) collective-permute-start(bf16[1,264,256]{2,1,0:T(8,128)(2,1)S(1)} %maximum_bitcast_fusion), channel_id=1, source_target_pairs={{0,8},{8,16},{16,24},{24,0},{1,9},{9,17},{17,25},{25,1},{2,10},{10... | collective-permute-start | bytes 405512 | tf_op jit(solution)/shard_map/ppermute | solution.py:60
  55.2 3.6 %collective-permute-start.8 = (bf16[1,264,128]{2,1,0:T(8,128)(2,1)S(1)}, bf16[1,264,128]{2,1,0:T(8,128)(2,1)S(1)}, u32[]{:S(2)}, u32[]{:S(2)}) collective-permute-start(bf16[1,264,128]{2,1,0:T(8,128)(2,1)S(1)} %get-tuple-element.26), channel_id=1, source_target_pairs={{0,16},{8,24},{16,0},{24,8},{1,17},{9,25},{17,1},{25,9},{2,18},{10... | collective-permute-start | bytes 202760 | tf_op jit(solution)/shard_map/ppermute | solution.py:60
  58.8 3.2 %collective-permute-start.9 = (bf16[1,264,128]{2,1,0:T(8,128)(2,1)S(1)}, bf16[1,264,128]{2,1,0:T(8,128)(2,1)S(1)}, u32[]{:S(2)}, u32[]{:S(2)}) collective-permute-start(bf16[1,264,128]{2,1,0:T(8,128)(2,1)S(1)} %get-tuple-element.25), channel_id=1, source_target_pairs={{0,16},{8,24},{16,0},{24,8},{1,17},{9,25},{17,1},{25,9},{2,18},{10... | collective-permute-start | bytes 202760 | tf_op jit(solution)/shard_map/ppermute | solution.py:60
  62.0 0.6 constant_dynamic-update-slice_fusion.6
  62.7 2.7 %collective-permute-done.9 = bf16[1,264,128]{2,1,0:T(8,128)(2,1)S(1)} collective-permute-done((bf16[1,264,128]{2,1,0:T(8,128)(2,1)S(1)}, bf16[1,264,128]{2,1,0:T(8,128)(2,1)S(1)}, u32[]{:S(2)}, u32[]{:S(2)}) %collective-permute-start.9) | collective-permute-done | bytes 67616 | tf_op jit(solution)/shard_map/ppermute | solution.py:60
  65.4 4.6 %collective-permute-start.11 = (bf16[4,264,256]{2,1,0:T(8,128)(2,1)S(1)}, bf16[4,264,256]{2,1,0:T(8,128)(2,1)S(1)}, u32[]{:S(2)}, u32[]{:S(2)}) collective-permute-start(bf16[4,264,256]{2,1,0:T(8,128)(2,1)S(1)} %pad_maximum_fusion), channel_id=1, source_target_pairs={{0,6},{2,0},{4,2},{6,4},{1,7},{3,1},{5,3},{7,5},{8,14},{10,8},{12,... | collective-permute-start | bytes 1622024 | tf_op jit(solution)/shard_map/ppermute | solution.py:60
  70.2 1.9 %collective-permute-start.14 = (bf16[4,264,256]{2,1,0:T(8,128)(2,1)S(1)}, bf16[4,264,256]{2,1,0:T(8,128)(2,1)S(1)}, u32[]{:S(2)}, u32[]{:S(2)}) collective-permute-start(bf16[4,264,256]{2,1,0:T(8,128)(2,1)S(1)} %pad_maximum_fusion), channel_id=1, source_target_pairs={{0,2},{2,4},{4,6},{6,0},{1,3},{3,5},{5,7},{7,1},{8,10},{10,12},{12... | collective-permute-start | bytes 1622024 | tf_op jit(solution)/shard_map/ppermute | solution.py:60
  72.2 3.5 %collective-permute-start.13 = (bf16[4,264,128]{2,1,0:T(8,128)(2,1)S(1)}, bf16[4,264,128]{2,1,0:T(8,128)(2,1)S(1)}, u32[]{:S(2)}, u32[]{:S(2)}) collective-permute-start(bf16[4,264,128]{2,1,0:T(8,128)(2,1)S(1)} %get-tuple-element.24), channel_id=1, source_target_pairs={{0,4},{2,6},{4,0},{6,2},{1,5},{3,7},{5,1},{7,3},{8,12},{10,14},{12... | collective-permute-start | bytes 811016 | tf_op jit(solution)/shard_map/ppermute | solution.py:60
  75.7 3.2 %collective-permute-start.12 = (bf16[4,264,128]{2,1,0:T(8,128)(2,1)S(1)}, bf16[4,264,128]{2,1,0:T(8,128)(2,1)S(1)}, u32[]{:S(2)}, u32[]{:S(2)}) collective-permute-start(bf16[4,264,128]{2,1,0:T(8,128)(2,1)S(1)} %get-tuple-element.23), channel_id=1, source_target_pairs={{0,4},{2,6},{4,0},{6,2},{1,5},{3,7},{5,1},{7,3},{8,12},{10,14},{12... | collective-permute-start | bytes 811016 | tf_op jit(solution)/shard_map/ppermute | solution.py:60
  79.0 0.7 constant_dynamic-update-slice_fusion.5
  79.6 0.6 constant_dynamic-update-slice_fusion.4
  80.3 0.7 constant_dynamic-update-slice_fusion.3
  80.9 0.7 constant_dynamic-update-slice_fusion.2
  81.6 0.8 constant_dynamic-update-slice_fusion.1
  82.4 1.1 collective-permute-done.13
  83.5 4.1 %collective-permute-done.12 = bf16[4,264,128]{2,1,0:T(8,128)(2,1)S(1)} collective-permute-done((bf16[4,264,128]{2,1,0:T(8,128)(2,1)S(1)}, bf16[4,264,128]{2,1,0:T(8,128)(2,1)S(1)}, u32[]{:S(2)}, u32[]{:S(2)}) %collective-permute-start.12) | collective-permute-done | bytes 270368 | tf_op jit(solution)/shard_map/ppermute | solution.py:60
  87.6 0.9 maximum_dynamic-update-slice_fusion
  88.5 0.8 constant_dynamic-update-slice_fusion
  89.3 13.0 %collective-permute-start.15 = (bf16[16,264,256]{2,1,0:T(8,128)(2,1)}, bf16[16,264,256]{2,1,0:T(8,128)(2,1)}, u32[]{:S(2)}, u32[]{:S(2)}) collective-permute-start(bf16[16,264,256]{2,1,0:T(8,128)(2,1)} %constant_dynamic-update-slice_fusion), channel_id=1, source_target_pairs={{0,1},{1,0},{2,3},{3,2},{4,5},{5,4},{6,7},{7,6},{8,9},{9,8},{10,11... | collective-permute-start | bytes 6488072 | tf_op jit(solution)/shard_map/ppermute | solution.py:173
  102.5 0.1 reduce_sum.30
  102.7 2.3 %copy.120 = bf16[24,32,8,256]{3,2,0,1:T(8,128)(2,1)S(1)} copy(bf16[24,32,8,256]{3,2,1,0:T(8,128)(2,1)} %bitcast.118) | data formatting | bytes 6291456 | tf_op jit(solution)/shard_map/reshape | solution.py:183
  105.4 0.2 copy.68
  105.6 0.2 and.85
  105.8 2.4 %gather_fusion = bf16[32,192,256]{2,1,0:T(8,128)(2,1)} fusion(bf16[192,32,256]{2,0,1:T(8,128)(2,1)S(1)} %bitcast.117, s32[1024]{0:T(1024)S(1)} %pad_clamp_fusion), kind=kCustom, calls=%fused_computation | custom fusion | bytes 6291584 | tf_op jit(solution)/shard_map/jit(_take)/gather | solution.py:182
  108.3 0.1 fusion.66
  108.4 0.9 slice.229
  109.3 3.4 %fusion.6 = f32[264,192]{0,1:T(8,128)S(1)} fusion(bf16[16,264,256]{2,1,0:T(8,128)(2,1)} %constant_dynamic-update-slice_fusion, bf16[192,32,256]{2,0,1:T(8,128)(2,1)} %bitcast.119), kind=kOutput, calls=%fused_computation.10 | convolution fusion | flops 415236096 | bytes 3938304 | tf_op jit(solution)/shard_map/dot_general | solution.py:186
  112.7 2.8 %fusion.9 = f32[264,192]{0,1:T(8,128)S(1)} fusion(bf16[16,264,256]{2,1,0:T(8,128)(2,1)} %collective-permute-done.15, bf16[192,32,256]{2,0,1:T(8,128)(2,1)S(1)} %bitcast.120), kind=kOutput, calls=%fused_computation.11 | convolution fusion | flops 415236096 | bytes 3938304 | tf_op jit(solution)/shard_map/dot_general | solution.py:191
  115.4 1.2 convolution_convert_fusion
  116.6 4.7 %all-to-all-start = ((bf16[32,32,192]{2,1,0:T(8,128)(2,1)}), bf16[32,32,192]{2,1,0:T(8,128)(2,1)S(1)}, u32[]{:S(2)}, u32[]{:S(2)}) async-start(bf16[32,32,192]{2,1,0:T(8,128)(2,1)} %convolution_convert_fusion), calls=%async_computation | async-start | bytes 1048576 | tf_op jit(solution)/shard_map/all_to_all | solution.py:223
  121.3 0.9 slice.230
  122.2 0.1 fusion.18
  122.3 0.6 multiply_reduce_fusion.1
  123.7 9.2 %all-to-all-done = bf16[32,32,192]{2,1,0:T(8,128)(2,1)S(1)} async-done(((bf16[32,32,192]{2,1,0:T(8,128)(2,1)}), bf16[32,32,192]{2,1,0:T(8,128)(2,1)S(1)}, u32[]{:S(2)}, u32[]{:S(2)}) %all-to-all-start) | async-done | bytes 393248 | tf_op jit(solution)/shard_map/all_to_all | solution.py:223
  132.9 0.3 copy.82
  133.2 0.5 all_to_all.16
  133.7 0.5 fusion.19
  134.2 1.0 fusion.23
  (78 shorter events, 2.1 us)
Async XLA Ops:
  0.0 7.1 %copy-start = (bf16[256,256]{1,0:T(8,128)(2,1)S(1)}, bf16[256,256]{1,0:T(8,128)(2,1)}, u32[]{:S(2)}) copy-start(bf16[256,256]{1,0:T(8,128)(2,1)} %param.8) | copy-start | bytes 393220
  2.3 8.0 %copy-start.4 = (f32[192]{0:T(256)S(1)}, f32[192]{0:T(256)}, u32[]{:S(2)}) copy-start(f32[192]{0:T(256)} %param.15) | copy-start | bytes 2308
  3.5 5.0 %collective-permute-start = (f32[2,136,128]{2,1,0:T(8,128)S(1)}, f32[2,136,128]{2,1,0:T(8,128)S(1)}, u32[]{:S(2)}, u32[]{:S(2)}) collective-permute-start(f32[2,136,128]{2,1,0:T(8,128)S(1)} %pad_maximum_fusion.1), channel_id=1, source_target_pairs={{0,32},{64,96},{128,160},{192,224},{256,288},{320,352},{384,416},{... | collective-permute-start | bytes 417800 | tf_op jit(solution)/shard_map/ppermute | solution.py:75
  8.6 0.8 collective-permute-start.1
  9.6 0.8 collective-permute-start.2
  10.5 2.5 %collective-permute-start.3 = (f32[2,136,128]{2,1,0:T(8,128)S(1)}, f32[2,136,128]{2,1,0:T(8,128)S(1)}, u32[]{:S(2)}, u32[]{:S(2)}) collective-permute-start(f32[2,136,128]{2,1,0:T(8,128)S(1)} %maximum_select_fusion.2), channel_id=1, source_target_pairs={{224,352},{225,353},{226,354},{227,355},{228,356},{229,357},{230,3... | collective-permute-start | bytes 417800 | tf_op jit(solution)/shard_map/ppermute | solution.py:75
  13.1 1.1 collective-permute-start.4
  14.3 2.3 %collective-permute-start.5 = (f32[2,136,128]{2,1,0:T(8,128)S(1)}, f32[2,136,128]{2,1,0:T(8,128)S(1)}, u32[]{:S(2)}, u32[]{:S(2)}) collective-permute-start(f32[2,136,128]{2,1,0:T(8,128)S(1)} %maximum_select_fusion.4), channel_id=1, source_target_pairs={{32,96},{96,160},{160,224},{224,288},{288,352},{352,416},{416,480}... | collective-permute-start | bytes 417800 | tf_op jit(solution)/shard_map/ppermute | solution.py:103
  15.2 55.0 %copy-start.3 = (s32[32,5]{0,1:T(8,128)}, s32[32,5]{0,1:T(8,128)S(1)}, u32[]{:S(2)}) copy-start(s32[32,5]{0,1:T(8,128)S(1)} %reduce-window.9) | copy-start | bytes 1924
  15.3 32.9 %collective-permute-start.6 = (f32[2,136,128]{2,1,0:T(8,128)S(1)}, f32[2,136,128]{2,1,0:T(8,128)S(1)}, u32[]{:S(2)}, u32[]{:S(2)}) collective-permute-start(f32[2,136,128]{2,1,0:T(8,128)S(1)} %maximum_select_fusion.4), channel_id=1, source_target_pairs={{32,64},{96,128},{160,192},{224,256},{288,320},{352,384},{416,448}... | collective-permute-start | bytes 417800 | tf_op jit(solution)/shard_map/ppermute | solution.py:102
  48.9 16.5 %collective-permute-start.7 = (bf16[1,264,256]{2,1,0:T(8,128)(2,1)S(1)}, bf16[1,264,256]{2,1,0:T(8,128)(2,1)S(1)}, u32[]{:S(2)}, u32[]{:S(2)}) collective-permute-start(bf16[1,264,256]{2,1,0:T(8,128)(2,1)S(1)} %maximum_bitcast_fusion), channel_id=1, source_target_pairs={{0,24},{8,0},{16,8},{24,16},{1,25},{9,1},{17,9},{25,17},{2,26},{10... | collective-permute-start | bytes 405512 | tf_op jit(solution)/shard_map/ppermute | solution.py:60
  53.3 12.1 %collective-permute-start.10 = (bf16[1,264,256]{2,1,0:T(8,128)(2,1)S(1)}, bf16[1,264,256]{2,1,0:T(8,128)(2,1)S(1)}, u32[]{:S(2)}, u32[]{:S(2)}) collective-permute-start(bf16[1,264,256]{2,1,0:T(8,128)(2,1)S(1)} %maximum_bitcast_fusion), channel_id=1, source_target_pairs={{0,8},{8,16},{16,24},{24,0},{1,9},{9,17},{17,25},{25,1},{2,10},{10... | collective-permute-start | bytes 405512 | tf_op jit(solution)/shard_map/ppermute | solution.py:60
  55.2 7.5 %collective-permute-start.8 = (bf16[1,264,128]{2,1,0:T(8,128)(2,1)S(1)}, bf16[1,264,128]{2,1,0:T(8,128)(2,1)S(1)}, u32[]{:S(2)}, u32[]{:S(2)}) collective-permute-start(bf16[1,264,128]{2,1,0:T(8,128)(2,1)S(1)} %get-tuple-element.26), channel_id=1, source_target_pairs={{0,16},{8,24},{16,0},{24,8},{1,17},{9,25},{17,1},{25,9},{2,18},{10... | collective-permute-start | bytes 202760 | tf_op jit(solution)/shard_map/ppermute | solution.py:60
  58.8 6.5 %collective-permute-start.9 = (bf16[1,264,128]{2,1,0:T(8,128)(2,1)S(1)}, bf16[1,264,128]{2,1,0:T(8,128)(2,1)S(1)}, u32[]{:S(2)}, u32[]{:S(2)}) collective-permute-start(bf16[1,264,128]{2,1,0:T(8,128)(2,1)S(1)} %get-tuple-element.25), channel_id=1, source_target_pairs={{0,16},{8,24},{16,0},{24,8},{1,17},{9,25},{17,1},{25,9},{2,18},{10... | collective-permute-start | bytes 202760 | tf_op jit(solution)/shard_map/ppermute | solution.py:60
  65.4 16.1 %collective-permute-start.11 = (bf16[4,264,256]{2,1,0:T(8,128)(2,1)S(1)}, bf16[4,264,256]{2,1,0:T(8,128)(2,1)S(1)}, u32[]{:S(2)}, u32[]{:S(2)}) collective-permute-start(bf16[4,264,256]{2,1,0:T(8,128)(2,1)S(1)} %pad_maximum_fusion), channel_id=1, source_target_pairs={{0,6},{2,0},{4,2},{6,4},{1,7},{3,1},{5,3},{7,5},{8,14},{10,8},{12,... | collective-permute-start | bytes 1622024 | tf_op jit(solution)/shard_map/ppermute | solution.py:60
  70.2 18.3 %collective-permute-start.14 = (bf16[4,264,256]{2,1,0:T(8,128)(2,1)S(1)}, bf16[4,264,256]{2,1,0:T(8,128)(2,1)S(1)}, u32[]{:S(2)}, u32[]{:S(2)}) collective-permute-start(bf16[4,264,256]{2,1,0:T(8,128)(2,1)S(1)} %pad_maximum_fusion), channel_id=1, source_target_pairs={{0,2},{2,4},{4,6},{6,0},{1,3},{3,5},{5,7},{7,1},{8,10},{10,12},{12... | collective-permute-start | bytes 1622024 | tf_op jit(solution)/shard_map/ppermute | solution.py:60
  72.1 30.2 %slice-start = ((s32[32,5]{0,1:T(8,128)}), s32[32,4]{0,1:T(4,128)S(1)}, s32[]{:S(2)}) async-start(s32[32,5]{0,1:T(8,128)} %copy-done.3), calls=%async_computation.1 | async-start | bytes 4096 | tf_op jit(solution)/shard_map/slice.3
  72.2 11.3 %collective-permute-start.13 = (bf16[4,264,128]{2,1,0:T(8,128)(2,1)S(1)}, bf16[4,264,128]{2,1,0:T(8,128)(2,1)S(1)}, u32[]{:S(2)}, u32[]{:S(2)}) collective-permute-start(bf16[4,264,128]{2,1,0:T(8,128)(2,1)S(1)} %get-tuple-element.24), channel_id=1, source_target_pairs={{0,4},{2,6},{4,0},{6,2},{1,5},{3,7},{5,1},{7,3},{8,12},{10,14},{12... | collective-permute-start | bytes 811016 | tf_op jit(solution)/shard_map/ppermute | solution.py:60
  75.7 11.9 %collective-permute-start.12 = (bf16[4,264,128]{2,1,0:T(8,128)(2,1)S(1)}, bf16[4,264,128]{2,1,0:T(8,128)(2,1)S(1)}, u32[]{:S(2)}, u32[]{:S(2)}) collective-permute-start(bf16[4,264,128]{2,1,0:T(8,128)(2,1)S(1)} %get-tuple-element.23), channel_id=1, source_target_pairs={{0,4},{2,6},{4,0},{6,2},{1,5},{3,7},{5,1},{7,3},{8,12},{10,14},{12... | collective-permute-start | bytes 811016 | tf_op jit(solution)/shard_map/ppermute | solution.py:60
  89.3 23.3 %collective-permute-start.15 = (bf16[16,264,256]{2,1,0:T(8,128)(2,1)}, bf16[16,264,256]{2,1,0:T(8,128)(2,1)}, u32[]{:S(2)}, u32[]{:S(2)}) collective-permute-start(bf16[16,264,256]{2,1,0:T(8,128)(2,1)} %constant_dynamic-update-slice_fusion), channel_id=1, source_target_pairs={{0,1},{1,0},{2,3},{3,2},{4,5},{5,4},{6,7},{7,6},{8,9},{9,8},{10,11... | collective-permute-start | bytes 6488072 | tf_op jit(solution)/shard_map/ppermute | solution.py:173
  102.7 2.6 %copy-start.5 = (s32[64]{0:T(128)S(1)}, s32[64]{0:T(128)}, u32[]{:S(2)}) copy-start(s32[64]{0:T(128)} %param.14) | copy-start | bytes 772
  102.7 2.7 %copy-start.2 = (s32[256,2]{0,1:T(2,128)S(1)}, s32[256,2]{0,1:T(2,128)}, u32[]{:S(2)}) copy-start(s32[256,2]{0,1:T(2,128)} %param.13) | copy-start | bytes 6148
  109.2 3.4 %copy-start.1 = (bf16[32,192,256]{2,1,0:T(8,128)(2,1)S(1)}, bf16[32,192,256]{2,1,0:T(8,128)(2,1)}, u32[]{:S(2)}) copy-start(bf16[32,192,256]{2,1,0:T(8,128)(2,1)} %gather_fusion) | copy-start | bytes 9437188
  116.6 16.3 %all-to-all-start = ((bf16[32,32,192]{2,1,0:T(8,128)(2,1)}), bf16[32,32,192]{2,1,0:T(8,128)(2,1)S(1)}, u32[]{:S(2)}, u32[]{:S(2)}) async-start(bf16[32,32,192]{2,1,0:T(8,128)(2,1)} %convolution_convert_fusion), calls=%async_computation | async-start | bytes 1048576 | tf_op jit(solution)/shard_map/all_to_all | solution.py:223
